TPU v7x, 32 devices: a whole 2x2x4 slice. The times are simulated.
32 devices in a mesh: gy: 4 (over z), gz: 8 (over y, x, core).
Axes of the slice: x: 2, y: 2, z: 4, core: 2. Of those that a mesh axis runs over, the one named last changes fastest.
Arguments:
- electric_x: float32 [64, 64, 256], P('gy', 'gz'), may hold values from -1.5 to 1.5
- electric_y: float32 [64, 64, 256], P('gy', 'gz'), may hold values from -1.5 to 1.5
- electric_z: float32 [64, 64, 256], P('gy', 'gz'), may hold values from -1.5 to 1.5
- magnetic_x: float32 [64, 64, 256], P('gy', 'gz'), may hold values from -0.024 to 0.024
- magnetic_y: float32 [64, 64, 256], P('gy', 'gz'), may hold values from -0.024 to 0.024
- magnetic_z: float32 [64, 64, 256], P('gy', 'gz'), may hold values from -0.024 to 0.024
- permittivity: float32 [64, 64, 256], P('gy', 'gz'), may hold values from 1 to 12
- conductivity: float32 [64, 64, 256], P('gy', 'gz'), may hold values from 0.05 to 2
Outputs:
- half_electric_x: float32 [64, 64, 256], P('gy', 'gz')
- half_electric_y: float32 [64, 64, 256], P('gy', 'gz')
- half_electric_z: float32 [64, 64, 256], P('gy', 'gz')
- half_magnetic_x: float32 [64, 64, 256], P('gy', 'gz')
- half_magnetic_y: float32 [64, 64, 256], P('gy', 'gz')
- half_magnetic_z: float32 [64, 64, 256], P('gy', 'gz')
All inputs are finite; a program needn't handle non-finite values.
Results may differ from a plain program's by a relative error of at most 0.0003.
Values sent between devices are 32-bit elements; how exact they have to be, the bound alone decides.
No kernel may reach another device: no remote copies, remote signals or barrier semaphores. Data moves between devices by JAX's collectives and lax.ppermute only.
A program may use at most 64 MiB of HBM per device.

v0:
```python
import jax
import jax.numpy as jnp
from jax import lax
from jax.sharding import PartitionSpec as P

step_ratio = 1024.0


def passed_along(value, axis, steps):
    count = lax.axis_size(axis)
    first, last = (max(0, -steps), min(count, count - steps))
    return lax.ppermute(value, axis, [(source, source + steps) for source in range(first, last)])


def take_rows(values, direction, start, length):
    return lax.slice_in_dim(values, start, start + length, axis=direction)


def edge_zeros(values, direction):
    return jnp.zeros_like(take_rows(values, direction, 0, 1))


def ahead_diff(values, direction, beyond):
    length = values.shape[direction]
    ahead = jnp.concatenate([take_rows(values, direction, 1, length - 1), beyond], axis=direction)
    return ahead - values


def behind_diff(values, direction, before):
    length = values.shape[direction]
    behind = jnp.concatenate([before, take_rows(values, direction, 0, length - 1)], axis=direction)
    return values - behind


def rows_from_below(values, direction, stride, fill_value):
    length = values.shape[direction]
    padding = jnp.full_like(take_rows(values, direction, 0, stride), fill_value)
    return jnp.concatenate(
        [padding, take_rows(values, direction, 0, length - stride)], axis=direction
    )


def rows_from_above(values, direction, stride, fill_value):
    length = values.shape[direction]
    padding = jnp.full_like(take_rows(values, direction, 0, stride), fill_value)
    return jnp.concatenate(
        [take_rows(values, direction, stride, length - stride), padding], axis=direction
    )


def reduce_lines(lower_band, main_band, upper_band, right_side, direction):
    length = main_band.shape[direction]
    stride = 1
    while stride < length:
        low_lower = rows_from_below(lower_band, direction, stride, 0.0)
        low_main = rows_from_below(main_band, direction, stride, 1.0)
        low_upper = rows_from_below(upper_band, direction, stride, 0.0)
        low_right = rows_from_below(right_side, direction + 1, stride, 0.0)
        high_lower = rows_from_above(lower_band, direction, stride, 0.0)
        high_main = rows_from_above(main_band, direction, stride, 1.0)
        high_upper = rows_from_above(upper_band, direction, stride, 0.0)
        high_right = rows_from_above(right_side, direction + 1, stride, 0.0)
        ratio_low = -lower_band / low_main
        ratio_high = -upper_band / high_main
        right_side = right_side + ratio_low[None] * low_right + ratio_high[None] * high_right
        main_band = main_band + ratio_low * low_upper + ratio_high * high_lower
        lower_band = ratio_low * low_lower
        upper_band = ratio_high * high_upper
        stride = stride * 2
    return right_side / main_band[None]


def bands(coupling, damping, row_index, line_length):
    lower_band = jnp.where(row_index >= 1, -coupling, 0.0)
    upper_band = jnp.where(row_index <= line_length - 2, -coupling, 0.0)
    main_band = 1.0 + damping + coupling * jnp.where(row_index >= 1, 2.0, 1.0)
    return (lower_band, main_band, upper_band)


def chain_solve(
    reduced_low,
    reduced_mid,
    reduced_high,
    reduced_right,
    total_devices,
    position,
    lower_shift,
    upper_shift,
):
    stride = 1
    while stride < total_devices:
        stacked = jnp.stack([reduced_low, reduced_mid, reduced_high, reduced_right])
        from_below = lower_shift(stacked, stride)
        from_above = upper_shift(stacked, stride)
        below_main = jnp.where(position >= stride, from_below[1], 1.0)
        above_main = jnp.where(position + stride < total_devices, from_above[1], 1.0)
        ratio_low = -reduced_low / below_main
        ratio_high = -reduced_high / above_main
        reduced_right = reduced_right + ratio_low * from_below[3] + ratio_high * from_above[3]
        reduced_mid = reduced_mid + ratio_low * from_below[2] + ratio_high * from_above[0]
        reduced_low = ratio_low * from_below[0]
        reduced_high = ratio_high * from_above[2]
        stride = stride * 2
    return reduced_right / reduced_mid


def partitioned(
    lower_band, main_band, upper_band, right_side, direction, send_heads, solve_reduced, send_last
):
    length = main_band.shape[direction]
    inner_rows = length - 1
    low_inner = take_rows(lower_band, direction, 0, inner_rows)
    main_inner = take_rows(main_band, direction, 0, inner_rows)
    up_inner = take_rows(upper_band, direction, 0, inner_rows)
    row_index = lax.broadcasted_iota(jnp.int32, low_inner.shape, direction)
    first_row = row_index == 0
    last_inner = row_index == inner_rows - 1
    left_column = jnp.where(first_row, -low_inner, 0.0)
    right_column = jnp.where(last_inner, -up_inner, 0.0)
    low_inner = jnp.where(first_row, 0.0, low_inner)
    up_inner = jnp.where(last_inner, 0.0, up_inner)
    stacked = jnp.stack(
        [take_rows(right_side, direction, 0, inner_rows), left_column, right_column]
    )
    solved = reduce_lines(low_inner, main_inner, up_inner, stacked, direction)
    next_heads = send_heads(take_rows(solved, direction + 1, 0, 1))
    own_tails = take_rows(solved, direction + 1, inner_rows - 1, 1)
    low_last = take_rows(lower_band, direction, inner_rows, 1)
    main_last = take_rows(main_band, direction, inner_rows, 1)
    up_last = take_rows(upper_band, direction, inner_rows, 1)
    right_last = take_rows(right_side, direction, inner_rows, 1)
    reduced_low = low_last * own_tails[1]
    reduced_mid = main_last + low_last * own_tails[2] + up_last * next_heads[1]
    reduced_high = up_last * next_heads[2]
    reduced_right = right_last - low_last * own_tails[0] - up_last * next_heads[0]
    interface = solve_reduced(reduced_low, reduced_mid, reduced_high, reduced_right)
    earlier = send_last(interface)
    interior = solved[0] + solved[1] * earlier + solved[2] * interface
    return jnp.concatenate([interior, interface], axis=direction)


def z_heads(values):
    return passed_along(values, "gz", -1)


def z_earlier(values):
    return passed_along(values, "gz", 1)


def z_chain_below(values, stride):
    return passed_along(values, "gz", stride)


def z_chain_above(values, stride):
    return passed_along(values, "gz", -stride)


def z_reduced_chain(reduced_low, reduced_mid, reduced_high, reduced_right):
    return chain_solve(
        reduced_low,
        reduced_mid,
        reduced_high,
        reduced_right,
        lax.axis_size("gz"),
        lax.axis_index("gz"),
        z_chain_below,
        z_chain_above,
    )


def y_heads(values):
    return passed_along(values, "gy", -1)


def y_earlier(values):
    return passed_along(values, "gy", 1)


def y_chain_below(values, stride):
    return passed_along(values, "gy", stride)


def y_chain_above(values, stride):
    return passed_along(values, "gy", -stride)


def y_reduced_chain(reduced_low, reduced_mid, reduced_high, reduced_right):
    return chain_solve(
        reduced_low,
        reduced_mid,
        reduced_high,
        reduced_right,
        lax.axis_size("gy"),
        lax.axis_index("gy"),
        y_chain_below,
        y_chain_above,
    )


def body(
    electric_x,
    electric_y,
    electric_z,
    magnetic_x,
    magnetic_y,
    magnetic_z,
    permittivity,
    conductivity,
):
    coupling = step_ratio / permittivity
    damping = conductivity / permittivity
    keeping = 1.0 - damping
    size_y = electric_x.shape[0]
    size_z = electric_x.shape[1]
    size_x = electric_x.shape[2]
    cross_y = ahead_diff(electric_y, 2, edge_zeros(electric_y, 2))
    below_y = passed_along(
        jnp.stack(
            [
                take_rows(magnetic_z, 0, size_y - 1, 1),
                take_rows(cross_y, 0, size_y - 1, 1),
                take_rows(magnetic_x, 0, size_y - 1, 1),
            ]
        ),
        "gy",
        1,
    )
    above_ez = passed_along(take_rows(electric_z, 0, 0, 1), "gy", -1)
    cross_z = ahead_diff(electric_z, 0, above_ez)
    below_z = passed_along(
        jnp.stack(
            [
                take_rows(magnetic_y, 1, size_z - 1, 1),
                take_rows(magnetic_x, 1, size_z - 1, 1),
                take_rows(cross_z, 1, size_z - 1, 1),
            ]
        ),
        "gz",
        1,
    )
    above_ex = passed_along(take_rows(electric_x, 1, 0, 1), "gz", -1)
    cross_x = ahead_diff(electric_x, 1, above_ex)
    source_x = keeping * electric_x + coupling * (
        behind_diff(magnetic_z, 0, below_y[0])
        - behind_diff(cross_y, 0, below_y[1])
        - behind_diff(magnetic_y, 1, below_z[0])
    )
    source_y = keeping * electric_y + coupling * (
        behind_diff(magnetic_x, 1, below_z[1])
        - behind_diff(cross_z, 1, below_z[2])
        - behind_diff(magnetic_z, 2, edge_zeros(magnetic_z, 2))
    )
    source_z = keeping * electric_z + coupling * (
        behind_diff(magnetic_y, 2, edge_zeros(magnetic_y, 2))
        - behind_diff(cross_x, 2, edge_zeros(cross_x, 2))
        - behind_diff(magnetic_x, 0, below_y[2])
    )
    index_x = lax.broadcasted_iota(jnp.int32, coupling.shape, 2)
    lower_x, main_x, upper_x = bands(coupling, damping, index_x, size_x)
    half_electric_z = reduce_lines(lower_x, main_x, upper_x, source_z[None], 2)[0]
    index_z = lax.broadcasted_iota(jnp.int32, coupling.shape, 1) + lax.axis_index("gz") * size_z
    lower_z, main_z, upper_z = bands(coupling, damping, index_z, size_z * lax.axis_size("gz"))
    half_electric_y = partitioned(
        lower_z, main_z, upper_z, source_y, 1, z_heads, z_reduced_chain, z_earlier
    )
    index_y = lax.broadcasted_iota(jnp.int32, coupling.shape, 0) + lax.axis_index("gy") * size_y
    lower_y, main_y, upper_y = bands(coupling, damping, index_y, size_y * lax.axis_size("gy"))
    half_electric_x = partitioned(
        lower_y, main_y, upper_y, source_x, 0, y_heads, y_reduced_chain, y_earlier
    )
    fresh_ex = passed_along(take_rows(half_electric_x, 0, 0, 1), "gy", -1)
    fresh_ey = passed_along(take_rows(half_electric_y, 1, 0, 1), "gz", -1)
    half_magnetic_x = magnetic_x + ahead_diff(half_electric_y, 1, fresh_ey) - cross_z
    half_magnetic_y = (
        magnetic_y + ahead_diff(half_electric_z, 2, edge_zeros(half_electric_z, 2)) - cross_x
    )
    half_magnetic_z = magnetic_z + ahead_diff(half_electric_x, 0, fresh_ex) - cross_y
    return (
        half_electric_x,
        half_electric_y,
        half_electric_z,
        half_magnetic_x,
        half_magnetic_y,
        half_magnetic_z,
    )


def solution(mesh):
    placed = (
        P("gy", "gz", None),
        P("gy", "gz", None),
        P("gy", "gz", None),
        P("gy", "gz", None),
        P("gy", "gz", None),
        P("gy", "gz", None),
        P("gy", "gz", None),
        P("gy", "gz", None),
    )
    return jax.shard_map(
        body,
        mesh=mesh,
        in_specs=placed,
        out_specs=(
            P("gy", "gz", None),
            P("gy", "gz", None),
            P("gy", "gz", None),
            P("gy", "gz", None),
            P("gy", "gz", None),
            P("gy", "gz", None),
        ),
        check_vma=False,
    )
```

profile of v0, /device:TPU:3, one launch (start us, length us, event | category | flops | bytes accessed | tf_op | source)
XLA Modules:
  0.0 91.5 jit_solution(8867250936147619575)
XLA Ops:
  0.6 0.7 slice.674
  1.4 1.3 %collective-permute-start.1 = (f32[1,8,256]{2,1,0:T(8,128)S(1)}, f32[1,8,256]{2,1,0:T(8,128)S(1)}, u32[]{:S(2)}, u32[]{:S(2)}) collective-permute-start(f32[1,8,256]{2,1,0:T(8,128)S(1)} %slice.674), channel_id=1, source_target_pairs={{8,0},{16,8},{24,16},{9,1},{17,9},{25,17},{10,2},{18,10},{26,18},{... | collective-permute-start | bytes 24584 | tf_op jit(solution)/shard_map/ppermute | solution.py:12
  2.7 0.9 %slice.809 = f32[16,1,256]{2,1,0:T(1,128)S(1)} slice(f32[16,8,256]{2,1,0:T(8,128)} %param.8), slice={[0:16], [0:1], [0:256]} | slice | bytes 32768 | tf_op jit(solution)/shard_map/slice | solution.py:16
  3.6 2.6 %collective-permute-start.17 = (f32[16,1,256]{2,1,0:T(1,128)S(1)}, f32[16,1,256]{2,1,0:T(1,128)S(1)}, u32[]{:S(2)}, u32[]{:S(2)}) collective-permute-start(f32[16,1,256]{2,1,0:T(1,128)S(1)} %slice.809), channel_id=1, source_target_pairs={{1,0},{2,1},{3,2},{4,3},{5,4},{6,5},{7,6},{9,8},{10,9},{11,10},{12... | collective-permute-start | bytes 49160 | tf_op jit(solution)/shard_map/ppermute | solution.py:12
  6.3 0.7 slice_bitcast_fusion.56
  7.0 1.0 %slice_bitcast_fusion.34 = (f32[1,16,1,256]{3,2,1,0:T(1,128)S(1)}, f32[1,16,1,256]{3,2,1,0:T(1,128)S(1)}) fusion(f32[16,8,256]{2,1,0:T(8,128)} %param.11, f32[16,8,256]{2,1,0:T(8,128)} %param.12), kind=kLoop, calls=%fused_computation.272 | loop fusion | bytes 65536 | tf_op jit(solution)/shard_map/stack | solution.py:231
  8.0 1.0 %multiply_add_fusion.12 = (f32[16,8,256]{2,1,0:T(8,128)S(1)}, f32[16,8,256]{2,1,0:T(8,128)S(1)}) fusion(f32[256]{0:T(256)S(1)} %broadcast_select_fusion.6, f32[16,8,256]{2,1,0:T(8,128)} %param.14, f32[16,8,256]{2,1,0:T(8,128)} %param.15), kind=kLoop, calls=%fused_computation.120 | loop fusion | flops 163840 | bytes 525312 | tf_op jit(solution)/shard_map/add | solution.py:76
  9.2 0.9 copy-done
  10.1 0.9 copy-done.4
  11.0 0.9 copy-done.7
  12.0 0.8 copy-done.5
  13.0 3.9 %collective-permute-start.2 = (f32[3,16,1,256]{3,2,1,0:T(1,128)S(1)}, f32[3,16,1,256]{3,2,1,0:T(1,128)S(1)}, u32[]{:S(2)}, u32[]{:S(2)}) collective-permute-start(f32[3,16,1,256]{3,2,1,0:T(1,128)S(1)} %pad_maximum_fusion.7), channel_id=1, source_target_pairs={{0,1},{1,2},{2,3},{3,4},{4,5},{5,6},{6,7},{8,9},{9,10},{10,11},{11... | collective-permute-start | bytes 147464 | tf_op jit(solution)/shard_map/ppermute | solution.py:12
  16.9 1.1 %collective-permute-done.2 = f32[3,16,1,256]{3,2,1,0:T(1,128)S(1)} collective-permute-done((f32[3,16,1,256]{3,2,1,0:T(1,128)S(1)}, f32[3,16,1,256]{3,2,1,0:T(1,128)S(1)}, u32[]{:S(2)}, u32[]{:S(2)}) %collective-permute-start.2) | collective-permute-done | bytes 49184 | tf_op jit(solution)/shard_map/ppermute | solution.py:12
  18.0 0.2 multiply_add_fusion.15
  18.3 4.0 %collective-permute-start = (f32[3,1,8,256]{3,2,1,0:T(8,128)S(1)}, f32[3,1,8,256]{3,2,1,0:T(8,128)S(1)}, u32[]{:S(2)}, u32[]{:S(2)}) collective-permute-start(f32[3,1,8,256]{3,2,1,0:T(8,128)S(1)} %pad_maximum_fusion.10), channel_id=1, source_target_pairs={{0,8},{8,16},{16,24},{1,9},{9,17},{17,25},{2,10},{10,18},{18,26},{... | collective-permute-start | bytes 73736 | tf_op jit(solution)/shard_map/ppermute | solution.py:12
  24.6 2.9 %collective-permute-start.9 = (f32[3,16,1,256]{3,2,1,0:T(1,128)S(1)}, f32[3,16,1,256]{3,2,1,0:T(1,128)S(1)}, u32[]{:S(2)}, u32[]{:S(2)}) collective-permute-start(f32[3,16,1,256]{3,2,1,0:T(1,128)S(1)} %slice.983), channel_id=1, source_target_pairs={{1,0},{2,1},{3,2},{4,3},{5,4},{6,5},{7,6},{9,8},{10,9},{11,10},{12... | collective-permute-start | bytes 147464 | tf_op jit(solution)/shard_map/ppermute | solution.py:12
  27.6 0.9 copy-done.2
  28.4 0.2 fusion.17
  29.3 1.3 %collective-permute-start.3 = (f32[3,1,8,256]{3,2,1,0:T(8,128)S(1)}, f32[3,1,8,256]{3,2,1,0:T(8,128)S(1)}, u32[]{:S(2)}, u32[]{:S(2)}) collective-permute-start(f32[3,1,8,256]{3,2,1,0:T(8,128)S(1)} %slice.926), channel_id=1, source_target_pairs={{8,0},{16,8},{24,16},{9,1},{17,9},{25,17},{10,2},{18,10},{26,18},{... | collective-permute-start | bytes 73736 | tf_op jit(solution)/shard_map/ppermute | solution.py:12
  31.5 0.2 fusion.35
  32.2 0.2 fusion.33
  33.0 0.2 fusion.31
  33.8 0.2 fusion.29
  34.6 0.2 fusion.27
  35.4 0.2 fusion.25
  35.8 0.2 pad_multiply_fusion
  36.2 0.5 copy-done.6
  36.8 0.7 add_subtract_fusion
  37.5 1.3 %collective-permute-start.5 = (f32[4,1,8,256]{3,2,1,0:T(8,128)S(1)}, f32[4,1,8,256]{3,2,1,0:T(8,128)S(1)}, u32[]{:S(2)}, u32[]{:S(2)}) collective-permute-start(f32[4,1,8,256]{3,2,1,0:T(8,128)S(1)} %pad_maximum_fusion.8), channel_id=1, source_target_pairs={{8,0},{16,8},{24,16},{9,1},{17,9},{25,17},{10,2},{18,10},{26,18},{... | collective-permute-start | bytes 98312 | tf_op jit(solution)/shard_map/ppermute | solution.py:12
  38.8 4.6 %collective-permute-start.4 = (f32[4,1,8,256]{3,2,1,0:T(8,128)S(1)}, f32[4,1,8,256]{3,2,1,0:T(8,128)S(1)}, u32[]{:S(2)}, u32[]{:S(2)}) collective-permute-start(f32[4,1,8,256]{3,2,1,0:T(8,128)S(1)} %pad_maximum_fusion.8), channel_id=1, source_target_pairs={{0,8},{8,16},{16,24},{1,9},{9,17},{17,25},{2,10},{10,18},{18,26},{... | collective-permute-start | bytes 98312 | tf_op jit(solution)/shard_map/ppermute | solution.py:12
  43.6 0.9 collective-permute-done.4
  44.5 1.3 %collective-permute-start.7 = (f32[4,1,8,256]{3,2,1,0:T(8,128)S(1)}, f32[4,1,8,256]{3,2,1,0:T(8,128)S(1)}, u32[]{:S(2)}, u32[]{:S(2)}) collective-permute-start(f32[4,1,8,256]{3,2,1,0:T(8,128)S(1)} %pad_maximum_fusion.9), channel_id=1, source_target_pairs={{16,0},{24,8},{17,1},{25,9},{18,2},{26,10},{19,3},{27,11},{20,4},{... | collective-permute-start | bytes 98312 | tf_op jit(solution)/shard_map/ppermute | solution.py:12
  45.8 4.9 %collective-permute-start.6 = (f32[4,1,8,256]{3,2,1,0:T(8,128)S(1)}, f32[4,1,8,256]{3,2,1,0:T(8,128)S(1)}, u32[]{:S(2)}, u32[]{:S(2)}) collective-permute-start(f32[4,1,8,256]{3,2,1,0:T(8,128)S(1)} %pad_maximum_fusion.9), channel_id=1, source_target_pairs={{0,16},{8,24},{1,17},{9,25},{2,18},{10,26},{3,19},{11,27},{4,20},{... | collective-permute-start | bytes 98312 | tf_op jit(solution)/shard_map/ppermute | solution.py:12
  50.8 3.8 %collective-permute-start.11 = (f32[4,16,1,256]{3,2,1,0:T(1,128)S(1)}, f32[4,16,1,256]{3,2,1,0:T(1,128)S(1)}, u32[]{:S(2)}, u32[]{:S(2)}) collective-permute-start(f32[4,16,1,256]{3,2,1,0:T(1,128)S(1)} %pad_maximum_fusion.4), channel_id=1, source_target_pairs={{1,0},{2,1},{3,2},{4,3},{5,4},{6,5},{7,6},{9,8},{10,9},{11,10},{12... | collective-permute-start | bytes 196616 | tf_op jit(solution)/shard_map/ppermute | solution.py:12
  54.6 4.5 %collective-permute-start.10 = (f32[4,16,1,256]{3,2,1,0:T(1,128)S(1)}, f32[4,16,1,256]{3,2,1,0:T(1,128)S(1)}, u32[]{:S(2)}, u32[]{:S(2)}) collective-permute-start(f32[4,16,1,256]{3,2,1,0:T(1,128)S(1)} %pad_maximum_fusion.4), channel_id=1, source_target_pairs={{0,1},{1,2},{2,3},{3,4},{4,5},{5,6},{6,7},{8,9},{9,10},{10,11},{11... | collective-permute-start | bytes 196616 | tf_op jit(solution)/shard_map/ppermute | solution.py:12
  59.2 3.7 %collective-permute-start.8 = (f32[1,8,256]{2,1,0:T(8,128)S(1)}, f32[1,8,256]{2,1,0:T(8,128)S(1)}, u32[]{:S(2)}, u32[]{:S(2)}) collective-permute-start(f32[1,8,256]{2,1,0:T(8,128)S(1)} %fusion.98), channel_id=1, source_target_pairs={{0,8},{8,16},{16,24},{1,9},{9,17},{17,25},{2,10},{10,18},{18,26},{... | collective-permute-start | bytes 24584 | tf_op jit(solution)/shard_map/ppermute | solution.py:12
  63.2 1.9 %collective-permute-start.13 = (f32[4,16,1,256]{3,2,1,0:T(1,128)S(1)}, f32[4,16,1,256]{3,2,1,0:T(1,128)S(1)}, u32[]{:S(2)}, u32[]{:S(2)}) collective-permute-start(f32[4,16,1,256]{3,2,1,0:T(1,128)S(1)} %pad_maximum_fusion.5), channel_id=1, source_target_pairs={{2,0},{3,1},{4,2},{5,3},{6,4},{7,5},{10,8},{11,9},{12,10},{13,11},... | collective-permute-start | bytes 196616 | tf_op jit(solution)/shard_map/ppermute | solution.py:12
  65.1 4.3 %collective-permute-start.12 = (f32[4,16,1,256]{3,2,1,0:T(1,128)S(1)}, f32[4,16,1,256]{3,2,1,0:T(1,128)S(1)}, u32[]{:S(2)}, u32[]{:S(2)}) collective-permute-start(f32[4,16,1,256]{3,2,1,0:T(1,128)S(1)} %pad_maximum_fusion.5), channel_id=1, source_target_pairs={{0,2},{1,3},{2,4},{3,5},{4,6},{5,7},{8,10},{9,11},{10,12},{11,13},... | collective-permute-start | bytes 196616 | tf_op jit(solution)/shard_map/ppermute | solution.py:12
  69.4 1.3 %collective-permute-start.19 = (f32[1,8,256]{2,1,0:T(8,128)S(1)}, f32[1,8,256]{2,1,0:T(8,128)S(1)}, u32[]{:S(2)}, u32[]{:S(2)}) collective-permute-start(f32[1,8,256]{2,1,0:T(8,128)S(1)} %slice.1083), channel_id=1, source_target_pairs={{8,0},{16,8},{24,16},{9,1},{17,9},{25,17},{10,2},{18,10},{26,18},{... | collective-permute-start | bytes 24584 | tf_op jit(solution)/shard_map/ppermute | solution.py:12
  71.0 1.3 %collective-permute-start.15 = (f32[4,16,1,256]{3,2,1,0:T(1,128)S(1)}, f32[4,16,1,256]{3,2,1,0:T(1,128)S(1)}, u32[]{:S(2)}, u32[]{:S(2)}) collective-permute-start(f32[4,16,1,256]{3,2,1,0:T(1,128)S(1)} %pad_maximum_fusion.6), channel_id=1, source_target_pairs={{4,0},{5,1},{6,2},{7,3},{12,8},{13,9},{14,10},{15,11},{20,16},{21,... | collective-permute-start | bytes 196616 | tf_op jit(solution)/shard_map/ppermute | solution.py:12
  72.3 4.0 %collective-permute-start.14 = (f32[4,16,1,256]{3,2,1,0:T(1,128)S(1)}, f32[4,16,1,256]{3,2,1,0:T(1,128)S(1)}, u32[]{:S(2)}, u32[]{:S(2)}) collective-permute-start(f32[4,16,1,256]{3,2,1,0:T(1,128)S(1)} %pad_maximum_fusion.6), channel_id=1, source_target_pairs={{0,4},{1,5},{2,6},{3,7},{8,12},{9,13},{10,14},{11,15},{16,20},{17,... | collective-permute-start | bytes 196616 | tf_op jit(solution)/shard_map/ppermute | solution.py:12
  76.3 0.6 collective-permute-done.15
  77.0 0.9 collective-permute-done.14
  78.0 5.3 %collective-permute-start.16 = (f32[16,1,256]{2,1,0:T(1,128)S(1)}, f32[16,1,256]{2,1,0:T(1,128)S(1)}, u32[]{:S(2)}, u32[]{:S(2)}) collective-permute-start(f32[16,1,256]{2,1,0:T(1,128)S(1)} %fusion.59), channel_id=1, source_target_pairs={{0,1},{1,2},{2,3},{3,4},{4,5},{5,6},{6,7},{8,9},{9,10},{10,11},{11... | collective-permute-start | bytes 49160 | tf_op jit(solution)/shard_map/ppermute | solution.py:12
  83.3 0.7 fusion.21
  84.2 1.9 %collective-permute-start.18 = (f32[16,1,256]{2,1,0:T(1,128)S(1)}, f32[16,1,256]{2,1,0:T(1,128)S(1)}, u32[]{:S(2)}, u32[]{:S(2)}) collective-permute-start(f32[16,1,256]{2,1,0:T(1,128)S(1)} %slice.1079), channel_id=1, source_target_pairs={{1,0},{2,1},{3,2},{4,3},{5,4},{6,5},{7,6},{9,8},{10,9},{11,10},{12... | collective-permute-start | bytes 49160 | tf_op jit(solution)/shard_map/ppermute | solution.py:12
  86.1 4.5 %collective-permute-done.18 = f32[16,1,256]{2,1,0:T(1,128)S(1)} collective-permute-done((f32[16,1,256]{2,1,0:T(1,128)S(1)}, f32[16,1,256]{2,1,0:T(1,128)S(1)}, u32[]{:S(2)}, u32[]{:S(2)}) %collective-permute-start.18) | collective-permute-done | bytes 16416 | tf_op jit(solution)/shard_map/ppermute | solution.py:12
  90.7 0.8 fusion.19
  (180 shorter events, 8.1 us)
Async XLA Ops:
  0.6 7.4 %copy-start.1 = (f32[16,8,256]{2,1,0:T(8,128)S(1)}, f32[16,8,256]{2,1,0:T(8,128)}, u32[]{:S(2)}) copy-start(f32[16,8,256]{2,1,0:T(8,128)} %param.13) | copy-start | bytes 393220
  1.4 10.6 %collective-permute-start.1 = (f32[1,8,256]{2,1,0:T(8,128)S(1)}, f32[1,8,256]{2,1,0:T(8,128)S(1)}, u32[]{:S(2)}, u32[]{:S(2)}) collective-permute-start(f32[1,8,256]{2,1,0:T(8,128)S(1)} %slice.674), channel_id=1, source_target_pairs={{8,0},{16,8},{24,16},{9,1},{17,9},{25,17},{10,2},{18,10},{26,18},{... | collective-permute-start | bytes 24584 | tf_op jit(solution)/shard_map/ppermute | solution.py:12
  3.6 13.3 %collective-permute-start.17 = (f32[16,1,256]{2,1,0:T(1,128)S(1)}, f32[16,1,256]{2,1,0:T(1,128)S(1)}, u32[]{:S(2)}, u32[]{:S(2)}) collective-permute-start(f32[16,1,256]{2,1,0:T(1,128)S(1)} %slice.809), channel_id=1, source_target_pairs={{1,0},{2,1},{3,2},{4,3},{5,4},{6,5},{7,6},{9,8},{10,9},{11,10},{12... | collective-permute-start | bytes 49160 | tf_op jit(solution)/shard_map/ppermute | solution.py:12
  9.1 0.9 copy-start
  10.0 0.9 copy-start.4
  11.0 0.9 copy-start.7
  11.9 0.9 copy-start.5
  11.9 1.0 %slice-start = ((f32[16,8,256]{2,1,0:T(8,128)}), f32[15,8,256]{2,1,0:T(8,128)S(1)}, s32[]{:S(2)}) async-start(f32[16,8,256]{2,1,0:T(8,128)} %param.10), calls=%async_computation | async-start | bytes 245760 | tf_op jit(solution)/shard_map/slice | solution.py:16
  13.0 5.0 %collective-permute-start.2 = (f32[3,16,1,256]{3,2,1,0:T(1,128)S(1)}, f32[3,16,1,256]{3,2,1,0:T(1,128)S(1)}, u32[]{:S(2)}, u32[]{:S(2)}) collective-permute-start(f32[3,16,1,256]{3,2,1,0:T(1,128)S(1)} %pad_maximum_fusion.7), channel_id=1, source_target_pairs={{0,1},{1,2},{2,3},{3,4},{4,5},{5,6},{6,7},{8,9},{9,10},{10,11},{11... | collective-permute-start | bytes 147464 | tf_op jit(solution)/shard_map/ppermute | solution.py:12
  16.8 1.2 %copy-start.3 = (f32[16,8,256]{2,1,0:T(8,128)S(1)}, f32[16,8,256]{2,1,0:T(8,128)}, u32[]{:S(2)}) copy-start(f32[16,8,256]{2,1,0:T(8,128)} %param.14) | copy-start | bytes 393220
  18.3 9.3 %collective-permute-start = (f32[3,1,8,256]{3,2,1,0:T(8,128)S(1)}, f32[3,1,8,256]{3,2,1,0:T(8,128)S(1)}, u32[]{:S(2)}, u32[]{:S(2)}) collective-permute-start(f32[3,1,8,256]{3,2,1,0:T(8,128)S(1)} %pad_maximum_fusion.10), channel_id=1, source_target_pairs={{0,8},{8,16},{16,24},{1,9},{9,17},{17,25},{2,10},{10,18},{18,26},{... | collective-permute-start | bytes 73736 | tf_op jit(solution)/shard_map/ppermute | solution.py:12
  24.6 18.8 %collective-permute-start.9 = (f32[3,16,1,256]{3,2,1,0:T(1,128)S(1)}, f32[3,16,1,256]{3,2,1,0:T(1,128)S(1)}, u32[]{:S(2)}, u32[]{:S(2)}) collective-permute-start(f32[3,16,1,256]{3,2,1,0:T(1,128)S(1)} %slice.983), channel_id=1, source_target_pairs={{1,0},{2,1},{3,2},{4,3},{5,4},{6,5},{7,6},{9,8},{10,9},{11,10},{12... | collective-permute-start | bytes 147464 | tf_op jit(solution)/shard_map/ppermute | solution.py:12
  27.5 0.9 copy-start.2
  29.3 8.1 %collective-permute-start.3 = (f32[3,1,8,256]{3,2,1,0:T(8,128)S(1)}, f32[3,1,8,256]{3,2,1,0:T(8,128)S(1)}, u32[]{:S(2)}, u32[]{:S(2)}) collective-permute-start(f32[3,1,8,256]{3,2,1,0:T(8,128)S(1)} %slice.926), channel_id=1, source_target_pairs={{8,0},{16,8},{24,16},{9,1},{17,9},{25,17},{10,2},{18,10},{26,18},{... | collective-permute-start | bytes 73736 | tf_op jit(solution)/shard_map/ppermute | solution.py:12
  36.1 0.7 copy-start.6
  37.5 6.9 %collective-permute-start.5 = (f32[4,1,8,256]{3,2,1,0:T(8,128)S(1)}, f32[4,1,8,256]{3,2,1,0:T(8,128)S(1)}, u32[]{:S(2)}, u32[]{:S(2)}) collective-permute-start(f32[4,1,8,256]{3,2,1,0:T(8,128)S(1)} %pad_maximum_fusion.8), channel_id=1, source_target_pairs={{8,0},{16,8},{24,16},{9,1},{17,9},{25,17},{10,2},{18,10},{26,18},{... | collective-permute-start | bytes 98312 | tf_op jit(solution)/shard_map/ppermute | solution.py:12
  38.8 5.6 %collective-permute-start.4 = (f32[4,1,8,256]{3,2,1,0:T(8,128)S(1)}, f32[4,1,8,256]{3,2,1,0:T(8,128)S(1)}, u32[]{:S(2)}, u32[]{:S(2)}) collective-permute-start(f32[4,1,8,256]{3,2,1,0:T(8,128)S(1)} %pad_maximum_fusion.8), channel_id=1, source_target_pairs={{0,8},{8,16},{16,24},{1,9},{9,17},{17,25},{2,10},{10,18},{18,26},{... | collective-permute-start | bytes 98312 | tf_op jit(solution)/shard_map/ppermute | solution.py:12
  44.5 14.6 %collective-permute-start.7 = (f32[4,1,8,256]{3,2,1,0:T(8,128)S(1)}, f32[4,1,8,256]{3,2,1,0:T(8,128)S(1)}, u32[]{:S(2)}, u32[]{:S(2)}) collective-permute-start(f32[4,1,8,256]{3,2,1,0:T(8,128)S(1)} %pad_maximum_fusion.9), channel_id=1, source_target_pairs={{16,0},{24,8},{17,1},{25,9},{18,2},{26,10},{19,3},{27,11},{20,4},{... | collective-permute-start | bytes 98312 | tf_op jit(solution)/shard_map/ppermute | solution.py:12
  45.8 13.3 %collective-permute-start.6 = (f32[4,1,8,256]{3,2,1,0:T(8,128)S(1)}, f32[4,1,8,256]{3,2,1,0:T(8,128)S(1)}, u32[]{:S(2)}, u32[]{:S(2)}) collective-permute-start(f32[4,1,8,256]{3,2,1,0:T(8,128)S(1)} %pad_maximum_fusion.9), channel_id=1, source_target_pairs={{0,16},{8,24},{1,17},{9,25},{2,18},{10,26},{3,19},{11,27},{4,20},{... | collective-permute-start | bytes 98312 | tf_op jit(solution)/shard_map/ppermute | solution.py:12
  50.8 12.2 %collective-permute-start.11 = (f32[4,16,1,256]{3,2,1,0:T(1,128)S(1)}, f32[4,16,1,256]{3,2,1,0:T(1,128)S(1)}, u32[]{:S(2)}, u32[]{:S(2)}) collective-permute-start(f32[4,16,1,256]{3,2,1,0:T(1,128)S(1)} %pad_maximum_fusion.4), channel_id=1, source_target_pairs={{1,0},{2,1},{3,2},{4,3},{5,4},{6,5},{7,6},{9,8},{10,9},{11,10},{12... | collective-permute-start | bytes 196616 | tf_op jit(solution)/shard_map/ppermute | solution.py:12
  54.6 8.3 %collective-permute-start.10 = (f32[4,16,1,256]{3,2,1,0:T(1,128)S(1)}, f32[4,16,1,256]{3,2,1,0:T(1,128)S(1)}, u32[]{:S(2)}, u32[]{:S(2)}) collective-permute-start(f32[4,16,1,256]{3,2,1,0:T(1,128)S(1)} %pad_maximum_fusion.4), channel_id=1, source_target_pairs={{0,1},{1,2},{2,3},{3,4},{4,5},{5,6},{6,7},{8,9},{9,10},{10,11},{11... | collective-permute-start | bytes 196616 | tf_op jit(solution)/shard_map/ppermute | solution.py:12
  59.2 10.2 %collective-permute-start.8 = (f32[1,8,256]{2,1,0:T(8,128)S(1)}, f32[1,8,256]{2,1,0:T(8,128)S(1)}, u32[]{:S(2)}, u32[]{:S(2)}) collective-permute-start(f32[1,8,256]{2,1,0:T(8,128)S(1)} %fusion.98), channel_id=1, source_target_pairs={{0,8},{8,16},{16,24},{1,9},{9,17},{17,25},{2,10},{10,18},{18,26},{... | collective-permute-start | bytes 24584 | tf_op jit(solution)/shard_map/ppermute | solution.py:12
  63.2 7.6 %collective-permute-start.13 = (f32[4,16,1,256]{3,2,1,0:T(1,128)S(1)}, f32[4,16,1,256]{3,2,1,0:T(1,128)S(1)}, u32[]{:S(2)}, u32[]{:S(2)}) collective-permute-start(f32[4,16,1,256]{3,2,1,0:T(1,128)S(1)} %pad_maximum_fusion.5), channel_id=1, source_target_pairs={{2,0},{3,1},{4,2},{5,3},{6,4},{7,5},{10,8},{11,9},{12,10},{13,11},... | collective-permute-start | bytes 196616 | tf_op jit(solution)/shard_map/ppermute | solution.py:12
  65.1 5.6 %collective-permute-start.12 = (f32[4,16,1,256]{3,2,1,0:T(1,128)S(1)}, f32[4,16,1,256]{3,2,1,0:T(1,128)S(1)}, u32[]{:S(2)}, u32[]{:S(2)}) collective-permute-start(f32[4,16,1,256]{3,2,1,0:T(1,128)S(1)} %pad_maximum_fusion.5), channel_id=1, source_target_pairs={{0,2},{1,3},{2,4},{3,5},{4,6},{5,7},{8,10},{9,11},{10,12},{11,13},... | collective-permute-start | bytes 196616 | tf_op jit(solution)/shard_map/ppermute | solution.py:12
  69.4 13.8 %collective-permute-start.19 = (f32[1,8,256]{2,1,0:T(8,128)S(1)}, f32[1,8,256]{2,1,0:T(8,128)S(1)}, u32[]{:S(2)}, u32[]{:S(2)}) collective-permute-start(f32[1,8,256]{2,1,0:T(8,128)S(1)} %slice.1083), channel_id=1, source_target_pairs={{8,0},{16,8},{24,16},{9,1},{17,9},{25,17},{10,2},{18,10},{26,18},{... | collective-permute-start | bytes 24584 | tf_op jit(solution)/shard_map/ppermute | solution.py:12
  71.0 5.9 %collective-permute-start.15 = (f32[4,16,1,256]{3,2,1,0:T(1,128)S(1)}, f32[4,16,1,256]{3,2,1,0:T(1,128)S(1)}, u32[]{:S(2)}, u32[]{:S(2)}) collective-permute-start(f32[4,16,1,256]{3,2,1,0:T(1,128)S(1)} %pad_maximum_fusion.6), channel_id=1, source_target_pairs={{4,0},{5,1},{6,2},{7,3},{12,8},{13,9},{14,10},{15,11},{20,16},{21,... | collective-permute-start | bytes 196616 | tf_op jit(solution)/shard_map/ppermute | solution.py:12
  72.3 5.5 %collective-permute-start.14 = (f32[4,16,1,256]{3,2,1,0:T(1,128)S(1)}, f32[4,16,1,256]{3,2,1,0:T(1,128)S(1)}, u32[]{:S(2)}, u32[]{:S(2)}) collective-permute-start(f32[4,16,1,256]{3,2,1,0:T(1,128)S(1)} %pad_maximum_fusion.6), channel_id=1, source_target_pairs={{0,4},{1,5},{2,6},{3,7},{8,12},{9,13},{10,14},{11,15},{16,20},{17,... | collective-permute-start | bytes 196616 | tf_op jit(solution)/shard_map/ppermute | solution.py:12
  78.0 6.1 %collective-permute-start.16 = (f32[16,1,256]{2,1,0:T(1,128)S(1)}, f32[16,1,256]{2,1,0:T(1,128)S(1)}, u32[]{:S(2)}, u32[]{:S(2)}) collective-permute-start(f32[16,1,256]{2,1,0:T(1,128)S(1)} %fusion.59), channel_id=1, source_target_pairs={{0,1},{1,2},{2,3},{3,4},{4,5},{5,6},{6,7},{8,9},{9,10},{10,11},{11... | collective-permute-start | bytes 49160 | tf_op jit(solution)/shard_map/ppermute | solution.py:12
  84.2 6.5 %collective-permute-start.18 = (f32[16,1,256]{2,1,0:T(1,128)S(1)}, f32[16,1,256]{2,1,0:T(1,128)S(1)}, u32[]{:S(2)}, u32[]{:S(2)}) collective-permute-start(f32[16,1,256]{2,1,0:T(1,128)S(1)} %slice.1079), channel_id=1, source_target_pairs={{1,0},{2,1},{3,2},{4,3},{5,4},{6,5},{7,6},{9,8},{10,9},{11,10},{12... | collective-permute-start | bytes 49160 | tf_op jit(solution)/shard_map/ppermute | solution.py:12
where the time goes:
time: 92.2 us; the launch traced here: 91.5 us
  starting transfers between devices  60 us (65%)
  local copies, waits for them, and re-layouts  11.9 us (13%)
  other arithmetic  9.33 us (10%)
  waiting for transfers between devices  8.17 us (9%)
  between operations  2.06 us (2%)
    ppermute x20, starting transfers between devices, passed_along(): lax.ppermute(value, axis, [(source, source + steps) for source in range(f...  60 us
    ppermute x20, waiting for transfers between devices, passed_along(): lax.ppermute(value, axis, [(source, source + steps) for source in range(f...  8.17 us
    slice x74, local copies, waits for them, and re-layouts, take_rows(): return lax.slice_in_dim(values, start, start + length, axis=direction)  5.34 us
    unnamed x18, local copies, waits for them, and re-layouts  4.85 us
    add x12, other arithmetic, reduce_lines(): right_side + ratio_low[None] * low_right + ratio_high[None] * high_right  2.04 us
  transfers between devices with their start and end apart: 20, of which 6 were waited for; matrix products, arithmetic and copies ran while one was open for 16% of the time, Pallas kernels for 0%

commit v1 on v0

--- a/solution.py
+++ b/solution.py
@@ -77,124 +77,63 @@
     return (lower_band, main_band, upper_band)
 
 
-def chain_solve(
-    reduced_low,
-    reduced_mid,
-    reduced_high,
-    reduced_right,
-    total_devices,
-    position,
-    lower_shift,
-    upper_shift,
-):
-    stride = 1
-    while stride < total_devices:
-        stacked = jnp.stack([reduced_low, reduced_mid, reduced_high, reduced_right])
-        from_below = lower_shift(stacked, stride)
-        from_above = upper_shift(stacked, stride)
-        below_main = jnp.where(position >= stride, from_below[1], 1.0)
-        above_main = jnp.where(position + stride < total_devices, from_above[1], 1.0)
-        ratio_low = -reduced_low / below_main
-        ratio_high = -reduced_high / above_main
-        reduced_right = reduced_right + ratio_low * from_below[3] + ratio_high * from_above[3]
-        reduced_mid = reduced_mid + ratio_low * from_below[2] + ratio_high * from_above[0]
-        reduced_low = ratio_low * from_below[0]
-        reduced_high = ratio_high * from_above[2]
-        stride = stride * 2
-    return reduced_right / reduced_mid
-
-
-def partitioned(
-    lower_band, main_band, upper_band, right_side, direction, send_heads, solve_reduced, send_last
-):
+def gathered(values, axis):
+    return lax.all_gather(values, axis)
+
+
+def block_spikes(lower_band, main_band, upper_band, right_side, direction):
     length = main_band.shape[direction]
-    inner_rows = length - 1
-    low_inner = take_rows(lower_band, direction, 0, inner_rows)
-    main_inner = take_rows(main_band, direction, 0, inner_rows)
-    up_inner = take_rows(upper_band, direction, 0, inner_rows)
-    row_index = lax.broadcasted_iota(jnp.int32, low_inner.shape, direction)
+    row_index = lax.broadcasted_iota(jnp.int32, main_band.shape, direction)
     first_row = row_index == 0
-    last_inner = row_index == inner_rows - 1
-    left_column = jnp.where(first_row, -low_inner, 0.0)
-    right_column = jnp.where(last_inner, -up_inner, 0.0)
-    low_inner = jnp.where(first_row, 0.0, low_inner)
-    up_inner = jnp.where(last_inner, 0.0, up_inner)
-    stacked = jnp.stack(
-        [take_rows(right_side, direction, 0, inner_rows), left_column, right_column]
-    )
-    solved = reduce_lines(low_inner, main_inner, up_inner, stacked, direction)
-    next_heads = send_heads(take_rows(solved, direction + 1, 0, 1))
-    own_tails = take_rows(solved, direction + 1, inner_rows - 1, 1)
-    low_last = take_rows(lower_band, direction, inner_rows, 1)
-    main_last = take_rows(main_band, direction, inner_rows, 1)
-    up_last = take_rows(upper_band, direction, inner_rows, 1)
-    right_last = take_rows(right_side, direction, inner_rows, 1)
-    reduced_low = low_last * own_tails[1]
-    reduced_mid = main_last + low_last * own_tails[2] + up_last * next_heads[1]
-    reduced_high = up_last * next_heads[2]
-    reduced_right = right_last - low_last * own_tails[0] - up_last * next_heads[0]
-    interface = solve_reduced(reduced_low, reduced_mid, reduced_high, reduced_right)
-    earlier = send_last(interface)
-    interior = solved[0] + solved[1] * earlier + solved[2] * interface
-    return jnp.concatenate([interior, interface], axis=direction)
-
-
-def z_heads(values):
-    return passed_along(values, "gz", -1)
-
-
-def z_earlier(values):
-    return passed_along(values, "gz", 1)
-
-
-def z_chain_below(values, stride):
-    return passed_along(values, "gz", stride)
-
-
-def z_chain_above(values, stride):
-    return passed_along(values, "gz", -stride)
-
-
-def z_reduced_chain(reduced_low, reduced_mid, reduced_high, reduced_right):
-    return chain_solve(
-        reduced_low,
-        reduced_mid,
-        reduced_high,
-        reduced_right,
-        lax.axis_size("gz"),
-        lax.axis_index("gz"),
-        z_chain_below,
-        z_chain_above,
-    )
-
-
-def y_heads(values):
-    return passed_along(values, "gy", -1)
-
-
-def y_earlier(values):
-    return passed_along(values, "gy", 1)
-
-
-def y_chain_below(values, stride):
-    return passed_along(values, "gy", stride)
-
-
-def y_chain_above(values, stride):
-    return passed_along(values, "gy", -stride)
-
-
-def y_reduced_chain(reduced_low, reduced_mid, reduced_high, reduced_right):
-    return chain_solve(
-        reduced_low,
-        reduced_mid,
-        reduced_high,
-        reduced_right,
-        lax.axis_size("gy"),
-        lax.axis_index("gy"),
-        y_chain_below,
-        y_chain_above,
-    )
+    last_row = row_index == length - 1
+    left_column = jnp.where(first_row, -lower_band, 0.0)
+    right_column = jnp.where(last_row, -upper_band, 0.0)
+    inner_lower = jnp.where(first_row, 0.0, lower_band)
+    inner_upper = jnp.where(last_row, 0.0, upper_band)
+    stacked = jnp.stack([right_side, left_column, right_column])
+    return reduce_lines(inner_lower, main_band, inner_upper, stacked, direction)
+
+
+def interface_sweep(coefficients, position):
+    blocks = coefficients.shape[0]
+    alpha = jnp.zeros_like(coefficients[0, 0])
+    beta = jnp.zeros_like(alpha)
+    carried = []
+    for block in range(blocks):
+        a0, a1, a2, b0, b1, b2 = [coefficients[block, index] for index in range(6)]
+        scale = 1.0 / (1.0 - a1 * beta)
+        p_term = (a0 + a1 * alpha) * scale
+        q_term = a2 * scale
+        carried.append((alpha, beta, p_term, q_term))
+        alpha = b0 + b1 * (alpha + beta * p_term)
+        beta = b1 * beta * q_term + b2
+    following = jnp.zeros_like(alpha)
+    firsts = [None] * blocks
+    earlier_lasts = [None] * blocks
+    for block in reversed(range(blocks)):
+        alpha_before, beta_before, p_term, q_term = carried[block]
+        first_value = p_term + q_term * following
+        firsts[block] = first_value
+        earlier_lasts[block] = alpha_before + beta_before * first_value
+        following = first_value
+    nexts = jnp.stack(firsts[1:] + [jnp.zeros_like(alpha)])
+    earlier = jnp.stack(earlier_lasts)
+    return (
+        lax.dynamic_index_in_dim(earlier, position, 0, keepdims=False),
+        lax.dynamic_index_in_dim(nexts, position, 0, keepdims=False),
+    )
+
+
+def partitioned(lower_band, main_band, upper_band, right_side, direction, axis):
+    length = main_band.shape[direction]
+    solved = block_spikes(lower_band, main_band, upper_band, right_side, direction)
+    edges = jnp.concatenate(
+        [take_rows(solved, direction + 1, 0, 1), take_rows(solved, direction + 1, length - 1, 1)]
+    )
+    everyone = gathered(edges, axis)
+    earlier, following = interface_sweep(everyone, lax.axis_index(axis))
+    result = solved[0] + solved[1] * earlier + solved[2] * following
+    return result, following
 
 
 def body(
@@ -260,16 +199,10 @@
     half_electric_z = reduce_lines(lower_x, main_x, upper_x, source_z[None], 2)[0]
     index_z = lax.broadcasted_iota(jnp.int32, coupling.shape, 1) + lax.axis_index("gz") * size_z
     lower_z, main_z, upper_z = bands(coupling, damping, index_z, size_z * lax.axis_size("gz"))
-    half_electric_y = partitioned(
-        lower_z, main_z, upper_z, source_y, 1, z_heads, z_reduced_chain, z_earlier
-    )
+    half_electric_y, fresh_ey = partitioned(lower_z, main_z, upper_z, source_y, 1, "gz")
     index_y = lax.broadcasted_iota(jnp.int32, coupling.shape, 0) + lax.axis_index("gy") * size_y
     lower_y, main_y, upper_y = bands(coupling, damping, index_y, size_y * lax.axis_size("gy"))
-    half_electric_x = partitioned(
-        lower_y, main_y, upper_y, source_x, 0, y_heads, y_reduced_chain, y_earlier
-    )
-    fresh_ex = passed_along(take_rows(half_electric_x, 0, 0, 1), "gy", -1)
-    fresh_ey = passed_along(take_rows(half_electric_y, 1, 0, 1), "gz", -1)
+    half_electric_x, fresh_ex = partitioned(lower_y, main_y, upper_y, source_x, 0, "gy")
     half_magnetic_x = magnetic_x + ahead_diff(half_electric_y, 1, fresh_ey) - cross_z
     half_magnetic_y = (
         magnetic_y + ahead_diff(half_electric_z, 2, edge_zeros(half_electric_z, 2)) - cross_x
@@ -286,27 +219,11 @@
 
 
 def solution(mesh):
-    placed = (
-        P("gy", "gz", None),
-        P("gy", "gz", None),
-        P("gy", "gz", None),
-        P("gy", "gz", None),
-        P("gy", "gz", None),
-        P("gy", "gz", None),
-        P("gy", "gz", None),
-        P("gy", "gz", None),
-    )
+    placed = (P("gy", "gz", None),) * 8
     return jax.shard_map(
         body,
         mesh=mesh,
         in_specs=placed,
-        out_specs=(
-            P("gy", "gz", None),
-            P("gy", "gz", None),
-            P("gy", "gz", None),
-            P("gy", "gz", None),
-            P("gy", "gz", None),
-            P("gy", "gz", None),
-        ),
+        out_specs=(P("gy", "gz", None),) * 6,
         check_vma=False,
     )

time: 92.2 us -> 67.8 us (0.74)
  the two profiles are of different devices: /device:TPU:3 before, /device:TPU:0 now
where the time goes in v1:
time: 67.8 us; the launch traced here: 67.3 us
  blocking collectives  29.1 us (43%)
  local copies, waits for them, and re-layouts  13.7 us (20%)
  starting transfers between devices  11.2 us (17%)
  other arithmetic  9.39 us (14%)
  waiting for transfers between devices  2.19 us (3%)
  between operations  1.83 us (3%)
    all_gather x2, blocking collectives, gathered(): return lax.all_gather(values, axis)  29.1 us
    ppermute x4, starting transfers between devices, passed_along(): lax.ppermute(value, axis, [(source, source + steps) for source in range(f...  11.2 us
    unnamed x22, local copies, waits for them, and re-layouts  6.21 us
    slice x74, local copies, waits for them, and re-layouts, take_rows(): return lax.slice_in_dim(values, start, start + length, axis=direction)  5.69 us
    ppermute x4, waiting for transfers between devices, passed_along(): lax.ppermute(value, axis, [(source, source + steps) for source in range(f...  2.19 us
    add x12, other arithmetic, reduce_lines(): right_side + ratio_low[None] * low_right + ratio_high[None] * high_right  1.88 us
  transfers between devices with their start and end apart: 4, of which 2 were waited for; matrix products, arithmetic and copies ran while one was open for 6% of the time, Pallas kernels for 0%

profile of v1, /device:TPU:0, one launch (start us, length us, event | category | flops | bytes accessed | tf_op | source)
XLA Modules:
  0.0 67.3 jit_solution(7507523967147730777)
XLA Ops:
  0.6 0.7 %slice.668 = f32[1,8,256]{2,1,0:T(8,128)S(1)} slice(f32[16,8,256]{2,1,0:T(8,128)} %param.10), slice={[0:1], [0:8], [0:256]} | slice | bytes 16384 | tf_op jit(solution)/shard_map/slice | solution.py:16
  1.4 1.3 %collective-permute-start.1 = (f32[1,8,256]{2,1,0:T(8,128)S(1)}, f32[1,8,256]{2,1,0:T(8,128)S(1)}, u32[]{:S(2)}, u32[]{:S(2)}) collective-permute-start(f32[1,8,256]{2,1,0:T(8,128)S(1)} %slice.668), channel_id=1, source_target_pairs={{8,0},{16,8},{24,16},{9,1},{17,9},{25,17},{10,2},{18,10},{26,18},{... | collective-permute-start | bytes 24584 | tf_op jit(solution)/shard_map/ppermute | solution.py:12
  2.7 0.9 %slice.807 = f32[16,1,256]{2,1,0:T(1,128)S(1)} slice(f32[16,8,256]{2,1,0:T(8,128)} %param.8), slice={[0:16], [0:1], [0:256]} | slice | bytes 32768 | tf_op jit(solution)/shard_map/slice | solution.py:16
  3.6 1.3 %collective-permute-start.3 = (f32[16,1,256]{2,1,0:T(1,128)S(1)}, f32[16,1,256]{2,1,0:T(1,128)S(1)}, u32[]{:S(2)}, u32[]{:S(2)}) collective-permute-start(f32[16,1,256]{2,1,0:T(1,128)S(1)} %slice.807), channel_id=1, source_target_pairs={{1,0},{2,1},{3,2},{4,3},{5,4},{6,5},{7,6},{9,8},{10,9},{11,10},{12... | collective-permute-start | bytes 49160 | tf_op jit(solution)/shard_map/ppermute | solution.py:12
  5.0 0.9 %slice_bitcast_fusion.10 = f32[1,16,1,256]{3,2,1,0:T(1,128)S(1)} fusion(f32[16,8,256]{2,1,0:T(8,128)} %param.11), kind=kLoop, calls=%fused_computation.302 | loop fusion | bytes 32768 | tf_op jit(solution)/shard_map/stack | solution.py:170
  6.0 0.7 %slice_bitcast_fusion.34 = f32[1,1,8,256]{3,2,1,0:T(8,128)S(1)} fusion(f32[16,8,256]{2,1,0:T(8,128)} %param.11), kind=kLoop, calls=%fused_computation.365 | loop fusion | bytes 16384 | tf_op jit(solution)/shard_map/stack | solution.py:157
  6.7 1.1 %select_select_fusion = (f32[16,8,256]{2,1,0:T(8,128)S(1)}, f32[1,16,8,256]{3,2,1,0:T(8,128)S(1)}, f32[16,8,256]{2,1,0:T(8,128)S(1)}, f32[16,8,256]{2,1,0:T(8,12...) fusion(pred[8]{0:T(512)(128)(4,1)S(1)} %fusion.111, pred[8]{0:T(512)(128)(4,1)S(1)} %iota_compare_fusion.2, ...), kind=kLoop, calls=%fused_computation.160 | loop fusion | flops 458752 | bytes 1049648 | tf_op jit(solution)/shard_map/jit(_where)/select_n | solution.py:92
  7.8 0.9 %copy-done.1 = f32[16,8,256]{2,1,0:T(8,128)S(1)} copy-done((f32[16,8,256]{2,1,0:T(8,128)S(1)}, f32[16,8,256]{2,1,0:T(8,128)}, u32[]{:S(2)}) %copy-start.1) | copy-done | bytes 131096
  8.9 0.9 %copy-done.4 = f32[16,8,256]{2,1,0:T(8,128)S(1)} copy-done((f32[16,8,256]{2,1,0:T(8,128)S(1)}, f32[16,8,256]{2,1,0:T(8,128)}, u32[]{:S(2)}) %copy-start.4) | copy-done | bytes 131096
  9.8 0.9 %copy-done = f32[16,8,256]{2,1,0:T(8,128)S(1)} copy-done((f32[16,8,256]{2,1,0:T(8,128)S(1)}, f32[16,8,256]{2,1,0:T(8,128)}, u32[]{:S(2)}) %copy-start) | copy-done | bytes 131096
  10.7 0.9 %copy-done.7 = f32[16,8,256]{2,1,0:T(8,128)S(1)} copy-done((f32[16,8,256]{2,1,0:T(8,128)S(1)}, f32[16,8,256]{2,1,0:T(8,128)}, u32[]{:S(2)}) %copy-start.7) | copy-done | bytes 131096
  11.7 0.8 %copy-done.5 = f32[16,8,256]{2,1,0:T(8,128)S(1)} copy-done((f32[16,8,256]{2,1,0:T(8,128)S(1)}, f32[16,8,256]{2,1,0:T(8,128)}, u32[]{:S(2)}) %copy-start.5) | copy-done | bytes 131096
  12.6 3.0 %collective-permute-start.2 = (f32[3,16,1,256]{3,2,1,0:T(1,128)S(1)}, f32[3,16,1,256]{3,2,1,0:T(1,128)S(1)}, u32[]{:S(2)}, u32[]{:S(2)}) collective-permute-start(f32[3,16,1,256]{3,2,1,0:T(1,128)S(1)} %pad_maximum_fusion.3), channel_id=1, source_target_pairs={{0,1},{1,2},{2,3},{3,4},{4,5},{5,6},{6,7},{8,9},{9,10},{10,11},{11... | collective-permute-start | bytes 147464 | tf_op jit(solution)/shard_map/ppermute | solution.py:12
  15.7 0.8 %collective-permute-done.2 = f32[3,16,1,256]{3,2,1,0:T(1,128)S(1)} collective-permute-done((f32[3,16,1,256]{3,2,1,0:T(1,128)S(1)}, f32[3,16,1,256]{3,2,1,0:T(1,128)S(1)}, u32[]{:S(2)}, u32[]{:S(2)}) %collective-permute-start.2) | collective-permute-done | bytes 49184 | tf_op jit(solution)/shard_map/ppermute | solution.py:12
  16.6 0.2 select_select_fusion.1
  17.6 5.6 %collective-permute-start = (f32[3,1,8,256]{3,2,1,0:T(8,128)S(1)}, f32[3,1,8,256]{3,2,1,0:T(8,128)S(1)}, u32[]{:S(2)}, u32[]{:S(2)}) collective-permute-start(f32[3,1,8,256]{3,2,1,0:T(8,128)S(1)} %pad_maximum_fusion.5), channel_id=1, source_target_pairs={{0,8},{8,16},{16,24},{1,9},{9,17},{17,25},{2,10},{10,18},{18,26},{... | collective-permute-start | bytes 73736 | tf_op jit(solution)/shard_map/ppermute | solution.py:12
  23.2 1.4 %collective-permute-done = f32[3,1,8,256]{3,2,1,0:T(8,128)S(1)} collective-permute-done((f32[3,1,8,256]{3,2,1,0:T(8,128)S(1)}, f32[3,1,8,256]{3,2,1,0:T(8,128)S(1)}, u32[]{:S(2)}, u32[]{:S(2)}) %collective-permute-start) | collective-permute-done | bytes 24608 | tf_op jit(solution)/shard_map/ppermute | solution.py:12
  24.6 0.2 fusion.21
  24.9 0.1 fusion.41
  25.2 0.1 fusion.177
  25.3 0.2 pad_multiply_fusion.16
  25.9 0.1 multiply_add_fusion.1
  26.1 0.1 multiply_add_fusion
  26.4 0.1 add_divide_fusion
  26.7 14.4 %all-gather.1 = f32[48,16,1,256]{3,1,2,0:T(8,128)S(1)} all-gather(f32[6,16,1,256]{3,1,2,0:T(8,128)S(1)} %copy.56), channel_id=3, replica_groups=mesh['gy'=4,'gz'=8] {'gz'}, dimensions={0}, use_global_device_ids=true | all-gather | bytes 884736 | tf_op jit(solution)/shard_map/all_gather | solution.py:81
  41.2 0.7 fusion.54
  41.8 0.4 constant_dynamic-update-slice_fusion.7
  43.2 14.6 %all-gather = f32[24,1,8,256]{3,2,1,0:T(8,128)S(1)} all-gather(f32[6,1,8,256]{3,2,1,0:T(8,128)S(1)} %pad_maximum_fusion.4), channel_id=2, replica_groups=mesh['gy'=4,'gz'=8] {'gy'}, dimensions={0}, use_global_device_ids=true | all-gather | bytes 245760 | tf_op jit(solution)/shard_map/all_gather | solution.py:81
  58.1 0.6 copy-done.9
  58.8 0.1 fusion.179
  58.9 0.2 fusion.39
  59.3 0.1 multiply_add_fusion.10
  59.7 0.2 fusion.37
  60.1 0.1 multiply_add_fusion.9
  60.4 0.2 fusion.35
  60.9 0.1 multiply_add_fusion.8
  61.2 0.2 fusion.33
  61.6 0.1 multiply_add_fusion.7
  62.0 0.2 fusion.31
  62.4 0.1 multiply_add_fusion.6
  62.8 0.2 fusion.29
  63.2 0.2 pad_multiply_fusion
  63.6 0.5 copy-done.6
  64.2 0.7 %add_subtract_fusion = f32[16,8,256]{2,1,0:T(8,128)} fusion(f32[16,8,256]{2,1,0:T(8,128)S(1)} %maximum_subtract_fusion.6, f32[16,8,256]{2,1,0:T(8,128)S(1)} %copy-done.2, f32[16,8,256]{2,1,0:T(8,128)S(1)} %fusion.26, f32[16,8,255]{2,1,0:T(8,128)S(1)} %slice.1078), kind=kLoop, calls=%fused_computation.85 | loop fusion | flops 98304 | bytes 654848 | tf_op jit(solution)/shard_map/sub | solution.py:208
  65.0 0.6 copy-done.8
  65.6 0.3 slice-done.1
  65.9 0.7 %fusion.25 = f32[16,8,256]{2,1,0:T(8,128)} fusion(f32[16,8,256]{2,1,0:T(8,128)S(1)} %get-tuple-element.255, f32[16,8,256]{2,1,0:T(8,128)S(1)} %copy-done.1, f32[1,8,256]{2,1,0:T(8,128)S(1)} %bitcast.697, f32[15,8,256]{2,1,0:T(8,128)S(1)} %slice-done.1, f32[8,256]{1,0:T(8,128)S(1)} %bitcast.696, f32[3,16,8,256]{3,2,1,0:T(8,128)S(1)} %add_divide_fusion.1, ...), kind=kLoop, calls=%fused_computation.50 | loop fusion | flops 262144 | bytes 933888 | tf_op jit(solution)/shard_map/sub | solution.py:210
  66.6 0.7 %fusion.23 = f32[16,8,256]{2,1,0:T(8,128)} fusion(f32[16,8,256]{2,1,0:T(8,128)S(1)} %maximum_subtract_fusion.2, f32[16,8,256]{2,1,0:T(8,128)S(1)} %copy-done, f32[16,1,256]{2,1,0:T(1,128)S(1)} %fusion.199, f32[16,7,256]{2,1,0:T(8,128)S(1)} %slice.1077, f32[16,256]{1,0:T(8,128)S(1)} %bitcast.692, f32[3,16,8,256]{3,2,1,0:T(8,128)S(1)} %add_divide_fusion, ...), kind=kLoop, calls=%fused_computation.47 | loop fusion | flops 262144 | bytes 950272 | tf_op jit(solution)/shard_map/sub | solution.py:206
  (155 shorter events, 5.7 us)
Async XLA Ops:
  0.6 6.0 %copy-start.2 = (f32[16,8,256]{2,1,0:T(8,128)S(1)}, f32[16,8,256]{2,1,0:T(8,128)}, u32[]{:S(2)}) copy-start(f32[16,8,256]{2,1,0:T(8,128)} %param.12) | copy-start | bytes 393220
  1.4 10.3 %collective-permute-start.1 = (f32[1,8,256]{2,1,0:T(8,128)S(1)}, f32[1,8,256]{2,1,0:T(8,128)S(1)}, u32[]{:S(2)}, u32[]{:S(2)}) collective-permute-start(f32[1,8,256]{2,1,0:T(8,128)S(1)} %slice.668), channel_id=1, source_target_pairs={{8,0},{16,8},{24,16},{9,1},{17,9},{25,17},{10,2},{18,10},{26,18},{... | collective-permute-start | bytes 24584 | tf_op jit(solution)/shard_map/ppermute | solution.py:12
  3.6 12.1 %collective-permute-start.3 = (f32[16,1,256]{2,1,0:T(1,128)S(1)}, f32[16,1,256]{2,1,0:T(1,128)S(1)}, u32[]{:S(2)}, u32[]{:S(2)}) collective-permute-start(f32[16,1,256]{2,1,0:T(1,128)S(1)} %slice.807), channel_id=1, source_target_pairs={{1,0},{2,1},{3,2},{4,3},{5,4},{6,5},{7,6},{9,8},{10,9},{11,10},{12... | collective-permute-start | bytes 49160 | tf_op jit(solution)/shard_map/ppermute | solution.py:12
  7.8 0.9 %copy-start.1 = (f32[16,8,256]{2,1,0:T(8,128)S(1)}, f32[16,8,256]{2,1,0:T(8,128)}, u32[]{:S(2)}) copy-start(f32[16,8,256]{2,1,0:T(8,128)} %param.13) | copy-start | bytes 393220
  8.8 0.9 %copy-start.4 = (f32[16,8,256]{2,1,0:T(8,128)S(1)}, f32[16,8,256]{2,1,0:T(8,128)}, u32[]{:S(2)}) copy-start(f32[16,8,256]{2,1,0:T(8,128)} %param.8) | copy-start | bytes 393220
  9.8 0.9 %copy-start = (f32[16,8,256]{2,1,0:T(8,128)S(1)}, f32[16,8,256]{2,1,0:T(8,128)}, u32[]{:S(2)}) copy-start(f32[16,8,256]{2,1,0:T(8,128)} %param.11) | copy-start | bytes 393220
  10.7 0.9 %copy-start.7 = (f32[16,8,256]{2,1,0:T(8,128)S(1)}, f32[16,8,256]{2,1,0:T(8,128)}, u32[]{:S(2)}) copy-start(f32[16,8,256]{2,1,0:T(8,128)} %param.9) | copy-start | bytes 393220
  11.6 0.9 %copy-start.5 = (f32[16,8,256]{2,1,0:T(8,128)S(1)}, f32[16,8,256]{2,1,0:T(8,128)}, u32[]{:S(2)}) copy-start(f32[16,8,256]{2,1,0:T(8,128)} %param.10) | copy-start | bytes 393220
  11.6 1.0 %slice-start = ((f32[16,8,256]{2,1,0:T(8,128)}), f32[15,8,256]{2,1,0:T(8,128)S(1)}, s32[]{:S(2)}) async-start(f32[16,8,256]{2,1,0:T(8,128)} %param.10), calls=%async_computation | async-start | bytes 245760 | tf_op jit(solution)/shard_map/slice | solution.py:16
  12.6 3.9 %collective-permute-start.2 = (f32[3,16,1,256]{3,2,1,0:T(1,128)S(1)}, f32[3,16,1,256]{3,2,1,0:T(1,128)S(1)}, u32[]{:S(2)}, u32[]{:S(2)}) collective-permute-start(f32[3,16,1,256]{3,2,1,0:T(1,128)S(1)} %pad_maximum_fusion.3), channel_id=1, source_target_pairs={{0,1},{1,2},{2,3},{3,4},{4,5},{5,6},{6,7},{8,9},{9,10},{10,11},{11... | collective-permute-start | bytes 147464 | tf_op jit(solution)/shard_map/ppermute | solution.py:12
  15.7 0.9 %copy-start.3 = (f32[16,8,256]{2,1,0:T(8,128)S(1)}, f32[16,8,256]{2,1,0:T(8,128)}, u32[]{:S(2)}) copy-start(f32[16,8,256]{2,1,0:T(8,128)} %param.14) | copy-start | bytes 393220
  17.6 7.1 %collective-permute-start = (f32[3,1,8,256]{3,2,1,0:T(8,128)S(1)}, f32[3,1,8,256]{3,2,1,0:T(8,128)S(1)}, u32[]{:S(2)}, u32[]{:S(2)}) collective-permute-start(f32[3,1,8,256]{3,2,1,0:T(8,128)S(1)} %pad_maximum_fusion.5), channel_id=1, source_target_pairs={{0,8},{8,16},{16,24},{1,9},{9,17},{17,25},{2,10},{10,18},{18,26},{... | collective-permute-start | bytes 73736 | tf_op jit(solution)/shard_map/ppermute | solution.py:12
  58.0 0.7 copy-start.9
  63.5 0.7 copy-start.6
  64.9 0.7 copy-start.8
  64.9 1.0 %slice-start.1 = ((f32[16,8,256]{2,1,0:T(8,128)}), f32[15,8,256]{2,1,0:T(8,128)S(1)}, s32[]{:S(2)}) async-start(f32[16,8,256]{2,1,0:T(8,128)} %copy-done.9), calls=%async_computation.1 | async-start | bytes 245760 | tf_op jit(solution)/shard_map/slice | solution.py:16

commit v2 on v1

--- a/solution.py
+++ b/solution.py
@@ -78,7 +78,23 @@
 
 
 def gathered(values, axis):
-    return lax.all_gather(values, axis)
+    count = lax.axis_size(axis)
+    shifted = [values] + [
+        lax.ppermute(values, axis, [(source, (source + shift) % count) for source in range(count)])
+        for shift in range(1, count)
+    ]
+    return jnp.stack(shifted)
+
+
+def diagonal_corner(values):
+    count_y = lax.axis_size("gy")
+    count_z = lax.axis_size("gz")
+    pairs = [
+        ((row + 1) * count_z + column - 1, row * count_z + column)
+        for row in range(count_y - 1)
+        for column in range(1, count_z)
+    ]
+    return lax.ppermute(values, ("gy", "gz"), pairs)
 
 
 def block_spikes(lower_band, main_band, upper_band, right_side, direction):
@@ -100,7 +116,8 @@
     beta = jnp.zeros_like(alpha)
     carried = []
     for block in range(blocks):
-        a0, a1, a2, b0, b1, b2 = [coefficients[block, index] for index in range(6)]
+        held = lax.dynamic_index_in_dim(coefficients, (position - block) % blocks, 0, False)
+        a0, a1, a2, b0, b1, b2 = [held[index] for index in range(6)]
         scale = 1.0 / (1.0 - a1 * beta)
         p_term = (a0 + a1 * alpha) * scale
         q_term = a2 * scale
@@ -171,12 +188,14 @@
             [
                 take_rows(magnetic_y, 1, size_z - 1, 1),
                 take_rows(magnetic_x, 1, size_z - 1, 1),
-                take_rows(cross_z, 1, size_z - 1, 1),
+                take_rows(electric_z, 1, size_z - 1, 1),
             ]
         ),
         "gz",
         1,
     )
+    corner = diagonal_corner(take_rows(take_rows(electric_z, 0, 0, 1), 1, size_z - 1, 1))
+    cross_z_below = ahead_diff(below_z[2], 0, corner)
     above_ex = passed_along(take_rows(electric_x, 1, 0, 1), "gz", -1)
     cross_x = ahead_diff(electric_x, 1, above_ex)
     source_x = keeping * electric_x + coupling * (
@@ -186,7 +205,7 @@
     )
     source_y = keeping * electric_y + coupling * (
         behind_diff(magnetic_x, 1, below_z[1])
-        - behind_diff(cross_z, 1, below_z[2])
+        - behind_diff(cross_z, 1, cross_z_below)
         - behind_diff(magnetic_z, 2, edge_zeros(magnetic_z, 2))
     )
     source_z = keeping * electric_z + coupling * (

time: 67.8 us -> 57.8 us (0.85)
  blocking collectives: 29.1 us -> 0 us
  starting transfers between devices: 11.2 us -> 29.5 us
  waiting for transfers between devices: 2.19 us -> 4.65 us
  local copies, waits for them, and re-layouts: 13.7 us -> 12.2 us
  other arithmetic: 9.39 us -> 8.59 us
    all_gather x2 -> x0, blocking collectives: 29.1 us -> none  [gathered(): return lax.all_gather(values, axis)]
    ppermute x0 -> x11, starting transfers between devices: none -> 16.9 us  [the longest x10 16.2 us: gathered(): lax.ppermute(values, axis, [(source, (source + shift) % count) for source...]
    ppermute x0 -> x11, waiting for transfers between devices: none -> 2.1 us  [the longest x10 2.1 us: gathered(): lax.ppermute(values, axis, [(source, (source + shift) % count) for source...]
    another operation x3, local copies, waits for them, and re-layouts: 0.95 us -> 2.8 us  [body(): jnp.stack([take_rows(magnetic_y, 1, size_z - 1, 1), take_rows(magnetic_x,...]
    unnamed x22 -> x32, local copies, waits for them, and re-layouts: 6.21 us -> 4.68 us
    ppermute x4, starting transfers between devices: 11.2 us -> 12.6 us  [passed_along(): lax.ppermute(value, axis, [(source, source + steps) for source in range(f...]
    slice x74, local copies, waits for them, and re-layouts: 5.69 us -> 4.6 us  [take_rows(): return lax.slice_in_dim(values, start, start + length, axis=direction)]
    select_n x1, other arithmetic: 1.09 us -> 0.12 us  [block_spikes(): inner_upper = jnp.where(last_row, 0.0, upper_band)]
  transfers between devices with their start and end apart: 4 -> 15, of which waited for: 2 -> 4; matrix products, arithmetic and copies ran while one was open for 6% -> 17% of each run, Pallas kernels for 0% -> 0%
where the time goes in v2:
time: 57.8 us; the launch traced here: 57.2 us
  starting transfers between devices  29.5 us (51%)
  local copies, waits for them, and re-layouts  12.2 us (21%)
  other arithmetic  8.59 us (15%)
  waiting for transfers between devices  4.65 us (8%)
  between operations  2.31 us (4%)
    ppermute x10, starting transfers between devices, gathered(): lax.ppermute(values, axis, [(source, (source + shift) % count) for source...  16.2 us
    ppermute x4, starting transfers between devices, passed_along(): lax.ppermute(value, axis, [(source, source + steps) for source in range(f...  12.6 us
    unnamed x32, local copies, waits for them, and re-layouts  4.68 us
    slice x74, local copies, waits for them, and re-layouts, take_rows(): return lax.slice_in_dim(values, start, start + length, axis=direction)  4.6 us
    another operation x3, local copies, waits for them, and re-layouts, body(): jnp.stack([take_rows(magnetic_y, 1, size_z - 1, 1), take_rows(magnetic_x,...  2.8 us
    ppermute x4, waiting for transfers between devices, passed_along(): lax.ppermute(value, axis, [(source, source + steps) for source in range(f...  2.55 us
    ppermute x10, waiting for transfers between devices, gathered(): lax.ppermute(values, axis, [(source, (source + shift) % count) for source...  2.1 us
    add x12, other arithmetic, reduce_lines(): right_side + ratio_low[None] * low_right + ratio_high[None] * high_right  1.91 us
  transfers between devices with their start and end apart: 15, of which 4 were waited for; matrix products, arithmetic and copies ran while one was open for 17% of the time, Pallas kernels for 0%

profile of v2, /device:TPU:0, one launch (start us, length us, event | category | flops | bytes accessed | tf_op | source)
XLA Modules:
  0.0 57.2 jit_solution(2125777636326926616)
XLA Ops:
  0.6 1.0 %slice_bitcast_fusion.10 = f32[1,16,1,256]{3,2,1,0:T(1,128)S(1)} fusion(f32[16,8,256]{2,1,0:T(8,128)} %param.11), kind=kLoop, calls=%fused_computation.379 | loop fusion | bytes 32768 | tf_op jit(solution)/shard_map/stack | solution.py:187
  1.6 0.9 %slice_bitcast_fusion.11 = f32[1,16,1,256]{3,2,1,0:T(1,128)S(1)} fusion(f32[16,8,256]{2,1,0:T(8,128)} %param.12), kind=kLoop, calls=%fused_computation.380 | loop fusion | bytes 32768 | tf_op jit(solution)/shard_map/stack | solution.py:187
  2.5 0.9 %slice_bitcast_fusion.9 = f32[1,16,1,256]{3,2,1,0:T(1,128)S(1)} fusion(f32[16,8,256]{2,1,0:T(8,128)} %param.10), kind=kLoop, calls=%fused_computation.378 | loop fusion | bytes 32768 | tf_op jit(solution)/shard_map/stack | solution.py:187
  3.5 2.4 %collective-permute-start.1 = (f32[3,16,1,256]{3,2,1,0:T(1,128)S(1)}, f32[3,16,1,256]{3,2,1,0:T(1,128)S(1)}, u32[]{:S(2)}, u32[]{:S(2)}) collective-permute-start(f32[3,16,1,256]{3,2,1,0:T(1,128)S(1)} %pad_maximum_fusion.4), channel_id=1, source_target_pairs={{0,1},{1,2},{2,3},{3,4},{4,5},{5,6},{6,7},{8,9},{9,10},{10,11},{11... | collective-permute-start | bytes 147464 | tf_op jit(solution)/shard_map/ppermute | solution.py:12
  5.9 0.7 %collective-permute-start.6 = (f32[1,1,256]{2,1,0:T(1,128)S(1)}, f32[1,1,256]{2,1,0:T(1,128)S(1)}, u32[]{:S(2)}, u32[]{:S(2)}) collective-permute-start(f32[1,1,256]{2,1,0:T(1,128)S(1)} %slice.807), channel_id=1, source_target_pairs={{8,1},{9,2},{10,3},{11,4},{12,5},{13,6},{14,7},{16,9},{17,10},{18,... | collective-permute-start | bytes 3080 | tf_op jit(solution)/shard_map/ppermute | solution.py:97
  6.6 1.3 %collective-permute-start.5 = (f32[1,8,256]{2,1,0:T(8,128)S(1)}, f32[1,8,256]{2,1,0:T(8,128)S(1)}, u32[]{:S(2)}, u32[]{:S(2)}) collective-permute-start(f32[1,8,256]{2,1,0:T(8,128)S(1)} %slice.805), channel_id=1, source_target_pairs={{8,0},{16,8},{24,16},{9,1},{17,9},{25,17},{10,2},{18,10},{26,18},{... | collective-permute-start | bytes 24584 | tf_op jit(solution)/shard_map/ppermute | solution.py:12
  7.9 0.9 %slice.885 = f32[16,1,256]{2,1,0:T(1,128)S(1)} slice(f32[16,8,256]{2,1,0:T(8,128)} %param.8), slice={[0:16], [0:1], [0:256]} | slice | bytes 32768 | tf_op jit(solution)/shard_map/slice | solution.py:16
  8.8 1.3 %collective-permute-start.14 = (f32[16,1,256]{2,1,0:T(1,128)S(1)}, f32[16,1,256]{2,1,0:T(1,128)S(1)}, u32[]{:S(2)}, u32[]{:S(2)}) collective-permute-start(f32[16,1,256]{2,1,0:T(1,128)S(1)} %slice.885), channel_id=1, source_target_pairs={{1,0},{2,1},{3,2},{4,3},{5,4},{6,5},{7,6},{9,8},{10,9},{11,10},{12... | collective-permute-start | bytes 49160 | tf_op jit(solution)/shard_map/ppermute | solution.py:12
  10.3 0.8 %copy-done = f32[16,8,256]{2,1,0:T(8,128)S(1)} copy-done((f32[16,8,256]{2,1,0:T(8,128)S(1)}, f32[16,8,256]{2,1,0:T(8,128)}, u32[]{:S(2)}) %copy-start) | copy-done | bytes 131096
  11.2 0.9 %copy-done.1 = f32[16,8,256]{2,1,0:T(8,128)S(1)} copy-done((f32[16,8,256]{2,1,0:T(8,128)S(1)}, f32[16,8,256]{2,1,0:T(8,128)}, u32[]{:S(2)}) %copy-start.1) | copy-done | bytes 131096
  12.2 0.8 %copy-done.3 = f32[16,8,256]{2,1,0:T(8,128)S(1)} copy-done((f32[16,8,256]{2,1,0:T(8,128)S(1)}, f32[16,8,256]{2,1,0:T(8,128)}, u32[]{:S(2)}) %copy-start.3) | copy-done | bytes 131096
  13.5 0.7 %copy-done.8 = f32[16,8,256]{2,1,0:T(8,128)S(1)} copy-done((f32[16,8,256]{2,1,0:T(8,128)S(1)}, f32[16,8,256]{2,1,0:T(8,128)}, u32[]{:S(2)}) %copy-start.8) | copy-done | bytes 131096
  14.4 1.2 %collective-permute-done.5 = f32[1,8,256]{2,1,0:T(8,128)S(1)} collective-permute-done((f32[1,8,256]{2,1,0:T(8,128)S(1)}, f32[1,8,256]{2,1,0:T(8,128)S(1)}, u32[]{:S(2)}, u32[]{:S(2)}) %collective-permute-start.5) | collective-permute-done | bytes 8224 | tf_op jit(solution)/shard_map/ppermute | solution.py:12
  15.7 0.3 select_select_fusion.1
  16.7 7.7 %collective-permute-start = (f32[3,1,8,256]{3,2,1,0:T(8,128)S(1)}, f32[3,1,8,256]{3,2,1,0:T(8,128)S(1)}, u32[]{:S(2)}, u32[]{:S(2)}) collective-permute-start(f32[3,1,8,256]{3,2,1,0:T(8,128)S(1)} %pad_maximum_fusion.6), channel_id=1, source_target_pairs={{0,8},{8,16},{16,24},{1,9},{9,17},{17,25},{2,10},{10,18},{18,26},{... | collective-permute-start | bytes 73736 | tf_op jit(solution)/shard_map/ppermute | solution.py:12
  24.5 1.4 %collective-permute-done = f32[3,1,8,256]{3,2,1,0:T(8,128)S(1)} collective-permute-done((f32[3,1,8,256]{3,2,1,0:T(8,128)S(1)}, f32[3,1,8,256]{3,2,1,0:T(8,128)S(1)}, u32[]{:S(2)}, u32[]{:S(2)}) %collective-permute-start) | collective-permute-done | bytes 24608 | tf_op jit(solution)/shard_map/ppermute | solution.py:12
  25.9 0.2 fusion.21
  26.8 2.5 %collective-permute-start.2 = (f32[6,1,8,256]{3,2,0,1:T(8,128)S(1)}, f32[6,1,8,256]{3,2,0,1:T(8,128)S(1)}, u32[]{:S(2)}, u32[]{:S(2)}) collective-permute-start(f32[6,1,8,256]{3,2,0,1:T(8,128)S(1)} %get-tuple-element.245), channel_id=1, source_target_pairs={{0,8},{8,16},{16,24},{24,0},{1,9},{9,17},{17,25},{25,1},{2,10},{10... | collective-permute-start | bytes 147464 | tf_op jit(solution)/shard_map/ppermute | solution.py:83
  29.3 3.0 %collective-permute-start.3 = (f32[6,1,8,256]{3,2,0,1:T(8,128)S(1)}, f32[6,1,8,256]{3,2,0,1:T(8,128)S(1)}, u32[]{:S(2)}, u32[]{:S(2)}) collective-permute-start(f32[6,1,8,256]{3,2,0,1:T(8,128)S(1)} %get-tuple-element.245), channel_id=1, source_target_pairs={{0,16},{8,24},{16,0},{24,8},{1,17},{9,25},{17,1},{25,9},{2,18},{10... | collective-permute-start | bytes 147464 | tf_op jit(solution)/shard_map/ppermute | solution.py:83
  32.4 0.1 fusion.41
  32.8 0.1 pad_multiply_fusion.16
  34.2 2.1 %collective-permute-start.8 = (f32[6,16,1,256]{3,2,1,0:T(1,128)S(1)}, f32[6,16,1,256]{3,2,1,0:T(1,128)S(1)}, u32[]{:S(2)}, u32[]{:S(2)}) collective-permute-start(f32[6,16,1,256]{3,2,1,0:T(1,128)S(1)} %pad_maximum_fusion.3), channel_id=1, source_target_pairs={{0,2},{1,3},{2,4},{3,5},{4,6},{5,7},{6,0},{7,1},{8,10},{9,11},{10,... | collective-permute-start | bytes 294920 | tf_op jit(solution)/shard_map/ppermute | solution.py:83
  36.2 1.4 %collective-permute-start.4 = (f32[6,1,8,256]{3,2,1,0:T(8,128)S(1)}, f32[6,1,8,256]{3,2,1,0:T(8,128)S(1)}, u32[]{:S(2)}, u32[]{:S(2)}) collective-permute-start(f32[6,1,8,256]{3,2,1,0:T(8,128)S(1)} %get-tuple-element.246), channel_id=1, source_target_pairs={{0,24},{8,0},{16,8},{24,16},{1,25},{9,1},{17,9},{25,17},{2,26},{10... | collective-permute-start | bytes 147464 | tf_op jit(solution)/shard_map/ppermute | solution.py:83
  37.8 0.2 fusion.39
  38.2 0.1 multiply_add_fusion.10
  38.6 0.2 fusion.37
  39.0 0.1 multiply_add_fusion.9
  39.3 0.2 fusion.35
  39.8 0.1 multiply_add_fusion.8
  40.1 0.2 fusion.33
  40.5 0.1 multiply_add_fusion.7
  40.9 0.2 fusion.31
  41.7 0.2 fusion.29
  42.1 0.2 pad_multiply_fusion
  42.5 0.5 copy-done.7
  43.1 0.7 %add_subtract_fusion = f32[16,8,256]{2,1,0:T(8,128)} fusion(f32[16,8,256]{2,1,0:T(8,128)S(1)} %maximum_subtract_fusion.6, f32[16,8,256]{2,1,0:T(8,128)S(1)} %copy-done.2, f32[16,8,256]{2,1,0:T(8,128)S(1)} %fusion.26, f32[16,8,255]{2,1,0:T(8,128)S(1)} %slice.1092), kind=kLoop, calls=%fused_computation.86 | loop fusion | flops 98304 | bytes 654848 | tf_op jit(solution)/shard_map/sub | solution.py:227
  43.9 1.9 %collective-permute-start.9 = (f32[6,16,1,256]{3,2,1,0:T(1,128)S(1)}, f32[6,16,1,256]{3,2,1,0:T(1,128)S(1)}, u32[]{:S(2)}, u32[]{:S(2)}) collective-permute-start(f32[6,16,1,256]{3,2,1,0:T(1,128)S(1)} %pad_maximum_fusion.3), channel_id=1, source_target_pairs={{0,3},{1,4},{2,5},{3,6},{4,7},{5,0},{6,1},{7,2},{8,11},{9,12},{10,... | collective-permute-start | bytes 294920 | tf_op jit(solution)/shard_map/ppermute | solution.py:83
  45.8 0.7 %collective-permute-start.10 = (f32[6,16,1,256]{3,2,1,0:T(1,128)S(1)}, f32[6,16,1,256]{3,2,1,0:T(1,128)S(1)}, u32[]{:S(2)}, u32[]{:S(2)}) collective-permute-start(f32[6,16,1,256]{3,2,1,0:T(1,128)S(1)} %pad_maximum_fusion.3), channel_id=1, source_target_pairs={{0,4},{1,5},{2,6},{3,7},{4,0},{5,1},{6,2},{7,3},{8,12},{9,13},{10,... | collective-permute-start | bytes 294920 | tf_op jit(solution)/shard_map/ppermute | solution.py:83
  46.5 0.5 collective-permute-start.11
  47.4 0.7 %fusion.25 = f32[16,8,256]{2,1,0:T(8,128)} fusion(f32[16,8,256]{2,1,0:T(8,128)S(1)} %get-tuple-element.212, f32[16,8,256]{2,1,0:T(8,128)S(1)} %copy-done.1, f32[1,8,256]{2,1,0:T(8,128)S(1)} %bitcast.716, f32[15,8,256]{2,1,0:T(8,128)S(1)} %slice.1093, f32[8,256]{1,0:T(8,128)S(1)} %bitcast.715, f32[3,16,8,256]{3,2,1,0:T(8,128)S(1)} %add_divide_fusion.1, ...), kind=kLoop, calls=%fused_computation.51 | loop fusion | flops 262144 | bytes 933888 | tf_op jit(solution)/shard_map/sub | solution.py:229
  48.1 2.0 %collective-permute-start.12 = (f32[6,16,1,256]{3,2,1,0:T(1,128)S(1)}, f32[6,16,1,256]{3,2,1,0:T(1,128)S(1)}, u32[]{:S(2)}, u32[]{:S(2)}) collective-permute-start(f32[6,16,1,256]{3,2,1,0:T(1,128)S(1)} %pad_maximum_fusion.3), channel_id=1, source_target_pairs={{0,6},{1,7},{2,0},{3,1},{4,2},{5,3},{6,4},{7,5},{8,14},{9,15},{10,... | collective-permute-start | bytes 294920 | tf_op jit(solution)/shard_map/ppermute | solution.py:83
  50.2 2.1 %collective-permute-start.13 = (f32[6,16,1,256]{3,2,1,0:T(1,128)S(1)}, f32[6,16,1,256]{3,2,1,0:T(1,128)S(1)}, u32[]{:S(2)}, u32[]{:S(2)}) collective-permute-start(f32[6,16,1,256]{3,2,1,0:T(1,128)S(1)} %pad_maximum_fusion.3), channel_id=1, source_target_pairs={{0,7},{1,0},{2,1},{3,2},{4,3},{5,4},{6,5},{7,6},{8,15},{9,8},{10,9... | collective-permute-start | bytes 294920 | tf_op jit(solution)/shard_map/ppermute | solution.py:83
  52.3 1.2 %collective-permute-done.12 = f32[6,16,1,256]{3,2,1,0:T(1,128)S(1)} collective-permute-done((f32[6,16,1,256]{3,2,1,0:T(1,128)S(1)}, f32[6,16,1,256]{3,2,1,0:T(1,128)S(1)}, u32[]{:S(2)}, u32[]{:S(2)}) %collective-permute-start.12) | collective-permute-done | bytes 98336 | tf_op jit(solution)/shard_map/ppermute | solution.py:83
  53.5 0.9 %collective-permute-done.13 = f32[6,16,1,256]{3,2,1,0:T(1,128)S(1)} collective-permute-done((f32[6,16,1,256]{3,2,1,0:T(1,128)S(1)}, f32[6,16,1,256]{3,2,1,0:T(1,128)S(1)}, u32[]{:S(2)}, u32[]{:S(2)}) %collective-permute-start.13) | collective-permute-done | bytes 98336 | tf_op jit(solution)/shard_map/ppermute | solution.py:83
  54.5 0.6 fusion.110
  55.0 0.3 constant_dynamic-update-slice_fusion.7
  55.8 0.6 %copy-done.9 = f32[16,8,256]{2,1,0:T(8,128)} copy-done((f32[16,8,256]{2,1,0:T(8,128)}, f32[16,8,256]{2,1,0:T(8,128)S(1)}, u32[]{:S(2)}) %copy-start.9) | copy-done | bytes 131096
  56.5 0.7 %fusion.23 = f32[16,8,256]{2,1,0:T(8,128)} fusion(f32[16,8,256]{2,1,0:T(8,128)S(1)} %maximum_subtract_fusion.4, f32[16,8,256]{2,1,0:T(8,128)S(1)} %copy-done, f32[16,1,256]{2,1,0:T(1,128)S(1)} %fusion.264, f32[16,7,256]{2,1,0:T(8,128)S(1)} %slice.1091, f32[16,256]{1,0:T(8,128)S(1)} %bitcast.711, f32[3,16,8,256]{3,2,1,0:T(8,128)S(1)} %add_divide_fusion, ...), kind=kLoop, calls=%fused_computation.48 | loop fusion | flops 262144 | bytes 950272 | tf_op jit(solution)/shard_map/sub | solution.py:225
  (187 shorter events, 6.9 us)
Async XLA Ops:
  0.6 5.2 %copy-start.4 = (f32[16,8,256]{2,1,0:T(8,128)S(1)}, f32[16,8,256]{2,1,0:T(8,128)}, u32[]{:S(2)}) copy-start(f32[16,8,256]{2,1,0:T(8,128)} %param.10) | copy-start | bytes 393220
  3.5 12.2 %collective-permute-start.1 = (f32[3,16,1,256]{3,2,1,0:T(1,128)S(1)}, f32[3,16,1,256]{3,2,1,0:T(1,128)S(1)}, u32[]{:S(2)}, u32[]{:S(2)}) collective-permute-start(f32[3,16,1,256]{3,2,1,0:T(1,128)S(1)} %pad_maximum_fusion.4), channel_id=1, source_target_pairs={{0,1},{1,2},{2,3},{3,4},{4,5},{5,6},{6,7},{8,9},{9,10},{10,11},{11... | collective-permute-start | bytes 147464 | tf_op jit(solution)/shard_map/ppermute | solution.py:12
  5.9 9.8 %collective-permute-start.6 = (f32[1,1,256]{2,1,0:T(1,128)S(1)}, f32[1,1,256]{2,1,0:T(1,128)S(1)}, u32[]{:S(2)}, u32[]{:S(2)}) collective-permute-start(f32[1,1,256]{2,1,0:T(1,128)S(1)} %slice.807), channel_id=1, source_target_pairs={{8,1},{9,2},{10,3},{11,4},{12,5},{13,6},{14,7},{16,9},{17,10},{18,... | collective-permute-start | bytes 3080 | tf_op jit(solution)/shard_map/ppermute | solution.py:97
  6.6 9.0 %collective-permute-start.5 = (f32[1,8,256]{2,1,0:T(8,128)S(1)}, f32[1,8,256]{2,1,0:T(8,128)S(1)}, u32[]{:S(2)}, u32[]{:S(2)}) collective-permute-start(f32[1,8,256]{2,1,0:T(8,128)S(1)} %slice.805), channel_id=1, source_target_pairs={{8,0},{16,8},{24,16},{9,1},{17,9},{25,17},{10,2},{18,10},{26,18},{... | collective-permute-start | bytes 24584 | tf_op jit(solution)/shard_map/ppermute | solution.py:12
  8.8 6.8 %collective-permute-start.14 = (f32[16,1,256]{2,1,0:T(1,128)S(1)}, f32[16,1,256]{2,1,0:T(1,128)S(1)}, u32[]{:S(2)}, u32[]{:S(2)}) collective-permute-start(f32[16,1,256]{2,1,0:T(1,128)S(1)} %slice.885), channel_id=1, source_target_pairs={{1,0},{2,1},{3,2},{4,3},{5,4},{6,5},{7,6},{9,8},{10,9},{11,10},{12... | collective-permute-start | bytes 49160 | tf_op jit(solution)/shard_map/ppermute | solution.py:12
  10.2 0.9 %copy-start = (f32[16,8,256]{2,1,0:T(8,128)S(1)}, f32[16,8,256]{2,1,0:T(8,128)}, u32[]{:S(2)}) copy-start(f32[16,8,256]{2,1,0:T(8,128)} %param.11) | copy-start | bytes 393220
  10.2 0.9 %copy-start.6 = (f32[16,8,256]{2,1,0:T(8,128)S(1)}, f32[16,8,256]{2,1,0:T(8,128)}, u32[]{:S(2)}) copy-start(f32[16,8,256]{2,1,0:T(8,128)} %param.8) | copy-start | bytes 393220
  11.2 0.9 %copy-start.1 = (f32[16,8,256]{2,1,0:T(8,128)S(1)}, f32[16,8,256]{2,1,0:T(8,128)}, u32[]{:S(2)}) copy-start(f32[16,8,256]{2,1,0:T(8,128)} %param.13) | copy-start | bytes 393220
  12.1 0.9 %copy-start.3 = (f32[16,8,256]{2,1,0:T(8,128)S(1)}, f32[16,8,256]{2,1,0:T(8,128)}, u32[]{:S(2)}) copy-start(f32[16,8,256]{2,1,0:T(8,128)} %param.14) | copy-start | bytes 393220
  12.1 1.0 %copy-start.11 = (f32[16,8,256]{2,1,0:T(8,128)S(1)}, f32[16,8,256]{2,1,0:T(8,128)}, u32[]{:S(2)}) copy-start(f32[16,8,256]{2,1,0:T(8,128)} %param.15) | copy-start | bytes 393220
  13.3 0.9 %copy-start.8 = (f32[16,8,256]{2,1,0:T(8,128)S(1)}, f32[16,8,256]{2,1,0:T(8,128)}, u32[]{:S(2)}) copy-start(f32[16,8,256]{2,1,0:T(8,128)} %param.9) | copy-start | bytes 393220
  14.3 1.3 %copy-start.5 = (f32[16,8,256]{2,1,0:T(8,128)S(1)}, f32[16,8,256]{2,1,0:T(8,128)}, u32[]{:S(2)}) copy-start(f32[16,8,256]{2,1,0:T(8,128)} %param.10) | copy-start | bytes 393220
  14.3 1.3 %slice-start = ((f32[16,8,256]{2,1,0:T(8,128)}), f32[15,8,256]{2,1,0:T(8,128)S(1)}, s32[]{:S(2)}) async-start(f32[16,8,256]{2,1,0:T(8,128)} %param.10), calls=%async_computation | async-start | bytes 245760 | tf_op jit(solution)/shard_map/slice | solution.py:16
  16.7 9.2 %collective-permute-start = (f32[3,1,8,256]{3,2,1,0:T(8,128)S(1)}, f32[3,1,8,256]{3,2,1,0:T(8,128)S(1)}, u32[]{:S(2)}, u32[]{:S(2)}) collective-permute-start(f32[3,1,8,256]{3,2,1,0:T(8,128)S(1)} %pad_maximum_fusion.6), channel_id=1, source_target_pairs={{0,8},{8,16},{16,24},{1,9},{9,17},{17,25},{2,10},{10,18},{18,26},{... | collective-permute-start | bytes 73736 | tf_op jit(solution)/shard_map/ppermute | solution.py:12
  24.5 1.4 %copy-start.2 = (f32[16,8,256]{2,1,0:T(8,128)S(1)}, f32[16,8,256]{2,1,0:T(8,128)}, u32[]{:S(2)}) copy-start(f32[16,8,256]{2,1,0:T(8,128)} %param.12) | copy-start | bytes 393220
  26.8 17.0 %collective-permute-start.2 = (f32[6,1,8,256]{3,2,0,1:T(8,128)S(1)}, f32[6,1,8,256]{3,2,0,1:T(8,128)S(1)}, u32[]{:S(2)}, u32[]{:S(2)}) collective-permute-start(f32[6,1,8,256]{3,2,0,1:T(8,128)S(1)} %get-tuple-element.245), channel_id=1, source_target_pairs={{0,8},{8,16},{16,24},{24,0},{1,9},{9,17},{17,25},{25,1},{2,10},{10... | collective-permute-start | bytes 147464 | tf_op jit(solution)/shard_map/ppermute | solution.py:83
  29.3 16.5 %collective-permute-start.3 = (f32[6,1,8,256]{3,2,0,1:T(8,128)S(1)}, f32[6,1,8,256]{3,2,0,1:T(8,128)S(1)}, u32[]{:S(2)}, u32[]{:S(2)}) collective-permute-start(f32[6,1,8,256]{3,2,0,1:T(8,128)S(1)} %get-tuple-element.245), channel_id=1, source_target_pairs={{0,16},{8,24},{16,0},{24,8},{1,17},{9,25},{17,1},{25,9},{2,18},{10... | collective-permute-start | bytes 147464 | tf_op jit(solution)/shard_map/ppermute | solution.py:83
  34.1 14.0 %collective-permute-start.7 = (f32[6,16,1,256]{3,2,1,0:T(1,128)S(1)}, f32[6,16,1,256]{3,2,1,0:T(1,128)S(1)}, u32[]{:S(2)}, u32[]{:S(2)}) collective-permute-start(f32[6,16,1,256]{3,2,1,0:T(1,128)S(1)} %pad_maximum_fusion.3), channel_id=1, source_target_pairs={{0,1},{1,2},{2,3},{3,4},{4,5},{5,6},{6,7},{7,0},{8,9},{9,10},{10,1... | collective-permute-start | bytes 294920 | tf_op jit(solution)/shard_map/ppermute | solution.py:83
  34.2 16.0 %collective-permute-start.8 = (f32[6,16,1,256]{3,2,1,0:T(1,128)S(1)}, f32[6,16,1,256]{3,2,1,0:T(1,128)S(1)}, u32[]{:S(2)}, u32[]{:S(2)}) collective-permute-start(f32[6,16,1,256]{3,2,1,0:T(1,128)S(1)} %pad_maximum_fusion.3), channel_id=1, source_target_pairs={{0,2},{1,3},{2,4},{3,5},{4,6},{5,7},{6,0},{7,1},{8,10},{9,11},{10,... | collective-permute-start | bytes 294920 | tf_op jit(solution)/shard_map/ppermute | solution.py:83
  36.2 10.3 %collective-permute-start.4 = (f32[6,1,8,256]{3,2,1,0:T(8,128)S(1)}, f32[6,1,8,256]{3,2,1,0:T(8,128)S(1)}, u32[]{:S(2)}, u32[]{:S(2)}) collective-permute-start(f32[6,1,8,256]{3,2,1,0:T(8,128)S(1)} %get-tuple-element.246), channel_id=1, source_target_pairs={{0,24},{8,0},{16,8},{24,16},{1,25},{9,1},{17,9},{25,17},{2,26},{10... | collective-permute-start | bytes 147464 | tf_op jit(solution)/shard_map/ppermute | solution.py:83
  42.4 0.7 %copy-start.7 = (f32[16,8,256]{2,1,0:T(8,128)}, f32[16,8,256]{2,1,0:T(8,128)S(1)}, u32[]{:S(2)}) copy-start(f32[16,8,256]{2,1,0:T(8,128)S(1)} %fusion.26) | copy-start | bytes 393220
  43.9 8.4 %collective-permute-start.9 = (f32[6,16,1,256]{3,2,1,0:T(1,128)S(1)}, f32[6,16,1,256]{3,2,1,0:T(1,128)S(1)}, u32[]{:S(2)}, u32[]{:S(2)}) collective-permute-start(f32[6,16,1,256]{3,2,1,0:T(1,128)S(1)} %pad_maximum_fusion.3), channel_id=1, source_target_pairs={{0,3},{1,4},{2,5},{3,6},{4,7},{5,0},{6,1},{7,2},{8,11},{9,12},{10,... | collective-permute-start | bytes 294920 | tf_op jit(solution)/shard_map/ppermute | solution.py:83
  45.8 6.5 %collective-permute-start.10 = (f32[6,16,1,256]{3,2,1,0:T(1,128)S(1)}, f32[6,16,1,256]{3,2,1,0:T(1,128)S(1)}, u32[]{:S(2)}, u32[]{:S(2)}) collective-permute-start(f32[6,16,1,256]{3,2,1,0:T(1,128)S(1)} %pad_maximum_fusion.3), channel_id=1, source_target_pairs={{0,4},{1,5},{2,6},{3,7},{4,0},{5,1},{6,2},{7,3},{8,12},{9,13},{10,... | collective-permute-start | bytes 294920 | tf_op jit(solution)/shard_map/ppermute | solution.py:83
  46.5 5.8 %collective-permute-start.11 = (f32[6,16,1,256]{3,2,1,0:T(1,128)S(1)}, f32[6,16,1,256]{3,2,1,0:T(1,128)S(1)}, u32[]{:S(2)}, u32[]{:S(2)}) collective-permute-start(f32[6,16,1,256]{3,2,1,0:T(1,128)S(1)} %pad_maximum_fusion.3), channel_id=1, source_target_pairs={{0,5},{1,6},{2,7},{3,0},{4,1},{5,2},{6,3},{7,4},{8,13},{9,14},{10,... | collective-permute-start | bytes 294920 | tf_op jit(solution)/shard_map/ppermute | solution.py:83
  47.4 0.7 %copy-start.10 = (f32[16,8,256]{2,1,0:T(8,128)}, f32[16,8,256]{2,1,0:T(8,128)S(1)}, u32[]{:S(2)}) copy-start(f32[16,8,256]{2,1,0:T(8,128)S(1)} %fusion.5) | copy-start | bytes 393220
  48.1 5.4 %collective-permute-start.12 = (f32[6,16,1,256]{3,2,1,0:T(1,128)S(1)}, f32[6,16,1,256]{3,2,1,0:T(1,128)S(1)}, u32[]{:S(2)}, u32[]{:S(2)}) collective-permute-start(f32[6,16,1,256]{3,2,1,0:T(1,128)S(1)} %pad_maximum_fusion.3), channel_id=1, source_target_pairs={{0,6},{1,7},{2,0},{3,1},{4,2},{5,3},{6,4},{7,5},{8,14},{9,15},{10,... | collective-permute-start | bytes 294920 | tf_op jit(solution)/shard_map/ppermute | solution.py:83
  50.2 4.3 %collective-permute-start.13 = (f32[6,16,1,256]{3,2,1,0:T(1,128)S(1)}, f32[6,16,1,256]{3,2,1,0:T(1,128)S(1)}, u32[]{:S(2)}, u32[]{:S(2)}) collective-permute-start(f32[6,16,1,256]{3,2,1,0:T(1,128)S(1)} %pad_maximum_fusion.3), channel_id=1, source_target_pairs={{0,7},{1,0},{2,1},{3,2},{4,3},{5,4},{6,5},{7,6},{8,15},{9,8},{10,9... | collective-permute-start | bytes 294920 | tf_op jit(solution)/shard_map/ppermute | solution.py:83
  55.8 0.7 %copy-start.9 = (f32[16,8,256]{2,1,0:T(8,128)}, f32[16,8,256]{2,1,0:T(8,128)S(1)}, u32[]{:S(2)}) copy-start(f32[16,8,256]{2,1,0:T(8,128)S(1)} %fusion.1) | copy-start | bytes 393220

commit v3 on v2

--- a/solution.py
+++ b/solution.py
@@ -86,17 +86,6 @@
     return jnp.stack(shifted)
 
 
-def diagonal_corner(values):
-    count_y = lax.axis_size("gy")
-    count_z = lax.axis_size("gz")
-    pairs = [
-        ((row + 1) * count_z + column - 1, row * count_z + column)
-        for row in range(count_y - 1)
-        for column in range(1, count_z)
-    ]
-    return lax.ppermute(values, ("gy", "gz"), pairs)
-
-
 def block_spikes(lower_band, main_band, upper_band, right_side, direction):
     length = main_band.shape[direction]
     row_index = lax.broadcasted_iota(jnp.int32, main_band.shape, direction)
@@ -114,10 +103,13 @@
     blocks = coefficients.shape[0]
     alpha = jnp.zeros_like(coefficients[0, 0])
     beta = jnp.zeros_like(alpha)
+    handed = jnp.zeros_like(alpha)
     carried = []
     for block in range(blocks):
         held = lax.dynamic_index_in_dim(coefficients, (position - block) % blocks, 0, False)
-        a0, a1, a2, b0, b1, b2 = [held[index] for index in range(6)]
+        a0, a1, a2, b0, b1, b2, passed = [held[index] for index in range(7)]
+        alpha = alpha + handed
+        handed = passed
         scale = 1.0 / (1.0 - a1 * beta)
         p_term = (a0 + a1 * alpha) * scale
         q_term = a2 * scale
@@ -141,11 +133,15 @@
     )
 
 
-def partitioned(lower_band, main_band, upper_band, right_side, direction, axis):
+def partitioned(lower_band, main_band, upper_band, right_side, direction, axis, handed_on):
     length = main_band.shape[direction]
     solved = block_spikes(lower_band, main_band, upper_band, right_side, direction)
     edges = jnp.concatenate(
-        [take_rows(solved, direction + 1, 0, 1), take_rows(solved, direction + 1, length - 1, 1)]
+        [
+            take_rows(solved, direction + 1, 0, 1),
+            take_rows(solved, direction + 1, length - 1, 1),
+            handed_on,
+        ]
     )
     everyone = gathered(edges, axis)
     earlier, following = interface_sweep(everyone, lax.axis_index(axis))
@@ -194,8 +190,12 @@
         "gz",
         1,
     )
-    corner = diagonal_corner(take_rows(take_rows(electric_z, 0, 0, 1), 1, size_z - 1, 1))
-    cross_z_below = ahead_diff(below_z[2], 0, corner)
+    cross_z_below = ahead_diff(below_z[2], 0, edge_zeros(below_z[2], 0))
+    corner = jnp.where(
+        lax.broadcasted_iota(jnp.int32, (size_y, 1, size_x), 0) == size_y - 1,
+        take_rows(above_ez[:, size_z - 1 :], 0, 0, 1),
+        0.0,
+    )
     above_ex = passed_along(take_rows(electric_x, 1, 0, 1), "gz", -1)
     cross_x = ahead_diff(electric_x, 1, above_ex)
     source_x = keeping * electric_x + coupling * (
@@ -218,10 +218,14 @@
     half_electric_z = reduce_lines(lower_x, main_x, upper_x, source_z[None], 2)[0]
     index_z = lax.broadcasted_iota(jnp.int32, coupling.shape, 1) + lax.axis_index("gz") * size_z
     lower_z, main_z, upper_z = bands(coupling, damping, index_z, size_z * lax.axis_size("gz"))
-    half_electric_y, fresh_ey = partitioned(lower_z, main_z, upper_z, source_y, 1, "gz")
+    half_electric_y, fresh_ey = partitioned(
+        lower_z, main_z, upper_z, source_y, 1, "gz", corner[None]
+    )
     index_y = lax.broadcasted_iota(jnp.int32, coupling.shape, 0) + lax.axis_index("gy") * size_y
     lower_y, main_y, upper_y = bands(coupling, damping, index_y, size_y * lax.axis_size("gy"))
-    half_electric_x, fresh_ex = partitioned(lower_y, main_y, upper_y, source_x, 0, "gy")
+    half_electric_x, fresh_ex = partitioned(
+        lower_y, main_y, upper_y, source_x, 0, "gy", jnp.zeros_like(source_x[None, :1])
+    )
     half_magnetic_x = magnetic_x + ahead_diff(half_electric_y, 1, fresh_ey) - cross_z
     half_magnetic_y = (
         magnetic_y + ahead_diff(half_electric_z, 2, edge_zeros(half_electric_z, 2)) - cross_x

time: 57.8 us -> 57.4 us (level)
  the two profiles are of different devices: /device:TPU:0 before, /device:TPU:3 now
where the time goes in v3:
time: 57.4 us; the launch traced here: 57.1 us
  starting transfers between devices  24.6 us (43%)
  local copies, waits for them, and re-layouts  13 us (23%)
  other arithmetic  8.78 us (15%)
  waiting for transfers between devices  8.29 us (14%)
  between operations  2.32 us (4%)
    ppermute x10, starting transfers between devices, gathered(): lax.ppermute(values, axis, [(source, (source + shift) % count) for source...  13.8 us
    ppermute x4, starting transfers between devices, passed_along(): lax.ppermute(value, axis, [(source, source + steps) for source in range(f...  10.9 us
    ppermute x10, waiting for transfers between devices, gathered(): lax.ppermute(values, axis, [(source, (source + shift) % count) for source...  7.46 us
    unnamed x32, local copies, waits for them, and re-layouts  5.46 us
    slice x74, local copies, waits for them, and re-layouts, take_rows(): return lax.slice_in_dim(values, start, start + length, axis=direction)  4.67 us
    another operation x3, local copies, waits for them, and re-layouts, body(): jnp.stack([take_rows(magnetic_y, 1, size_z - 1, 1), take_rows(magnetic_x,...  2.8 us
    add x12, other arithmetic, reduce_lines(): right_side + ratio_low[None] * low_right + ratio_high[None] * high_right  1.91 us
  transfers between devices with their start and end apart: 14, of which 3 were waited for; matrix products, arithmetic and copies ran while one was open for 17% of the time, Pallas kernels for 0%

profile of v3, /device:TPU:3, one launch (start us, length us, event | category | flops | bytes accessed | tf_op | source)
XLA Modules:
  0.0 57.1 jit_solution(15914007000892496298)
XLA Ops:
  0.6 1.0 %slice_bitcast_fusion.10 = f32[1,16,1,256]{3,2,1,0:T(1,128)S(1)} fusion(f32[16,8,256]{2,1,0:T(8,128)} %param.11), kind=kLoop, calls=%fused_computation.404 | loop fusion | bytes 32768 | tf_op jit(solution)/shard_map/stack | solution.py:183
  1.6 0.9 %slice_bitcast_fusion.11 = f32[1,16,1,256]{3,2,1,0:T(1,128)S(1)} fusion(f32[16,8,256]{2,1,0:T(8,128)} %param.12), kind=kLoop, calls=%fused_computation.405 | loop fusion | bytes 32768 | tf_op jit(solution)/shard_map/stack | solution.py:183
  2.5 0.9 %slice_bitcast_fusion.9 = f32[1,16,1,256]{3,2,1,0:T(1,128)S(1)} fusion(f32[16,8,256]{2,1,0:T(8,128)} %param.10), kind=kLoop, calls=%fused_computation.403 | loop fusion | bytes 32768 | tf_op jit(solution)/shard_map/stack | solution.py:183
  3.5 3.7 %collective-permute-start.1 = (f32[3,16,1,256]{3,2,1,0:T(1,128)S(1)}, f32[3,16,1,256]{3,2,1,0:T(1,128)S(1)}, u32[]{:S(2)}, u32[]{:S(2)}) collective-permute-start(f32[3,16,1,256]{3,2,1,0:T(1,128)S(1)} %pad_maximum_fusion.5), channel_id=1, source_target_pairs={{0,1},{1,2},{2,3},{3,4},{4,5},{5,6},{6,7},{8,9},{9,10},{10,11},{11... | collective-permute-start | bytes 147464 | tf_op jit(solution)/shard_map/ppermute | solution.py:12
  7.2 1.3 %collective-permute-start.5 = (f32[1,8,256]{2,1,0:T(8,128)S(1)}, f32[1,8,256]{2,1,0:T(8,128)S(1)}, u32[]{:S(2)}, u32[]{:S(2)}) collective-permute-start(f32[1,8,256]{2,1,0:T(8,128)S(1)} %slice.848), channel_id=1, source_target_pairs={{8,0},{16,8},{24,16},{9,1},{17,9},{25,17},{10,2},{18,10},{26,18},{... | collective-permute-start | bytes 24584 | tf_op jit(solution)/shard_map/ppermute | solution.py:12
  8.5 0.9 %slice.936 = f32[16,1,256]{2,1,0:T(1,128)S(1)} slice(f32[16,8,256]{2,1,0:T(8,128)} %param.8), slice={[0:16], [0:1], [0:256]} | slice | bytes 32768 | tf_op jit(solution)/shard_map/slice | solution.py:16
  9.4 1.9 %collective-permute-start.13 = (f32[16,1,256]{2,1,0:T(1,128)S(1)}, f32[16,1,256]{2,1,0:T(1,128)S(1)}, u32[]{:S(2)}, u32[]{:S(2)}) collective-permute-start(f32[16,1,256]{2,1,0:T(1,128)S(1)} %slice.936), channel_id=1, source_target_pairs={{1,0},{2,1},{3,2},{4,3},{5,4},{6,5},{7,6},{9,8},{10,9},{11,10},{12... | collective-permute-start | bytes 49160 | tf_op jit(solution)/shard_map/ppermute | solution.py:12
  11.5 0.8 %copy-done = f32[16,8,256]{2,1,0:T(8,128)S(1)} copy-done((f32[16,8,256]{2,1,0:T(8,128)S(1)}, f32[16,8,256]{2,1,0:T(8,128)}, u32[]{:S(2)}) %copy-start) | copy-done | bytes 131096
  12.5 0.9 %copy-done.1 = f32[16,8,256]{2,1,0:T(8,128)S(1)} copy-done((f32[16,8,256]{2,1,0:T(8,128)S(1)}, f32[16,8,256]{2,1,0:T(8,128)}, u32[]{:S(2)}) %copy-start.1) | copy-done | bytes 131096
  13.5 0.8 %copy-done.3 = f32[16,8,256]{2,1,0:T(8,128)S(1)} copy-done((f32[16,8,256]{2,1,0:T(8,128)S(1)}, f32[16,8,256]{2,1,0:T(8,128)}, u32[]{:S(2)}) %copy-start.3) | copy-done | bytes 131096
  14.3 0.1 select_select_fusion
  14.8 0.7 %copy-done.8 = f32[16,8,256]{2,1,0:T(8,128)S(1)} copy-done((f32[16,8,256]{2,1,0:T(8,128)S(1)}, f32[16,8,256]{2,1,0:T(8,128)}, u32[]{:S(2)}) %copy-start.8) | copy-done | bytes 131096
  15.7 0.7 %copy-done.5 = f32[16,8,256]{2,1,0:T(8,128)S(1)} copy-done((f32[16,8,256]{2,1,0:T(8,128)S(1)}, f32[16,8,256]{2,1,0:T(8,128)}, u32[]{:S(2)}) %copy-start.5) | copy-done | bytes 131096
  16.7 0.3 select_select_fusion.1
  17.7 4.0 %collective-permute-start = (f32[3,1,8,256]{3,2,1,0:T(8,128)S(1)}, f32[3,1,8,256]{3,2,1,0:T(8,128)S(1)}, u32[]{:S(2)}, u32[]{:S(2)}) collective-permute-start(f32[3,1,8,256]{3,2,1,0:T(8,128)S(1)} %pad_maximum_fusion.6), channel_id=1, source_target_pairs={{0,8},{8,16},{16,24},{1,9},{9,17},{17,25},{2,10},{10,18},{18,26},{... | collective-permute-start | bytes 73736 | tf_op jit(solution)/shard_map/ppermute | solution.py:12
  21.8 0.8 %collective-permute-done = f32[3,1,8,256]{3,2,1,0:T(8,128)S(1)} collective-permute-done((f32[3,1,8,256]{3,2,1,0:T(8,128)S(1)}, f32[3,1,8,256]{3,2,1,0:T(8,128)S(1)}, u32[]{:S(2)}, u32[]{:S(2)}) %collective-permute-start) | collective-permute-done | bytes 24608 | tf_op jit(solution)/shard_map/ppermute | solution.py:12
  22.7 0.2 fusion.21
  23.6 1.7 %collective-permute-start.2 = (f32[7,1,8,256]{3,2,0,1:T(8,128)S(1)}, f32[7,1,8,256]{3,2,0,1:T(8,128)S(1)}, u32[]{:S(2)}, u32[]{:S(2)}) collective-permute-start(f32[7,1,8,256]{3,2,0,1:T(8,128)S(1)} %get-tuple-element.243), channel_id=1, source_target_pairs={{0,8},{8,16},{16,24},{24,0},{1,9},{9,17},{17,25},{25,1},{2,10},{10... | collective-permute-start | bytes 172040 | tf_op jit(solution)/shard_map/ppermute | solution.py:83
  25.4 2.3 %collective-permute-start.3 = (f32[7,1,8,256]{3,2,0,1:T(8,128)S(1)}, f32[7,1,8,256]{3,2,0,1:T(8,128)S(1)}, u32[]{:S(2)}, u32[]{:S(2)}) collective-permute-start(f32[7,1,8,256]{3,2,0,1:T(8,128)S(1)} %get-tuple-element.243), channel_id=1, source_target_pairs={{0,16},{8,24},{16,0},{24,8},{1,17},{9,25},{17,1},{25,9},{2,18},{10... | collective-permute-start | bytes 172040 | tf_op jit(solution)/shard_map/ppermute | solution.py:83
  27.8 0.1 fusion.41
  28.1 0.1 pad_multiply_fusion.16
  29.5 4.4 %collective-permute-start.6 = (f32[7,16,1,256]{3,2,1,0:T(1,128)S(1)}, f32[7,16,1,256]{3,2,1,0:T(1,128)S(1)}, u32[]{:S(2)}, u32[]{:S(2)}) collective-permute-start(f32[7,16,1,256]{3,2,1,0:T(1,128)S(1)} %pad_maximum_fusion.3), channel_id=1, source_target_pairs={{0,1},{1,2},{2,3},{3,4},{4,5},{5,6},{6,7},{7,0},{8,9},{9,10},{10,1... | collective-permute-start | bytes 344072 | tf_op jit(solution)/shard_map/ppermute | solution.py:83
  33.9 0.3 collective-permute-start.7
  34.2 1.1 %collective-permute-start.4 = (f32[7,1,8,256]{3,2,1,0:T(8,128)S(1)}, f32[7,1,8,256]{3,2,1,0:T(8,128)S(1)}, u32[]{:S(2)}, u32[]{:S(2)}) collective-permute-start(f32[7,1,8,256]{3,2,1,0:T(8,128)S(1)} %get-tuple-element.244), channel_id=1, source_target_pairs={{0,24},{8,0},{16,8},{24,16},{1,25},{9,1},{17,9},{25,17},{2,26},{10... | collective-permute-start | bytes 172040 | tf_op jit(solution)/shard_map/ppermute | solution.py:83
  35.5 0.2 fusion.39
  35.9 0.1 multiply_add_fusion.10
  36.2 0.2 fusion.37
  36.6 0.1 multiply_add_fusion.9
  37.0 0.2 fusion.35
  37.4 0.1 multiply_add_fusion.8
  37.8 0.2 fusion.33
  38.2 0.1 multiply_add_fusion.7
  38.5 0.2 fusion.31
  39.0 0.1 multiply_add_fusion.6
  39.3 0.2 fusion.29
  39.7 0.2 pad_multiply_fusion
  40.2 0.5 copy-done.7
  40.7 0.7 %add_subtract_fusion = f32[16,8,256]{2,1,0:T(8,128)} fusion(f32[16,8,256]{2,1,0:T(8,128)S(1)} %maximum_subtract_fusion.6, f32[16,8,256]{2,1,0:T(8,128)S(1)} %copy-done.2, f32[16,8,256]{2,1,0:T(8,128)S(1)} %fusion.26, f32[16,8,255]{2,1,0:T(8,128)S(1)} %slice.1144), kind=kLoop, calls=%fused_computation.86 | loop fusion | flops 98304 | bytes 654848 | tf_op jit(solution)/shard_map/sub | solution.py:231
  41.6 1.8 %collective-permute-start.9 = (f32[7,16,1,256]{3,2,1,0:T(1,128)S(1)}, f32[7,16,1,256]{3,2,1,0:T(1,128)S(1)}, u32[]{:S(2)}, u32[]{:S(2)}) collective-permute-start(f32[7,16,1,256]{3,2,1,0:T(1,128)S(1)} %pad_maximum_fusion.3), channel_id=1, source_target_pairs={{0,4},{1,5},{2,6},{3,7},{4,0},{5,1},{6,2},{7,3},{8,12},{9,13},{10,... | collective-permute-start | bytes 344072 | tf_op jit(solution)/shard_map/ppermute | solution.py:83
  43.4 0.5 collective-permute-start.10
  44.2 0.7 %fusion.25 = f32[16,8,256]{2,1,0:T(8,128)} fusion(f32[16,8,256]{2,1,0:T(8,128)S(1)} %get-tuple-element.212, f32[16,8,256]{2,1,0:T(8,128)S(1)} %copy-done.1, f32[1,8,256]{2,1,0:T(8,128)S(1)} %bitcast.786, f32[15,8,256]{2,1,0:T(8,128)S(1)} %slice.1145, f32[8,256]{1,0:T(8,128)S(1)} %bitcast.785, f32[3,16,8,256]{3,2,1,0:T(8,128)S(1)} %add_divide_fusion.1, ...), kind=kLoop, calls=%fused_computation.51 | loop fusion | flops 262144 | bytes 933888 | tf_op jit(solution)/shard_map/sub | solution.py:233
  44.9 1.6 %collective-permute-start.11 = (f32[7,16,1,256]{3,2,1,0:T(1,128)S(1)}, f32[7,16,1,256]{3,2,1,0:T(1,128)S(1)}, u32[]{:S(2)}, u32[]{:S(2)}) collective-permute-start(f32[7,16,1,256]{3,2,1,0:T(1,128)S(1)} %pad_maximum_fusion.3), channel_id=1, source_target_pairs={{0,6},{1,7},{2,0},{3,1},{4,2},{5,3},{6,4},{7,5},{8,14},{9,15},{10,... | collective-permute-start | bytes 344072 | tf_op jit(solution)/shard_map/ppermute | solution.py:83
  46.7 6.4 %collective-permute-done.9 = f32[7,16,1,256]{3,2,1,0:T(1,128)S(1)} collective-permute-done((f32[7,16,1,256]{3,2,1,0:T(1,128)S(1)}, f32[7,16,1,256]{3,2,1,0:T(1,128)S(1)}, u32[]{:S(2)}, u32[]{:S(2)}) %collective-permute-start.9) | collective-permute-done | bytes 114720 | tf_op jit(solution)/shard_map/ppermute | solution.py:83
  53.2 1.0 %collective-permute-done.10 = f32[7,16,1,256]{3,2,1,0:T(1,128)S(1)} collective-permute-done((f32[7,16,1,256]{3,2,1,0:T(1,128)S(1)}, f32[7,16,1,256]{3,2,1,0:T(1,128)S(1)}, u32[]{:S(2)}, u32[]{:S(2)}) %collective-permute-start.10) | collective-permute-done | bytes 114720 | tf_op jit(solution)/shard_map/ppermute | solution.py:83
  54.3 0.6 %fusion.121 = (f32[1,16,1,256]{3,2,1,0:T(1,128)S(1)}, f32[1,16,1,256]{3,2,1,0:T(1,128)S(1)}, f32[1,16,1,256]{3,2,1,0:T(1,128)S(1)}, f32[1,16,1,256]{3,2,1,0:T(1,...) fusion(f32[8,7,16,1,256]{4,3,2,1,0:T(1,128)S(1)} %bitcast_dynam, ...), kind=kLoop, calls=%fused_computation.360 | loop fusion | flops 385024 | bytes 1130548 | tf_op jit(solution)/shard_map/mul | solution.py:114
  54.9 0.3 constant_dynamic-update-slice_fusion.7
  55.7 0.6 %copy-done.9 = f32[16,8,256]{2,1,0:T(8,128)} copy-done((f32[16,8,256]{2,1,0:T(8,128)}, f32[16,8,256]{2,1,0:T(8,128)S(1)}, u32[]{:S(2)}) %copy-start.9) | copy-done | bytes 131096
  56.3 0.7 %fusion.23 = f32[16,8,256]{2,1,0:T(8,128)} fusion(f32[16,8,256]{2,1,0:T(8,128)S(1)} %maximum_subtract_fusion.4, f32[16,8,256]{2,1,0:T(8,128)S(1)} %copy-done, f32[16,1,256]{2,1,0:T(1,128)S(1)} %fusion.284, f32[16,7,256]{2,1,0:T(8,128)S(1)} %slice.1143, f32[16,256]{1,0:T(8,128)S(1)} %bitcast.781, f32[3,16,8,256]{3,2,1,0:T(8,128)S(1)} %add_divide_fusion, ...), kind=kLoop, calls=%fused_computation.48 | loop fusion | flops 262144 | bytes 950272 | tf_op jit(solution)/shard_map/sub | solution.py:229
  (186 shorter events, 7.0 us)
Async XLA Ops:
  0.6 6.6 %copy-start.4 = (f32[16,8,256]{2,1,0:T(8,128)S(1)}, f32[16,8,256]{2,1,0:T(8,128)}, u32[]{:S(2)}) copy-start(f32[16,8,256]{2,1,0:T(8,128)} %param.10) | copy-start | bytes 393220
  3.5 13.2 %collective-permute-start.1 = (f32[3,16,1,256]{3,2,1,0:T(1,128)S(1)}, f32[3,16,1,256]{3,2,1,0:T(1,128)S(1)}, u32[]{:S(2)}, u32[]{:S(2)}) collective-permute-start(f32[3,16,1,256]{3,2,1,0:T(1,128)S(1)} %pad_maximum_fusion.5), channel_id=1, source_target_pairs={{0,1},{1,2},{2,3},{3,4},{4,5},{5,6},{6,7},{8,9},{9,10},{10,11},{11... | collective-permute-start | bytes 147464 | tf_op jit(solution)/shard_map/ppermute | solution.py:12
  7.2 8.5 %collective-permute-start.5 = (f32[1,8,256]{2,1,0:T(8,128)S(1)}, f32[1,8,256]{2,1,0:T(8,128)S(1)}, u32[]{:S(2)}, u32[]{:S(2)}) collective-permute-start(f32[1,8,256]{2,1,0:T(8,128)S(1)} %slice.848), channel_id=1, source_target_pairs={{8,0},{16,8},{24,16},{9,1},{17,9},{25,17},{10,2},{18,10},{26,18},{... | collective-permute-start | bytes 24584 | tf_op jit(solution)/shard_map/ppermute | solution.py:12
  9.4 7.2 %collective-permute-start.13 = (f32[16,1,256]{2,1,0:T(1,128)S(1)}, f32[16,1,256]{2,1,0:T(1,128)S(1)}, u32[]{:S(2)}, u32[]{:S(2)}) collective-permute-start(f32[16,1,256]{2,1,0:T(1,128)S(1)} %slice.936), channel_id=1, source_target_pairs={{1,0},{2,1},{3,2},{4,3},{5,4},{6,5},{7,6},{9,8},{10,9},{11,10},{12... | collective-permute-start | bytes 49160 | tf_op jit(solution)/shard_map/ppermute | solution.py:12
  11.5 0.9 %copy-start = (f32[16,8,256]{2,1,0:T(8,128)S(1)}, f32[16,8,256]{2,1,0:T(8,128)}, u32[]{:S(2)}) copy-start(f32[16,8,256]{2,1,0:T(8,128)} %param.11) | copy-start | bytes 393220
  11.5 0.9 %copy-start.6 = (f32[16,8,256]{2,1,0:T(8,128)S(1)}, f32[16,8,256]{2,1,0:T(8,128)}, u32[]{:S(2)}) copy-start(f32[16,8,256]{2,1,0:T(8,128)} %param.8) | copy-start | bytes 393220
  12.4 0.9 %copy-start.1 = (f32[16,8,256]{2,1,0:T(8,128)S(1)}, f32[16,8,256]{2,1,0:T(8,128)}, u32[]{:S(2)}) copy-start(f32[16,8,256]{2,1,0:T(8,128)} %param.13) | copy-start | bytes 393220
  13.4 0.9 %copy-start.3 = (f32[16,8,256]{2,1,0:T(8,128)S(1)}, f32[16,8,256]{2,1,0:T(8,128)}, u32[]{:S(2)}) copy-start(f32[16,8,256]{2,1,0:T(8,128)} %param.14) | copy-start | bytes 393220
  13.4 1.0 %copy-start.11 = (f32[16,8,256]{2,1,0:T(8,128)S(1)}, f32[16,8,256]{2,1,0:T(8,128)}, u32[]{:S(2)}) copy-start(f32[16,8,256]{2,1,0:T(8,128)} %param.15) | copy-start | bytes 393220
  14.6 0.9 %copy-start.8 = (f32[16,8,256]{2,1,0:T(8,128)S(1)}, f32[16,8,256]{2,1,0:T(8,128)}, u32[]{:S(2)}) copy-start(f32[16,8,256]{2,1,0:T(8,128)} %param.9) | copy-start | bytes 393220
  15.5 0.9 %copy-start.5 = (f32[16,8,256]{2,1,0:T(8,128)S(1)}, f32[16,8,256]{2,1,0:T(8,128)}, u32[]{:S(2)}) copy-start(f32[16,8,256]{2,1,0:T(8,128)} %param.10) | copy-start | bytes 393220
  15.5 1.0 %slice-start = ((f32[16,8,256]{2,1,0:T(8,128)}), f32[15,8,256]{2,1,0:T(8,128)S(1)}, s32[]{:S(2)}) async-start(f32[16,8,256]{2,1,0:T(8,128)} %param.10), calls=%async_computation | async-start | bytes 245760 | tf_op jit(solution)/shard_map/slice | solution.py:16
  17.7 4.9 %collective-permute-start = (f32[3,1,8,256]{3,2,1,0:T(8,128)S(1)}, f32[3,1,8,256]{3,2,1,0:T(8,128)S(1)}, u32[]{:S(2)}, u32[]{:S(2)}) collective-permute-start(f32[3,1,8,256]{3,2,1,0:T(8,128)S(1)} %pad_maximum_fusion.6), channel_id=1, source_target_pairs={{0,8},{8,16},{16,24},{1,9},{9,17},{17,25},{2,10},{10,18},{18,26},{... | collective-permute-start | bytes 73736 | tf_op jit(solution)/shard_map/ppermute | solution.py:12
  21.8 0.9 %copy-start.2 = (f32[16,8,256]{2,1,0:T(8,128)S(1)}, f32[16,8,256]{2,1,0:T(8,128)}, u32[]{:S(2)}) copy-start(f32[16,8,256]{2,1,0:T(8,128)} %param.12) | copy-start | bytes 393220
  23.6 17.9 %collective-permute-start.2 = (f32[7,1,8,256]{3,2,0,1:T(8,128)S(1)}, f32[7,1,8,256]{3,2,0,1:T(8,128)S(1)}, u32[]{:S(2)}, u32[]{:S(2)}) collective-permute-start(f32[7,1,8,256]{3,2,0,1:T(8,128)S(1)} %get-tuple-element.243), channel_id=1, source_target_pairs={{0,8},{8,16},{16,24},{24,0},{1,9},{9,17},{17,25},{25,1},{2,10},{10... | collective-permute-start | bytes 172040 | tf_op jit(solution)/shard_map/ppermute | solution.py:83
  25.4 16.2 %collective-permute-start.3 = (f32[7,1,8,256]{3,2,0,1:T(8,128)S(1)}, f32[7,1,8,256]{3,2,0,1:T(8,128)S(1)}, u32[]{:S(2)}, u32[]{:S(2)}) collective-permute-start(f32[7,1,8,256]{3,2,0,1:T(8,128)S(1)} %get-tuple-element.243), channel_id=1, source_target_pairs={{0,16},{8,24},{16,0},{24,8},{1,17},{9,25},{17,1},{25,9},{2,18},{10... | collective-permute-start | bytes 172040 | tf_op jit(solution)/shard_map/ppermute | solution.py:83
  29.5 15.5 %collective-permute-start.6 = (f32[7,16,1,256]{3,2,1,0:T(1,128)S(1)}, f32[7,16,1,256]{3,2,1,0:T(1,128)S(1)}, u32[]{:S(2)}, u32[]{:S(2)}) collective-permute-start(f32[7,16,1,256]{3,2,1,0:T(1,128)S(1)} %pad_maximum_fusion.3), channel_id=1, source_target_pairs={{0,1},{1,2},{2,3},{3,4},{4,5},{5,6},{6,7},{7,0},{8,9},{9,10},{10,1... | collective-permute-start | bytes 344072 | tf_op jit(solution)/shard_map/ppermute | solution.py:83
  33.9 12.7 %collective-permute-start.7 = (f32[7,16,1,256]{3,2,1,0:T(1,128)S(1)}, f32[7,16,1,256]{3,2,1,0:T(1,128)S(1)}, u32[]{:S(2)}, u32[]{:S(2)}) collective-permute-start(f32[7,16,1,256]{3,2,1,0:T(1,128)S(1)} %pad_maximum_fusion.3), channel_id=1, source_target_pairs={{0,2},{1,3},{2,4},{3,5},{4,6},{5,7},{6,0},{7,1},{8,10},{9,11},{10,... | collective-permute-start | bytes 344072 | tf_op jit(solution)/shard_map/ppermute | solution.py:83
  34.2 9.2 %collective-permute-start.4 = (f32[7,1,8,256]{3,2,1,0:T(8,128)S(1)}, f32[7,1,8,256]{3,2,1,0:T(8,128)S(1)}, u32[]{:S(2)}, u32[]{:S(2)}) collective-permute-start(f32[7,1,8,256]{3,2,1,0:T(8,128)S(1)} %get-tuple-element.244), channel_id=1, source_target_pairs={{0,24},{8,0},{16,8},{24,16},{1,25},{9,1},{17,9},{25,17},{2,26},{10... | collective-permute-start | bytes 172040 | tf_op jit(solution)/shard_map/ppermute | solution.py:83
  40.1 0.7 %copy-start.7 = (f32[16,8,256]{2,1,0:T(8,128)}, f32[16,8,256]{2,1,0:T(8,128)S(1)}, u32[]{:S(2)}) copy-start(f32[16,8,256]{2,1,0:T(8,128)S(1)} %fusion.26) | copy-start | bytes 393220
  41.5 5.1 %collective-permute-start.8 = (f32[7,16,1,256]{3,2,1,0:T(1,128)S(1)}, f32[7,16,1,256]{3,2,1,0:T(1,128)S(1)}, u32[]{:S(2)}, u32[]{:S(2)}) collective-permute-start(f32[7,16,1,256]{3,2,1,0:T(1,128)S(1)} %pad_maximum_fusion.3), channel_id=1, source_target_pairs={{0,3},{1,4},{2,5},{3,6},{4,7},{5,0},{6,1},{7,2},{8,11},{9,12},{10,... | collective-permute-start | bytes 344072 | tf_op jit(solution)/shard_map/ppermute | solution.py:83
  41.6 11.5 %collective-permute-start.9 = (f32[7,16,1,256]{3,2,1,0:T(1,128)S(1)}, f32[7,16,1,256]{3,2,1,0:T(1,128)S(1)}, u32[]{:S(2)}, u32[]{:S(2)}) collective-permute-start(f32[7,16,1,256]{3,2,1,0:T(1,128)S(1)} %pad_maximum_fusion.3), channel_id=1, source_target_pairs={{0,4},{1,5},{2,6},{3,7},{4,0},{5,1},{6,2},{7,3},{8,12},{9,13},{10,... | collective-permute-start | bytes 344072 | tf_op jit(solution)/shard_map/ppermute | solution.py:83
  43.4 10.8 %collective-permute-start.10 = (f32[7,16,1,256]{3,2,1,0:T(1,128)S(1)}, f32[7,16,1,256]{3,2,1,0:T(1,128)S(1)}, u32[]{:S(2)}, u32[]{:S(2)}) collective-permute-start(f32[7,16,1,256]{3,2,1,0:T(1,128)S(1)} %pad_maximum_fusion.3), channel_id=1, source_target_pairs={{0,5},{1,6},{2,7},{3,0},{4,1},{5,2},{6,3},{7,4},{8,13},{9,14},{10,... | collective-permute-start | bytes 344072 | tf_op jit(solution)/shard_map/ppermute | solution.py:83
  44.2 0.7 %copy-start.10 = (f32[16,8,256]{2,1,0:T(8,128)}, f32[16,8,256]{2,1,0:T(8,128)S(1)}, u32[]{:S(2)}) copy-start(f32[16,8,256]{2,1,0:T(8,128)S(1)} %fusion.5) | copy-start | bytes 393220
  44.9 9.2 %collective-permute-start.11 = (f32[7,16,1,256]{3,2,1,0:T(1,128)S(1)}, f32[7,16,1,256]{3,2,1,0:T(1,128)S(1)}, u32[]{:S(2)}, u32[]{:S(2)}) collective-permute-start(f32[7,16,1,256]{3,2,1,0:T(1,128)S(1)} %pad_maximum_fusion.3), channel_id=1, source_target_pairs={{0,6},{1,7},{2,0},{3,1},{4,2},{5,3},{6,4},{7,5},{8,14},{9,15},{10,... | collective-permute-start | bytes 344072 | tf_op jit(solution)/shard_map/ppermute | solution.py:83
  46.6 7.6 %collective-permute-start.12 = (f32[7,16,1,256]{3,2,1,0:T(1,128)S(1)}, f32[7,16,1,256]{3,2,1,0:T(1,128)S(1)}, u32[]{:S(2)}, u32[]{:S(2)}) collective-permute-start(f32[7,16,1,256]{3,2,1,0:T(1,128)S(1)} %pad_maximum_fusion.3), channel_id=1, source_target_pairs={{0,7},{1,0},{2,1},{3,2},{4,3},{5,4},{6,5},{7,6},{8,15},{9,8},{10,9... | collective-permute-start | bytes 344072 | tf_op jit(solution)/shard_map/ppermute | solution.py:83
  55.7 0.7 %copy-start.9 = (f32[16,8,256]{2,1,0:T(8,128)}, f32[16,8,256]{2,1,0:T(8,128)S(1)}, u32[]{:S(2)}) copy-start(f32[16,8,256]{2,1,0:T(8,128)S(1)} %fusion.1) | copy-start | bytes 393220

commit v4 on v3

--- a/solution.py
+++ b/solution.py
@@ -178,7 +178,6 @@
         1,
     )
     above_ez = passed_along(take_rows(electric_z, 0, 0, 1), "gy", -1)
-    cross_z = ahead_diff(electric_z, 0, above_ez)
     below_z = passed_along(
         jnp.stack(
             [
@@ -197,6 +196,10 @@
         0.0,
     )
     above_ex = passed_along(take_rows(electric_x, 1, 0, 1), "gz", -1)
+    below_y, above_ez, below_z, above_ex = lax.optimization_barrier(
+        (below_y, above_ez, below_z, above_ex)
+    )
+    cross_z = ahead_diff(electric_z, 0, above_ez)
     cross_x = ahead_diff(electric_x, 1, above_ex)
     source_x = keeping * electric_x + coupling * (
         behind_diff(magnetic_z, 0, below_y[0])

time: 57.4 us -> 54.2 us (0.944)
  local copies, waits for them, and re-layouts: 13 us -> 9.55 us
  waiting for transfers between devices: 8.29 us -> 9.81 us
  starting transfers between devices: 24.6 us -> 23.1 us
    another operation x3, local copies, waits for them, and re-layouts: 2.8 us -> 0.05 us  [body(): jnp.stack([take_rows(magnetic_y, 1, size_z - 1, 1), take_rows(magnetic_x,...]
    unnamed x32 -> x36, local copies, waits for them, and re-layouts: 5.46 us -> 3.88 us
    ppermute x4, waiting for transfers between devices: 0.82 us -> 2.36 us  [passed_along(): lax.ppermute(value, axis, [(source, source + steps) for source in range(f...]
    ppermute x10, starting transfers between devices: 13.8 us -> 12.6 us  [gathered(): lax.ppermute(values, axis, [(source, (source + shift) % count) for source...]
    another operation x3 -> x2, local copies, waits for them, and re-layouts: 0.01 us -> 0.7 us  [body(): jnp.stack([take_rows(magnetic_z, 0, size_y - 1, 1), take_rows(cross_y, 0,...]
    add x11 -> x13, other arithmetic: 1.08 us -> 1.28 us  [reduce_lines(): main_band = main_band + ratio_low * low_upper + ratio_high * high_lower]
    slice x74 -> x78, local copies, waits for them, and re-layouts: 4.67 us -> 4.83 us  [take_rows(): return lax.slice_in_dim(values, start, start + length, axis=direction)]
where the time goes in v4:
time: 54.2 us; the launch traced here: 53.9 us
  starting transfers between devices  23.1 us (43%)
  waiting for transfers between devices  9.81 us (18%)
  local copies, waits for them, and re-layouts  9.55 us (18%)
  other arithmetic  9.13 us (17%)
  between operations  2.3 us (4%)
    ppermute x10, starting transfers between devices, gathered(): lax.ppermute(values, axis, [(source, (source + shift) % count) for source...  12.6 us
    ppermute x4, starting transfers between devices, passed_along(): lax.ppermute(value, axis, [(source, source + steps) for source in range(f...  10.5 us
    ppermute x10, waiting for transfers between devices, gathered(): lax.ppermute(values, axis, [(source, (source + shift) % count) for source...  7.45 us
    slice x78, local copies, waits for them, and re-layouts, take_rows(): return lax.slice_in_dim(values, start, start + length, axis=direction)  4.83 us
    unnamed x36, local copies, waits for them, and re-layouts  3.88 us
    ppermute x4, waiting for transfers between devices, passed_along(): lax.ppermute(value, axis, [(source, source + steps) for source in range(f...  2.36 us
    add x12, other arithmetic, reduce_lines(): right_side + ratio_low[None] * low_right + ratio_high[None] * high_right  2.12 us
    add x13, other arithmetic, reduce_lines(): main_band = main_band + ratio_low * low_upper + ratio_high * high_lower  1.28 us
  transfers between devices with their start and end apart: 14, of which 3 were waited for; matrix products, arithmetic and copies ran while one was open for 17% of the time, Pallas kernels for 0%

profile of v4, /device:TPU:3, one launch (start us, length us, event | category | flops | bytes accessed | tf_op | source)
XLA Modules:
  0.0 53.9 jit_solution(2606446735676474288)
XLA Ops:
  0.6 0.7 %slice_bitcast_fusion.19 = f32[1,1,8,256]{3,2,1,0:T(8,128)S(1)} fusion(f32[16,8,256]{2,1,0:T(8,128)} %param.11), kind=kLoop, calls=%fused_computation.474 | loop fusion | bytes 16384 | tf_op jit(solution)/shard_map/stack | solution.py:170
  1.3 1.1 %slice.774 = f32[16,8,255]{2,1,0:T(8,128)S(1)} slice(f32[16,8,256]{2,1,0:T(8,128)} %param.9), slice={[0:16], [0:8], [1:256]} | slice | bytes 261120 | tf_op jit(solution)/shard_map/slice | solution.py:16
  2.5 0.8 %copy-done.1 = f32[16,8,256]{2,1,0:T(8,128)S(1)} copy-done((f32[16,8,256]{2,1,0:T(8,128)S(1)}, f32[16,8,256]{2,1,0:T(8,128)}, u32[]{:S(2)}) %copy-start.1) | copy-done | bytes 131096
  3.3 3.3 %collective-permute-start = (f32[3,1,8,256]{3,2,1,0:T(8,128)S(1)}, f32[3,1,8,256]{3,2,1,0:T(8,128)S(1)}, u32[]{:S(2)}, u32[]{:S(2)}) collective-permute-start(f32[3,1,8,256]{3,2,1,0:T(8,128)S(1)} %pad_maximum_fusion.6), channel_id=1, source_target_pairs={{0,8},{8,16},{16,24},{1,9},{9,17},{17,25},{2,10},{10,18},{18,26},{... | collective-permute-start | bytes 73736 | tf_op jit(solution)/shard_map/ppermute | solution.py:12
  6.7 1.3 %collective-permute-start.1 = (f32[1,8,256]{2,1,0:T(8,128)S(1)}, f32[1,8,256]{2,1,0:T(8,128)S(1)}, u32[]{:S(2)}, u32[]{:S(2)}) collective-permute-start(f32[1,8,256]{2,1,0:T(8,128)S(1)} %slice.777), channel_id=1, source_target_pairs={{8,0},{16,8},{24,16},{9,1},{17,9},{25,17},{10,2},{18,10},{26,18},{... | collective-permute-start | bytes 24584 | tf_op jit(solution)/shard_map/ppermute | solution.py:12
  8.2 4.0 %collective-permute-start.2 = (f32[3,16,1,256]{3,2,1,0:T(1,128)S(1)}, f32[3,16,1,256]{3,2,1,0:T(1,128)S(1)}, u32[]{:S(2)}, u32[]{:S(2)}) collective-permute-start(f32[3,16,1,256]{3,2,1,0:T(1,128)S(1)} %pad_maximum_fusion.5), channel_id=1, source_target_pairs={{0,1},{1,2},{2,3},{3,4},{4,5},{5,6},{6,7},{8,9},{9,10},{10,11},{11... | collective-permute-start | bytes 147464 | tf_op jit(solution)/shard_map/ppermute | solution.py:12
  12.2 1.9 %collective-permute-start.3 = (f32[16,1,256]{2,1,0:T(1,128)S(1)}, f32[16,1,256]{2,1,0:T(1,128)S(1)}, u32[]{:S(2)}, u32[]{:S(2)}) collective-permute-start(f32[16,1,256]{2,1,0:T(1,128)S(1)} %slice.781), channel_id=1, source_target_pairs={{1,0},{2,1},{3,2},{4,3},{5,4},{6,5},{7,6},{9,8},{10,9},{11,10},{12... | collective-permute-start | bytes 49160 | tf_op jit(solution)/shard_map/ppermute | solution.py:12
  14.3 0.8 %copy-done.5 = f32[16,8,256]{2,1,0:T(8,128)S(1)} copy-done((f32[16,8,256]{2,1,0:T(8,128)S(1)}, f32[16,8,256]{2,1,0:T(8,128)}, u32[]{:S(2)}) %copy-start.5) | copy-done | bytes 131096
  15.8 2.4 %collective-permute-done.3 = f32[16,1,256]{2,1,0:T(1,128)S(1)} collective-permute-done((f32[16,1,256]{2,1,0:T(1,128)S(1)}, f32[16,1,256]{2,1,0:T(1,128)S(1)}, u32[]{:S(2)}, u32[]{:S(2)}) %collective-permute-start.3) | collective-permute-done | bytes 16416 | tf_op jit(solution)/shard_map/ppermute | solution.py:12
  18.3 0.8 %copy-done.4 = f32[16,8,256]{2,1,0:T(8,128)S(1)} copy-done((f32[16,8,256]{2,1,0:T(8,128)S(1)}, f32[16,8,256]{2,1,0:T(8,128)}, u32[]{:S(2)}) %copy-start.4) | copy-done | bytes 131096
  19.3 0.2 fusion.21
  19.5 0.3 select_select_fusion.1
  20.1 0.1 multiply_add_fusion.4
  21.3 3.4 %collective-permute-start.5 = (f32[7,1,8,256]{3,2,0,1:T(8,128)S(1)}, f32[7,1,8,256]{3,2,0,1:T(8,128)S(1)}, u32[]{:S(2)}, u32[]{:S(2)}) collective-permute-start(f32[7,1,8,256]{3,2,0,1:T(8,128)S(1)} %get-tuple-element.249), channel_id=1, source_target_pairs={{0,16},{8,24},{16,0},{24,8},{1,17},{9,25},{17,1},{25,9},{2,18},{10... | collective-permute-start | bytes 172040 | tf_op jit(solution)/shard_map/ppermute | solution.py:83
  24.7 1.3 %collective-permute-start.4 = (f32[7,1,8,256]{3,2,0,1:T(8,128)S(1)}, f32[7,1,8,256]{3,2,0,1:T(8,128)S(1)}, u32[]{:S(2)}, u32[]{:S(2)}) collective-permute-start(f32[7,1,8,256]{3,2,0,1:T(8,128)S(1)} %get-tuple-element.249), channel_id=1, source_target_pairs={{0,8},{8,16},{16,24},{24,0},{1,9},{9,17},{17,25},{25,1},{2,10},{10... | collective-permute-start | bytes 172040 | tf_op jit(solution)/shard_map/ppermute | solution.py:83
  26.2 0.2 multiply_add_fusion.1
  26.7 0.1 multiply_add_fusion
  27.2 0.1 add_divide_fusion
  27.4 0.1 pad_maximum_fusion.3
  27.5 1.6 %collective-permute-start.7 = (f32[7,16,1,256]{3,2,1,0:T(1,128)S(1)}, f32[7,16,1,256]{3,2,1,0:T(1,128)S(1)}, u32[]{:S(2)}, u32[]{:S(2)}) collective-permute-start(f32[7,16,1,256]{3,2,1,0:T(1,128)S(1)} %pad_maximum_fusion.3), channel_id=1, source_target_pairs={{0,1},{1,2},{2,3},{3,4},{4,5},{5,6},{6,7},{7,0},{8,9},{9,10},{10,1... | collective-permute-start | bytes 344072 | tf_op jit(solution)/shard_map/ppermute | solution.py:83
  29.1 0.3 collective-permute-start.8
  29.4 2.0 %collective-permute-start.6 = (f32[7,1,8,256]{3,2,1,0:T(8,128)S(1)}, f32[7,1,8,256]{3,2,1,0:T(8,128)S(1)}, u32[]{:S(2)}, u32[]{:S(2)}) collective-permute-start(f32[7,1,8,256]{3,2,1,0:T(8,128)S(1)} %get-tuple-element.250), channel_id=1, source_target_pairs={{0,24},{8,0},{16,8},{24,16},{1,25},{9,1},{17,9},{25,17},{2,26},{10... | collective-permute-start | bytes 172040 | tf_op jit(solution)/shard_map/ppermute | solution.py:83
  31.5 0.1 fusion.41
  31.9 0.1 multiply_add_fusion.11
  32.2 0.2 fusion.39
  32.7 0.1 multiply_add_fusion.10
  33.0 0.2 fusion.37
  33.5 0.1 multiply_add_fusion.9
  33.7 0.2 fusion.35
  34.3 0.1 multiply_add_fusion.8
  34.5 0.2 fusion.33
  35.1 0.1 multiply_add_fusion.7
  35.3 0.2 fusion.31
  35.9 0.1 multiply_add_fusion.6
  36.1 0.2 fusion.29
  36.5 0.2 pad_multiply_fusion
  37.0 0.5 %copy-done.10 = f32[16,8,256]{2,1,0:T(8,128)} copy-done((f32[16,8,256]{2,1,0:T(8,128)}, f32[16,8,256]{2,1,0:T(8,128)S(1)}, u32[]{:S(2)}) %copy-start.10) | copy-done | bytes 131096
  37.5 0.7 %add_subtract_fusion = f32[16,8,256]{2,1,0:T(8,128)} fusion(f32[16,8,256]{2,1,0:T(8,128)S(1)} %maximum_subtract_fusion.6, f32[16,8,256]{2,1,0:T(8,128)S(1)} %copy-done.2, f32[16,8,256]{2,1,0:T(8,128)S(1)} %fusion.26, f32[16,8,255]{2,1,0:T(8,128)S(1)} %slice.1139), kind=kLoop, calls=%fused_computation.86 | loop fusion | flops 98304 | bytes 654848 | tf_op jit(solution)/shard_map/sub | solution.py:234
  38.4 1.8 %collective-permute-start.10 = (f32[7,16,1,256]{3,2,1,0:T(1,128)S(1)}, f32[7,16,1,256]{3,2,1,0:T(1,128)S(1)}, u32[]{:S(2)}, u32[]{:S(2)}) collective-permute-start(f32[7,16,1,256]{3,2,1,0:T(1,128)S(1)} %pad_maximum_fusion.3), channel_id=1, source_target_pairs={{0,4},{1,5},{2,6},{3,7},{4,0},{5,1},{6,2},{7,3},{8,12},{9,13},{10,... | collective-permute-start | bytes 344072 | tf_op jit(solution)/shard_map/ppermute | solution.py:83
  40.2 0.5 collective-permute-start.11
  41.0 0.7 %fusion.25 = f32[16,8,256]{2,1,0:T(8,128)} fusion(f32[16,8,256]{2,1,0:T(8,128)S(1)} %copy-done.4, f32[16,8,256]{2,1,0:T(8,128)S(1)} %copy-done.1, f32[1,8,256]{2,1,0:T(8,128)S(1)} %bitcast.786, f32[15,8,256]{2,1,0:T(8,128)S(1)} %slice.1140, f32[8,256]{1,0:T(8,128)S(1)} %bitcast.785, f32[3,16,8,256]{3,2,1,0:T(8,128)S(1)} %add_divide_fusion.1, ...), kind=kLoop, calls=%fused_computation.51 | loop fusion | flops 262144 | bytes 933888 | tf_op jit(solution)/shard_map/sub | solution.py:236
  41.8 1.6 %collective-permute-start.12 = (f32[7,16,1,256]{3,2,1,0:T(1,128)S(1)}, f32[7,16,1,256]{3,2,1,0:T(1,128)S(1)}, u32[]{:S(2)}, u32[]{:S(2)}) collective-permute-start(f32[7,16,1,256]{3,2,1,0:T(1,128)S(1)} %pad_maximum_fusion.3), channel_id=1, source_target_pairs={{0,6},{1,7},{2,0},{3,1},{4,2},{5,3},{6,4},{7,5},{8,14},{9,15},{10,... | collective-permute-start | bytes 344072 | tf_op jit(solution)/shard_map/ppermute | solution.py:83
  43.5 6.4 %collective-permute-done.10 = f32[7,16,1,256]{3,2,1,0:T(1,128)S(1)} collective-permute-done((f32[7,16,1,256]{3,2,1,0:T(1,128)S(1)}, f32[7,16,1,256]{3,2,1,0:T(1,128)S(1)}, u32[]{:S(2)}, u32[]{:S(2)}) %collective-permute-start.10) | collective-permute-done | bytes 114720 | tf_op jit(solution)/shard_map/ppermute | solution.py:83
  50.0 1.0 %collective-permute-done.11 = f32[7,16,1,256]{3,2,1,0:T(1,128)S(1)} collective-permute-done((f32[7,16,1,256]{3,2,1,0:T(1,128)S(1)}, f32[7,16,1,256]{3,2,1,0:T(1,128)S(1)}, u32[]{:S(2)}, u32[]{:S(2)}) %collective-permute-start.11) | collective-permute-done | bytes 114720 | tf_op jit(solution)/shard_map/ppermute | solution.py:83
  51.1 0.6 %fusion.121 = (f32[1,16,1,256]{3,2,1,0:T(1,128)S(1)}, f32[1,16,1,256]{3,2,1,0:T(1,128)S(1)}, f32[1,16,1,256]{3,2,1,0:T(1,128)S(1)}, f32[1,16,1,256]{3,2,1,0:T(1,...) fusion(f32[8,7,16,1,256]{4,3,2,1,0:T(1,128)S(1)} %bitcast_dynam, ...), kind=kLoop, calls=%fused_computation.360 | loop fusion | flops 385024 | bytes 1130548 | tf_op jit(solution)/shard_map/mul | solution.py:114
  51.7 0.3 constant_dynamic-update-slice_fusion.7
  52.5 0.6 %copy-done.11 = f32[16,8,256]{2,1,0:T(8,128)} copy-done((f32[16,8,256]{2,1,0:T(8,128)}, f32[16,8,256]{2,1,0:T(8,128)S(1)}, u32[]{:S(2)}) %copy-start.11) | copy-done | bytes 131096
  53.1 0.7 %fusion.23 = f32[16,8,256]{2,1,0:T(8,128)} fusion(f32[16,8,256]{2,1,0:T(8,128)S(1)} %maximum_subtract_fusion.4, f32[16,8,256]{2,1,0:T(8,128)S(1)} %copy-done, f32[16,1,256]{2,1,0:T(1,128)S(1)} %fusion.284, f32[16,7,256]{2,1,0:T(8,128)S(1)} %slice.1138, f32[16,256]{1,0:T(8,128)S(1)} %bitcast.781, f32[3,16,8,256]{3,2,1,0:T(8,128)S(1)} %add_divide_fusion, ...), kind=kLoop, calls=%fused_computation.48 | loop fusion | flops 262144 | bytes 950272 | tf_op jit(solution)/shard_map/sub | solution.py:232
  (193 shorter events, 6.6 us)
Async XLA Ops:
  1.3 1.1 %copy-start.9 = (f32[16,8,256]{2,1,0:T(8,128)S(1)}, f32[16,8,256]{2,1,0:T(8,128)}, u32[]{:S(2)}) copy-start(f32[16,8,256]{2,1,0:T(8,128)} %param.9) | copy-start | bytes 393220
  2.4 0.9 %copy-start.1 = (f32[16,8,256]{2,1,0:T(8,128)S(1)}, f32[16,8,256]{2,1,0:T(8,128)}, u32[]{:S(2)}) copy-start(f32[16,8,256]{2,1,0:T(8,128)} %param.13) | copy-start | bytes 393220
  2.4 4.3 %copy-start.6 = (f32[16,8,256]{2,1,0:T(8,128)S(1)}, f32[16,8,256]{2,1,0:T(8,128)}, u32[]{:S(2)}) copy-start(f32[16,8,256]{2,1,0:T(8,128)} %param.10) | copy-start | bytes 393220
  2.4 5.6 %copy-start.2 = (f32[16,8,256]{2,1,0:T(8,128)S(1)}, f32[16,8,256]{2,1,0:T(8,128)}, u32[]{:S(2)}) copy-start(f32[16,8,256]{2,1,0:T(8,128)} %param.12) | copy-start | bytes 393220
  3.3 10.9 %copy-start.3 = (f32[16,8,256]{2,1,0:T(8,128)}, f32[16,8,256]{2,1,0:T(8,128)S(1)}, u32[]{:S(2)}) copy-start(f32[16,8,256]{2,1,0:T(8,128)S(1)} %pad_subtract_fusion) | copy-start | bytes 393220
  3.3 4.7 %copy-start = (f32[16,8,256]{2,1,0:T(8,128)S(1)}, f32[16,8,256]{2,1,0:T(8,128)}, u32[]{:S(2)}) copy-start(f32[16,8,256]{2,1,0:T(8,128)} %param.11) | copy-start | bytes 393220
  3.3 8.8 %copy-start.8 = (f32[16,8,256]{2,1,0:T(8,128)S(1)}, f32[16,8,256]{2,1,0:T(8,128)}, u32[]{:S(2)}) copy-start(f32[16,8,256]{2,1,0:T(8,128)} %param.8) | copy-start | bytes 393220
  3.3 14.8 %collective-permute-start = (f32[3,1,8,256]{3,2,1,0:T(8,128)S(1)}, f32[3,1,8,256]{3,2,1,0:T(8,128)S(1)}, u32[]{:S(2)}, u32[]{:S(2)}) collective-permute-start(f32[3,1,8,256]{3,2,1,0:T(8,128)S(1)} %pad_maximum_fusion.6), channel_id=1, source_target_pairs={{0,8},{8,16},{16,24},{1,9},{9,17},{17,25},{2,10},{10,18},{18,26},{... | collective-permute-start | bytes 73736 | tf_op jit(solution)/shard_map/ppermute | solution.py:12
  6.7 8.9 %collective-permute-start.1 = (f32[1,8,256]{2,1,0:T(8,128)S(1)}, f32[1,8,256]{2,1,0:T(8,128)S(1)}, u32[]{:S(2)}, u32[]{:S(2)}) collective-permute-start(f32[1,8,256]{2,1,0:T(8,128)S(1)} %slice.777), channel_id=1, source_target_pairs={{8,0},{16,8},{24,16},{9,1},{17,9},{25,17},{10,2},{18,10},{26,18},{... | collective-permute-start | bytes 24584 | tf_op jit(solution)/shard_map/ppermute | solution.py:12
  8.2 10.0 %collective-permute-start.2 = (f32[3,16,1,256]{3,2,1,0:T(1,128)S(1)}, f32[3,16,1,256]{3,2,1,0:T(1,128)S(1)}, u32[]{:S(2)}, u32[]{:S(2)}) collective-permute-start(f32[3,16,1,256]{3,2,1,0:T(1,128)S(1)} %pad_maximum_fusion.5), channel_id=1, source_target_pairs={{0,1},{1,2},{2,3},{3,4},{4,5},{5,6},{6,7},{8,9},{9,10},{10,11},{11... | collective-permute-start | bytes 147464 | tf_op jit(solution)/shard_map/ppermute | solution.py:12
  12.2 6.0 %collective-permute-start.3 = (f32[16,1,256]{2,1,0:T(1,128)S(1)}, f32[16,1,256]{2,1,0:T(1,128)S(1)}, u32[]{:S(2)}, u32[]{:S(2)}) collective-permute-start(f32[16,1,256]{2,1,0:T(1,128)S(1)} %slice.781), channel_id=1, source_target_pairs={{1,0},{2,1},{3,2},{4,3},{5,4},{6,5},{7,6},{9,8},{10,9},{11,10},{12... | collective-permute-start | bytes 49160 | tf_op jit(solution)/shard_map/ppermute | solution.py:12
  14.2 0.9 %copy-start.5 = (f32[16,8,256]{2,1,0:T(8,128)S(1)}, f32[16,8,256]{2,1,0:T(8,128)}, u32[]{:S(2)}) copy-start(f32[16,8,256]{2,1,0:T(8,128)} %param.14) | copy-start | bytes 393220
  14.2 1.0 %copy-start.13 = (f32[16,8,256]{2,1,0:T(8,128)S(1)}, f32[16,8,256]{2,1,0:T(8,128)}, u32[]{:S(2)}) copy-start(f32[16,8,256]{2,1,0:T(8,128)} %param.15) | copy-start | bytes 393220
  15.6 2.6 %copy-start.7 = (f32[16,8,256]{2,1,0:T(8,128)S(1)}, f32[16,8,256]{2,1,0:T(8,128)}, u32[]{:S(2)}) copy-start(f32[16,8,256]{2,1,0:T(8,128)} %param.10) | copy-start | bytes 393220
  15.6 2.6 %slice-start.3 = ((f32[16,8,256]{2,1,0:T(8,128)}), f32[15,8,256]{2,1,0:T(8,128)S(1)}, s32[]{:S(2)}) async-start(f32[16,8,256]{2,1,0:T(8,128)} %param.10), calls=%async_computation.3 | async-start | bytes 245760 | tf_op jit(solution)/shard_map/slice | solution.py:16
  18.2 0.9 %copy-start.4 = (f32[16,8,256]{2,1,0:T(8,128)S(1)}, f32[16,8,256]{2,1,0:T(8,128)}, u32[]{:S(2)}) copy-start(f32[16,8,256]{2,1,0:T(8,128)} %copy-done.3) | copy-start | bytes 393220
  18.2 0.9 %slice-start = ((f32[16,8,256]{2,1,0:T(8,128)}), f32[15,8,256]{2,1,0:T(8,128)S(1)}, s32[]{:S(2)}) async-start(f32[16,8,256]{2,1,0:T(8,128)} %param.11), calls=%async_computation | async-start | bytes 245760 | tf_op jit(solution)/shard_map/slice | solution.py:16
  18.2 1.0 %slice-start.1 = ((f32[16,8,256]{2,1,0:T(8,128)}), f32[15,8,256]{2,1,0:T(8,128)S(1)}, s32[]{:S(2)}) async-start(f32[16,8,256]{2,1,0:T(8,128)} %param.13), calls=%async_computation.1 | async-start | bytes 245760 | tf_op jit(solution)/shard_map/slice | solution.py:16
  18.2 1.0 %slice-start.2 = ((f32[16,8,256]{2,1,0:T(8,128)}), f32[15,8,256]{2,1,0:T(8,128)S(1)}, s32[]{:S(2)}) async-start(f32[16,8,256]{2,1,0:T(8,128)} %copy-done.3), calls=%async_computation.2 | async-start | bytes 245760 | tf_op jit(solution)/shard_map/slice | solution.py:16
  21.3 17.2 %collective-permute-start.5 = (f32[7,1,8,256]{3,2,0,1:T(8,128)S(1)}, f32[7,1,8,256]{3,2,0,1:T(8,128)S(1)}, u32[]{:S(2)}, u32[]{:S(2)}) collective-permute-start(f32[7,1,8,256]{3,2,0,1:T(8,128)S(1)} %get-tuple-element.249), channel_id=1, source_target_pairs={{0,16},{8,24},{16,0},{24,8},{1,17},{9,25},{17,1},{25,9},{2,18},{10... | collective-permute-start | bytes 172040 | tf_op jit(solution)/shard_map/ppermute | solution.py:83
  24.7 15.5 %collective-permute-start.4 = (f32[7,1,8,256]{3,2,0,1:T(8,128)S(1)}, f32[7,1,8,256]{3,2,0,1:T(8,128)S(1)}, u32[]{:S(2)}, u32[]{:S(2)}) collective-permute-start(f32[7,1,8,256]{3,2,0,1:T(8,128)S(1)} %get-tuple-element.249), channel_id=1, source_target_pairs={{0,8},{8,16},{16,24},{24,0},{1,9},{9,17},{17,25},{25,1},{2,10},{10... | collective-permute-start | bytes 172040 | tf_op jit(solution)/shard_map/ppermute | solution.py:83
  27.5 14.3 %collective-permute-start.7 = (f32[7,16,1,256]{3,2,1,0:T(1,128)S(1)}, f32[7,16,1,256]{3,2,1,0:T(1,128)S(1)}, u32[]{:S(2)}, u32[]{:S(2)}) collective-permute-start(f32[7,16,1,256]{3,2,1,0:T(1,128)S(1)} %pad_maximum_fusion.3), channel_id=1, source_target_pairs={{0,1},{1,2},{2,3},{3,4},{4,5},{5,6},{6,7},{7,0},{8,9},{9,10},{10,1... | collective-permute-start | bytes 344072 | tf_op jit(solution)/shard_map/ppermute | solution.py:83
  29.1 14.3 %collective-permute-start.8 = (f32[7,16,1,256]{3,2,1,0:T(1,128)S(1)}, f32[7,16,1,256]{3,2,1,0:T(1,128)S(1)}, u32[]{:S(2)}, u32[]{:S(2)}) collective-permute-start(f32[7,16,1,256]{3,2,1,0:T(1,128)S(1)} %pad_maximum_fusion.3), channel_id=1, source_target_pairs={{0,2},{1,3},{2,4},{3,5},{4,6},{5,7},{6,0},{7,1},{8,10},{9,11},{10,... | collective-permute-start | bytes 344072 | tf_op jit(solution)/shard_map/ppermute | solution.py:83
  29.4 9.0 %collective-permute-start.6 = (f32[7,1,8,256]{3,2,1,0:T(8,128)S(1)}, f32[7,1,8,256]{3,2,1,0:T(8,128)S(1)}, u32[]{:S(2)}, u32[]{:S(2)}) collective-permute-start(f32[7,1,8,256]{3,2,1,0:T(8,128)S(1)} %get-tuple-element.250), channel_id=1, source_target_pairs={{0,24},{8,0},{16,8},{24,16},{1,25},{9,1},{17,9},{25,17},{2,26},{10... | collective-permute-start | bytes 172040 | tf_op jit(solution)/shard_map/ppermute | solution.py:83
  36.9 0.7 %copy-start.10 = (f32[16,8,256]{2,1,0:T(8,128)}, f32[16,8,256]{2,1,0:T(8,128)S(1)}, u32[]{:S(2)}) copy-start(f32[16,8,256]{2,1,0:T(8,128)S(1)} %fusion.26) | copy-start | bytes 393220
  38.4 5.1 %collective-permute-start.9 = (f32[7,16,1,256]{3,2,1,0:T(1,128)S(1)}, f32[7,16,1,256]{3,2,1,0:T(1,128)S(1)}, u32[]{:S(2)}, u32[]{:S(2)}) collective-permute-start(f32[7,16,1,256]{3,2,1,0:T(1,128)S(1)} %pad_maximum_fusion.3), channel_id=1, source_target_pairs={{0,3},{1,4},{2,5},{3,6},{4,7},{5,0},{6,1},{7,2},{8,11},{9,12},{10,... | collective-permute-start | bytes 344072 | tf_op jit(solution)/shard_map/ppermute | solution.py:83
  38.4 11.5 %collective-permute-start.10 = (f32[7,16,1,256]{3,2,1,0:T(1,128)S(1)}, f32[7,16,1,256]{3,2,1,0:T(1,128)S(1)}, u32[]{:S(2)}, u32[]{:S(2)}) collective-permute-start(f32[7,16,1,256]{3,2,1,0:T(1,128)S(1)} %pad_maximum_fusion.3), channel_id=1, source_target_pairs={{0,4},{1,5},{2,6},{3,7},{4,0},{5,1},{6,2},{7,3},{8,12},{9,13},{10,... | collective-permute-start | bytes 344072 | tf_op jit(solution)/shard_map/ppermute | solution.py:83
  40.2 10.8 %collective-permute-start.11 = (f32[7,16,1,256]{3,2,1,0:T(1,128)S(1)}, f32[7,16,1,256]{3,2,1,0:T(1,128)S(1)}, u32[]{:S(2)}, u32[]{:S(2)}) collective-permute-start(f32[7,16,1,256]{3,2,1,0:T(1,128)S(1)} %pad_maximum_fusion.3), channel_id=1, source_target_pairs={{0,5},{1,6},{2,7},{3,0},{4,1},{5,2},{6,3},{7,4},{8,13},{9,14},{10,... | collective-permute-start | bytes 344072 | tf_op jit(solution)/shard_map/ppermute | solution.py:83
  41.0 0.8 %copy-start.12 = (f32[16,8,256]{2,1,0:T(8,128)}, f32[16,8,256]{2,1,0:T(8,128)S(1)}, u32[]{:S(2)}) copy-start(f32[16,8,256]{2,1,0:T(8,128)S(1)} %fusion.5) | copy-start | bytes 393220
  41.8 9.2 %collective-permute-start.12 = (f32[7,16,1,256]{3,2,1,0:T(1,128)S(1)}, f32[7,16,1,256]{3,2,1,0:T(1,128)S(1)}, u32[]{:S(2)}, u32[]{:S(2)}) collective-permute-start(f32[7,16,1,256]{3,2,1,0:T(1,128)S(1)} %pad_maximum_fusion.3), channel_id=1, source_target_pairs={{0,6},{1,7},{2,0},{3,1},{4,2},{5,3},{6,4},{7,5},{8,14},{9,15},{10,... | collective-permute-start | bytes 344072 | tf_op jit(solution)/shard_map/ppermute | solution.py:83
  43.4 7.6 %collective-permute-start.13 = (f32[7,16,1,256]{3,2,1,0:T(1,128)S(1)}, f32[7,16,1,256]{3,2,1,0:T(1,128)S(1)}, u32[]{:S(2)}, u32[]{:S(2)}) collective-permute-start(f32[7,16,1,256]{3,2,1,0:T(1,128)S(1)} %pad_maximum_fusion.3), channel_id=1, source_target_pairs={{0,7},{1,0},{2,1},{3,2},{4,3},{5,4},{6,5},{7,6},{8,15},{9,8},{10,9... | collective-permute-start | bytes 344072 | tf_op jit(solution)/shard_map/ppermute | solution.py:83
  52.5 0.7 %copy-start.11 = (f32[16,8,256]{2,1,0:T(8,128)}, f32[16,8,256]{2,1,0:T(8,128)S(1)}, u32[]{:S(2)}) copy-start(f32[16,8,256]{2,1,0:T(8,128)S(1)} %fusion.1) | copy-start | bytes 393220

commit v5 on v4

--- a/solution.py
+++ b/solution.py
@@ -216,9 +216,6 @@
         - behind_diff(cross_x, 2, edge_zeros(cross_x, 2))
         - behind_diff(magnetic_x, 0, below_y[2])
     )
-    index_x = lax.broadcasted_iota(jnp.int32, coupling.shape, 2)
-    lower_x, main_x, upper_x = bands(coupling, damping, index_x, size_x)
-    half_electric_z = reduce_lines(lower_x, main_x, upper_x, source_z[None], 2)[0]
     index_z = lax.broadcasted_iota(jnp.int32, coupling.shape, 1) + lax.axis_index("gz") * size_z
     lower_z, main_z, upper_z = bands(coupling, damping, index_z, size_z * lax.axis_size("gz"))
     half_electric_y, fresh_ey = partitioned(
@@ -229,6 +226,10 @@
     half_electric_x, fresh_ex = partitioned(
         lower_y, main_y, upper_y, source_x, 0, "gy", jnp.zeros_like(source_x[None, :1])
     )
+    source_z, _ = lax.optimization_barrier((source_z, fresh_ex))
+    index_x = lax.broadcasted_iota(jnp.int32, coupling.shape, 2)
+    lower_x, main_x, upper_x = bands(coupling, damping, index_x, size_x)
+    half_electric_z = reduce_lines(lower_x, main_x, upper_x, source_z[None], 2)[0]
     half_magnetic_x = magnetic_x + ahead_diff(half_electric_y, 1, fresh_ey) - cross_z
     half_magnetic_y = (
         magnetic_y + ahead_diff(half_electric_z, 2, edge_zeros(half_electric_z, 2)) - cross_x

time: 54.2 us -> 52.6 us (0.970)
  the two profiles are of different devices: /device:TPU:3 before, /device:TPU:0 now
where the time goes in v5:
time: 52.6 us; the launch traced here: 52.1 us
  starting transfers between devices  27.8 us (53%)
  other arithmetic  9.14 us (17%)
  local copies, waits for them, and re-layouts  9.01 us (17%)
  waiting for transfers between devices  3.91 us (7%)
  between operations  2.27 us (4%)
    ppermute x10, starting transfers between devices, gathered(): lax.ppermute(values, axis, [(source, (source + shift) % count) for source...  18.7 us
    ppermute x4, starting transfers between devices, passed_along(): lax.ppermute(value, axis, [(source, source + steps) for source in range(f...  9.11 us
    slice x78, local copies, waits for them, and re-layouts, take_rows(): return lax.slice_in_dim(values, start, start + length, axis=direction)  4.83 us
    unnamed x36, local copies, waits for them, and re-layouts  3.33 us
    ppermute x10, waiting for transfers between devices, gathered(): lax.ppermute(values, axis, [(source, (source + shift) % count) for source...  2.24 us
    add x12, other arithmetic, reduce_lines(): right_side + ratio_low[None] * low_right + ratio_high[None] * high_right  2.13 us
    ppermute x4, waiting for transfers between devices, passed_along(): lax.ppermute(value, axis, [(source, source + steps) for source in range(f...  1.67 us
    add x13, other arithmetic, reduce_lines(): main_band = main_band + ratio_low * low_upper + ratio_high * high_lower  1.28 us
  transfers between devices with their start and end apart: 14, of which 3 were waited for; matrix products, arithmetic and copies ran while one was open for 17% of the time, Pallas kernels for 0%

profile of v5, /device:TPU:0, one launch (start us, length us, event | category | flops | bytes accessed | tf_op | source)
XLA Modules:
  0.0 52.1 jit_solution(208478779126837344)
XLA Ops:
  0.6 0.7 %slice_bitcast_fusion.19 = f32[1,1,8,256]{3,2,1,0:T(8,128)S(1)} fusion(f32[16,8,256]{2,1,0:T(8,128)} %param.11), kind=kLoop, calls=%fused_computation.473 | loop fusion | bytes 16384 | tf_op jit(solution)/shard_map/stack | solution.py:170
  1.3 1.1 %slice.774 = f32[16,8,255]{2,1,0:T(8,128)S(1)} slice(f32[16,8,256]{2,1,0:T(8,128)} %param.9), slice={[0:16], [0:8], [1:256]} | slice | bytes 261120 | tf_op jit(solution)/shard_map/slice | solution.py:16
  2.5 0.8 %copy-done.1 = f32[16,8,256]{2,1,0:T(8,128)S(1)} copy-done((f32[16,8,256]{2,1,0:T(8,128)S(1)}, f32[16,8,256]{2,1,0:T(8,128)}, u32[]{:S(2)}) %copy-start.1) | copy-done | bytes 131096
  3.3 5.1 %collective-permute-start = (f32[3,1,8,256]{3,2,1,0:T(8,128)S(1)}, f32[3,1,8,256]{3,2,1,0:T(8,128)S(1)}, u32[]{:S(2)}, u32[]{:S(2)}) collective-permute-start(f32[3,1,8,256]{3,2,1,0:T(8,128)S(1)} %pad_maximum_fusion.6), channel_id=1, source_target_pairs={{0,8},{8,16},{16,24},{1,9},{9,17},{17,25},{2,10},{10,18},{18,26},{... | collective-permute-start | bytes 73736 | tf_op jit(solution)/shard_map/ppermute | solution.py:12
  8.4 1.3 %collective-permute-start.1 = (f32[1,8,256]{2,1,0:T(8,128)S(1)}, f32[1,8,256]{2,1,0:T(8,128)S(1)}, u32[]{:S(2)}, u32[]{:S(2)}) collective-permute-start(f32[1,8,256]{2,1,0:T(8,128)S(1)} %slice.777), channel_id=1, source_target_pairs={{8,0},{16,8},{24,16},{9,1},{17,9},{25,17},{10,2},{18,10},{26,18},{... | collective-permute-start | bytes 24584 | tf_op jit(solution)/shard_map/ppermute | solution.py:12
  9.9 1.5 %collective-permute-start.2 = (f32[3,16,1,256]{3,2,1,0:T(1,128)S(1)}, f32[3,16,1,256]{3,2,1,0:T(1,128)S(1)}, u32[]{:S(2)}, u32[]{:S(2)}) collective-permute-start(f32[3,16,1,256]{3,2,1,0:T(1,128)S(1)} %pad_maximum_fusion.5), channel_id=1, source_target_pairs={{0,1},{1,2},{2,3},{3,4},{4,5},{5,6},{6,7},{8,9},{9,10},{10,11},{11... | collective-permute-start | bytes 147464 | tf_op jit(solution)/shard_map/ppermute | solution.py:12
  11.4 1.3 %collective-permute-start.3 = (f32[16,1,256]{2,1,0:T(1,128)S(1)}, f32[16,1,256]{2,1,0:T(1,128)S(1)}, u32[]{:S(2)}, u32[]{:S(2)}) collective-permute-start(f32[16,1,256]{2,1,0:T(1,128)S(1)} %slice.781), channel_id=1, source_target_pairs={{1,0},{2,1},{3,2},{4,3},{5,4},{6,5},{7,6},{9,8},{10,9},{11,10},{12... | collective-permute-start | bytes 49160 | tf_op jit(solution)/shard_map/ppermute | solution.py:12
  12.9 0.8 %copy-done.5 = f32[16,8,256]{2,1,0:T(8,128)S(1)} copy-done((f32[16,8,256]{2,1,0:T(8,128)S(1)}, f32[16,8,256]{2,1,0:T(8,128)}, u32[]{:S(2)}) %copy-start.5) | copy-done | bytes 131096
  14.4 1.7 %collective-permute-done.3 = f32[16,1,256]{2,1,0:T(1,128)S(1)} collective-permute-done((f32[16,1,256]{2,1,0:T(1,128)S(1)}, f32[16,1,256]{2,1,0:T(1,128)S(1)}, u32[]{:S(2)}, u32[]{:S(2)}) %collective-permute-start.3) | collective-permute-done | bytes 16416 | tf_op jit(solution)/shard_map/ppermute | solution.py:12
  16.2 0.8 %copy-done.4 = f32[16,8,256]{2,1,0:T(8,128)S(1)} copy-done((f32[16,8,256]{2,1,0:T(8,128)S(1)}, f32[16,8,256]{2,1,0:T(8,128)}, u32[]{:S(2)}) %copy-start.4) | copy-done | bytes 131096
  17.2 0.2 fusion.20
  17.4 0.3 select_select_fusion.1
  18.0 0.1 multiply_add_fusion.4
  19.2 3.7 %collective-permute-start.5 = (f32[7,1,8,256]{3,2,0,1:T(8,128)S(1)}, f32[7,1,8,256]{3,2,0,1:T(8,128)S(1)}, u32[]{:S(2)}, u32[]{:S(2)}) collective-permute-start(f32[7,1,8,256]{3,2,0,1:T(8,128)S(1)} %get-tuple-element.251), channel_id=1, source_target_pairs={{0,16},{8,24},{16,0},{24,8},{1,17},{9,25},{17,1},{25,9},{2,18},{10... | collective-permute-start | bytes 172040 | tf_op jit(solution)/shard_map/ppermute | solution.py:83
  22.9 1.6 %collective-permute-start.4 = (f32[7,1,8,256]{3,2,0,1:T(8,128)S(1)}, f32[7,1,8,256]{3,2,0,1:T(8,128)S(1)}, u32[]{:S(2)}, u32[]{:S(2)}) collective-permute-start(f32[7,1,8,256]{3,2,0,1:T(8,128)S(1)} %get-tuple-element.251), channel_id=1, source_target_pairs={{0,8},{8,16},{16,24},{24,0},{1,9},{9,17},{17,25},{25,1},{2,10},{10... | collective-permute-start | bytes 172040 | tf_op jit(solution)/shard_map/ppermute | solution.py:83
  24.5 2.3 %collective-permute-start.6 = (f32[7,1,8,256]{3,2,1,0:T(8,128)S(1)}, f32[7,1,8,256]{3,2,1,0:T(8,128)S(1)}, u32[]{:S(2)}, u32[]{:S(2)}) collective-permute-start(f32[7,1,8,256]{3,2,1,0:T(8,128)S(1)} %get-tuple-element.252), channel_id=1, source_target_pairs={{0,24},{8,0},{16,8},{24,16},{1,25},{9,1},{17,9},{25,17},{2,26},{10... | collective-permute-start | bytes 172040 | tf_op jit(solution)/shard_map/ppermute | solution.py:83
  27.0 0.2 multiply_add_fusion.1
  27.4 0.1 multiply_add_fusion
  27.9 0.1 add_divide_fusion
  28.3 1.7 %collective-permute-start.7 = (f32[7,16,1,256]{3,2,1,0:T(1,128)S(1)}, f32[7,16,1,256]{3,2,1,0:T(1,128)S(1)}, u32[]{:S(2)}, u32[]{:S(2)}) collective-permute-start(f32[7,16,1,256]{3,2,1,0:T(1,128)S(1)} %pad_maximum_fusion.3), channel_id=1, source_target_pairs={{0,1},{1,2},{2,3},{3,4},{4,5},{5,6},{6,7},{7,0},{8,9},{9,10},{10,1... | collective-permute-start | bytes 344072 | tf_op jit(solution)/shard_map/ppermute | solution.py:83
  30.0 2.4 %collective-permute-start.8 = (f32[7,16,1,256]{3,2,1,0:T(1,128)S(1)}, f32[7,16,1,256]{3,2,1,0:T(1,128)S(1)}, u32[]{:S(2)}, u32[]{:S(2)}) collective-permute-start(f32[7,16,1,256]{3,2,1,0:T(1,128)S(1)} %pad_maximum_fusion.3), channel_id=1, source_target_pairs={{0,2},{1,3},{2,4},{3,5},{4,6},{5,7},{6,0},{7,1},{8,10},{9,11},{10,... | collective-permute-start | bytes 344072 | tf_op jit(solution)/shard_map/ppermute | solution.py:83
  32.4 1.8 %collective-permute-start.9 = (f32[7,16,1,256]{3,2,1,0:T(1,128)S(1)}, f32[7,16,1,256]{3,2,1,0:T(1,128)S(1)}, u32[]{:S(2)}, u32[]{:S(2)}) collective-permute-start(f32[7,16,1,256]{3,2,1,0:T(1,128)S(1)} %pad_maximum_fusion.3), channel_id=1, source_target_pairs={{0,3},{1,4},{2,5},{3,6},{4,7},{5,0},{6,1},{7,2},{8,11},{9,12},{10,... | collective-permute-start | bytes 344072 | tf_op jit(solution)/shard_map/ppermute | solution.py:83
  34.2 0.5 collective-permute-start.10
  34.7 0.7 %collective-permute-start.11 = (f32[7,16,1,256]{3,2,1,0:T(1,128)S(1)}, f32[7,16,1,256]{3,2,1,0:T(1,128)S(1)}, u32[]{:S(2)}, u32[]{:S(2)}) collective-permute-start(f32[7,16,1,256]{3,2,1,0:T(1,128)S(1)} %pad_maximum_fusion.3), channel_id=1, source_target_pairs={{0,5},{1,6},{2,7},{3,0},{4,1},{5,2},{6,3},{7,4},{8,13},{9,14},{10,... | collective-permute-start | bytes 344072 | tf_op jit(solution)/shard_map/ppermute | solution.py:83
  35.8 0.1 fusion.40
  36.2 0.1 multiply_add_fusion.11
  36.5 0.2 fusion.38
  37.0 0.1 multiply_add_fusion.10
  37.3 0.2 fusion.36
  37.8 0.1 multiply_add_fusion.9
  38.0 0.2 fusion.34
  38.6 0.1 multiply_add_fusion.8
  38.8 0.2 fusion.32
  39.4 0.1 multiply_add_fusion.7
  39.6 0.2 fusion.30
  40.2 0.1 multiply_add_fusion.6
  40.4 0.2 fusion.28
  40.8 0.2 pad_multiply_fusion
  41.4 0.7 %fusion.24 = f32[16,8,256]{2,1,0:T(8,128)} fusion(f32[16,8,256]{2,1,0:T(8,128)S(1)} %copy-done.4, f32[16,8,256]{2,1,0:T(8,128)S(1)} %copy-done.1, f32[1,8,256]{2,1,0:T(8,128)S(1)} %bitcast.787, f32[15,8,256]{2,1,0:T(8,128)S(1)} %slice.1140, f32[8,256]{1,0:T(8,128)S(1)} %bitcast.786, f32[3,16,8,256]{3,2,1,0:T(8,128)S(1)} %add_divide_fusion.1, ...), kind=kLoop, calls=%fused_computation.50 | loop fusion | flops 262144 | bytes 933888 | tf_op jit(solution)/shard_map/sub | solution.py:237
  42.1 0.7 %add_subtract_fusion = f32[16,8,256]{2,1,0:T(8,128)} fusion(f32[16,8,256]{2,1,0:T(8,128)S(1)} %maximum_subtract_fusion.6, f32[16,8,256]{2,1,0:T(8,128)S(1)} %copy-done.2, f32[16,8,256]{2,1,0:T(8,128)S(1)} %fusion.25, f32[16,8,255]{2,1,0:T(8,128)S(1)} %slice.1139), kind=kLoop, calls=%fused_computation.85 | loop fusion | flops 98304 | bytes 654848 | tf_op jit(solution)/shard_map/sub | solution.py:235
  42.8 1.7 %collective-permute-start.12 = (f32[7,16,1,256]{3,2,1,0:T(1,128)S(1)}, f32[7,16,1,256]{3,2,1,0:T(1,128)S(1)}, u32[]{:S(2)}, u32[]{:S(2)}) collective-permute-start(f32[7,16,1,256]{3,2,1,0:T(1,128)S(1)} %pad_maximum_fusion.3), channel_id=1, source_target_pairs={{0,6},{1,7},{2,0},{3,1},{4,2},{5,3},{6,4},{7,5},{8,14},{9,15},{10,... | collective-permute-start | bytes 344072 | tf_op jit(solution)/shard_map/ppermute | solution.py:83
  44.6 2.4 %collective-permute-start.13 = (f32[7,16,1,256]{3,2,1,0:T(1,128)S(1)}, f32[7,16,1,256]{3,2,1,0:T(1,128)S(1)}, u32[]{:S(2)}, u32[]{:S(2)}) collective-permute-start(f32[7,16,1,256]{3,2,1,0:T(1,128)S(1)} %pad_maximum_fusion.3), channel_id=1, source_target_pairs={{0,7},{1,0},{2,1},{3,2},{4,3},{5,4},{6,5},{7,6},{8,15},{9,8},{10,9... | collective-permute-start | bytes 344072 | tf_op jit(solution)/shard_map/ppermute | solution.py:83
  47.1 1.5 %collective-permute-done.12 = f32[7,16,1,256]{3,2,1,0:T(1,128)S(1)} collective-permute-done((f32[7,16,1,256]{3,2,1,0:T(1,128)S(1)}, f32[7,16,1,256]{3,2,1,0:T(1,128)S(1)}, u32[]{:S(2)}, u32[]{:S(2)}) %collective-permute-start.12) | collective-permute-done | bytes 114720 | tf_op jit(solution)/shard_map/ppermute | solution.py:83
  48.5 0.8 %collective-permute-done.13 = f32[7,16,1,256]{3,2,1,0:T(1,128)S(1)} collective-permute-done((f32[7,16,1,256]{3,2,1,0:T(1,128)S(1)}, f32[7,16,1,256]{3,2,1,0:T(1,128)S(1)}, u32[]{:S(2)}, u32[]{:S(2)}) %collective-permute-start.13) | collective-permute-done | bytes 114720 | tf_op jit(solution)/shard_map/ppermute | solution.py:83
  49.3 0.6 %fusion.120 = (f32[1,16,1,256]{3,2,1,0:T(1,128)S(1)}, f32[1,16,1,256]{3,2,1,0:T(1,128)S(1)}, f32[1,16,1,256]{3,2,1,0:T(1,128)S(1)}, f32[1,16,1,256]{3,2,1,0:T(1,...) fusion(f32[8,7,16,1,256]{4,3,2,1,0:T(1,128)S(1)} %bitcast_dynam, ...), kind=kLoop, calls=%fused_computation.359 | loop fusion | flops 385024 | bytes 1130548 | tf_op jit(solution)/shard_map/mul | solution.py:114
  49.9 0.3 constant_dynamic-update-slice_fusion.7
  50.8 0.6 %copy-done.11 = f32[16,8,256]{2,1,0:T(8,128)} copy-done((f32[16,8,256]{2,1,0:T(8,128)}, f32[16,8,256]{2,1,0:T(8,128)S(1)}, u32[]{:S(2)}) %copy-start.11) | copy-done | bytes 131096
  51.4 0.7 %fusion.22 = f32[16,8,256]{2,1,0:T(8,128)} fusion(f32[16,8,256]{2,1,0:T(8,128)S(1)} %maximum_subtract_fusion.4, f32[16,8,256]{2,1,0:T(8,128)S(1)} %copy-done, f32[16,1,256]{2,1,0:T(1,128)S(1)} %fusion.283, f32[16,7,256]{2,1,0:T(8,128)S(1)} %slice.1138, f32[16,256]{1,0:T(8,128)S(1)} %bitcast.782, f32[3,16,8,256]{3,2,1,0:T(8,128)S(1)} %add_divide_fusion, ...), kind=kLoop, calls=%fused_computation.47 | loop fusion | flops 262144 | bytes 950272 | tf_op jit(solution)/shard_map/sub | solution.py:233
  (193 shorter events, 6.6 us)
Async XLA Ops:
  1.3 1.1 %copy-start.9 = (f32[16,8,256]{2,1,0:T(8,128)S(1)}, f32[16,8,256]{2,1,0:T(8,128)}, u32[]{:S(2)}) copy-start(f32[16,8,256]{2,1,0:T(8,128)} %param.9) | copy-start | bytes 393220
  2.4 0.9 %copy-start.1 = (f32[16,8,256]{2,1,0:T(8,128)S(1)}, f32[16,8,256]{2,1,0:T(8,128)}, u32[]{:S(2)}) copy-start(f32[16,8,256]{2,1,0:T(8,128)} %param.13) | copy-start | bytes 393220
  2.4 6.0 %copy-start.6 = (f32[16,8,256]{2,1,0:T(8,128)S(1)}, f32[16,8,256]{2,1,0:T(8,128)}, u32[]{:S(2)}) copy-start(f32[16,8,256]{2,1,0:T(8,128)} %param.10) | copy-start | bytes 393220
  2.4 7.4 %copy-start.2 = (f32[16,8,256]{2,1,0:T(8,128)S(1)}, f32[16,8,256]{2,1,0:T(8,128)}, u32[]{:S(2)}) copy-start(f32[16,8,256]{2,1,0:T(8,128)} %param.12) | copy-start | bytes 393220
  3.3 9.5 %copy-start.3 = (f32[16,8,256]{2,1,0:T(8,128)}, f32[16,8,256]{2,1,0:T(8,128)S(1)}, u32[]{:S(2)}) copy-start(f32[16,8,256]{2,1,0:T(8,128)S(1)} %pad_subtract_fusion) | copy-start | bytes 393220
  3.3 6.4 %copy-start = (f32[16,8,256]{2,1,0:T(8,128)S(1)}, f32[16,8,256]{2,1,0:T(8,128)}, u32[]{:S(2)}) copy-start(f32[16,8,256]{2,1,0:T(8,128)} %param.11) | copy-start | bytes 393220
  3.3 8.0 %copy-start.8 = (f32[16,8,256]{2,1,0:T(8,128)S(1)}, f32[16,8,256]{2,1,0:T(8,128)}, u32[]{:S(2)}) copy-start(f32[16,8,256]{2,1,0:T(8,128)} %param.8) | copy-start | bytes 393220
  3.3 12.7 %collective-permute-start = (f32[3,1,8,256]{3,2,1,0:T(8,128)S(1)}, f32[3,1,8,256]{3,2,1,0:T(8,128)S(1)}, u32[]{:S(2)}, u32[]{:S(2)}) collective-permute-start(f32[3,1,8,256]{3,2,1,0:T(8,128)S(1)} %pad_maximum_fusion.6), channel_id=1, source_target_pairs={{0,8},{8,16},{16,24},{1,9},{9,17},{17,25},{2,10},{10,18},{18,26},{... | collective-permute-start | bytes 73736 | tf_op jit(solution)/shard_map/ppermute | solution.py:12
  8.4 5.8 %collective-permute-start.1 = (f32[1,8,256]{2,1,0:T(8,128)S(1)}, f32[1,8,256]{2,1,0:T(8,128)S(1)}, u32[]{:S(2)}, u32[]{:S(2)}) collective-permute-start(f32[1,8,256]{2,1,0:T(8,128)S(1)} %slice.777), channel_id=1, source_target_pairs={{8,0},{16,8},{24,16},{9,1},{17,9},{25,17},{10,2},{18,10},{26,18},{... | collective-permute-start | bytes 24584 | tf_op jit(solution)/shard_map/ppermute | solution.py:12
  9.9 6.1 %collective-permute-start.2 = (f32[3,16,1,256]{3,2,1,0:T(1,128)S(1)}, f32[3,16,1,256]{3,2,1,0:T(1,128)S(1)}, u32[]{:S(2)}, u32[]{:S(2)}) collective-permute-start(f32[3,16,1,256]{3,2,1,0:T(1,128)S(1)} %pad_maximum_fusion.5), channel_id=1, source_target_pairs={{0,1},{1,2},{2,3},{3,4},{4,5},{5,6},{6,7},{8,9},{9,10},{10,11},{11... | collective-permute-start | bytes 147464 | tf_op jit(solution)/shard_map/ppermute | solution.py:12
  11.4 4.6 %collective-permute-start.3 = (f32[16,1,256]{2,1,0:T(1,128)S(1)}, f32[16,1,256]{2,1,0:T(1,128)S(1)}, u32[]{:S(2)}, u32[]{:S(2)}) collective-permute-start(f32[16,1,256]{2,1,0:T(1,128)S(1)} %slice.781), channel_id=1, source_target_pairs={{1,0},{2,1},{3,2},{4,3},{5,4},{6,5},{7,6},{9,8},{10,9},{11,10},{12... | collective-permute-start | bytes 49160 | tf_op jit(solution)/shard_map/ppermute | solution.py:12
  12.8 0.9 %copy-start.5 = (f32[16,8,256]{2,1,0:T(8,128)S(1)}, f32[16,8,256]{2,1,0:T(8,128)}, u32[]{:S(2)}) copy-start(f32[16,8,256]{2,1,0:T(8,128)} %param.14) | copy-start | bytes 393220
  12.8 1.0 %copy-start.13 = (f32[16,8,256]{2,1,0:T(8,128)S(1)}, f32[16,8,256]{2,1,0:T(8,128)}, u32[]{:S(2)}) copy-start(f32[16,8,256]{2,1,0:T(8,128)} %param.15) | copy-start | bytes 393220
  14.2 1.9 %copy-start.7 = (f32[16,8,256]{2,1,0:T(8,128)S(1)}, f32[16,8,256]{2,1,0:T(8,128)}, u32[]{:S(2)}) copy-start(f32[16,8,256]{2,1,0:T(8,128)} %param.10) | copy-start | bytes 393220
  14.2 1.9 %slice-start.3 = ((f32[16,8,256]{2,1,0:T(8,128)}), f32[15,8,256]{2,1,0:T(8,128)S(1)}, s32[]{:S(2)}) async-start(f32[16,8,256]{2,1,0:T(8,128)} %param.10), calls=%async_computation.3 | async-start | bytes 245760 | tf_op jit(solution)/shard_map/slice | solution.py:16
  16.1 0.9 %copy-start.4 = (f32[16,8,256]{2,1,0:T(8,128)S(1)}, f32[16,8,256]{2,1,0:T(8,128)}, u32[]{:S(2)}) copy-start(f32[16,8,256]{2,1,0:T(8,128)} %copy-done.3) | copy-start | bytes 393220
  16.1 0.9 %slice-start = ((f32[16,8,256]{2,1,0:T(8,128)}), f32[15,8,256]{2,1,0:T(8,128)S(1)}, s32[]{:S(2)}) async-start(f32[16,8,256]{2,1,0:T(8,128)} %param.11), calls=%async_computation | async-start | bytes 245760 | tf_op jit(solution)/shard_map/slice | solution.py:16
  16.1 1.0 %slice-start.1 = ((f32[16,8,256]{2,1,0:T(8,128)}), f32[15,8,256]{2,1,0:T(8,128)S(1)}, s32[]{:S(2)}) async-start(f32[16,8,256]{2,1,0:T(8,128)} %param.13), calls=%async_computation.1 | async-start | bytes 245760 | tf_op jit(solution)/shard_map/slice | solution.py:16
  16.1 1.0 %slice-start.2 = ((f32[16,8,256]{2,1,0:T(8,128)}), f32[15,8,256]{2,1,0:T(8,128)S(1)}, s32[]{:S(2)}) async-start(f32[16,8,256]{2,1,0:T(8,128)} %copy-done.3), calls=%async_computation.2 | async-start | bytes 245760 | tf_op jit(solution)/shard_map/slice | solution.py:16
  19.2 15.0 %collective-permute-start.5 = (f32[7,1,8,256]{3,2,0,1:T(8,128)S(1)}, f32[7,1,8,256]{3,2,0,1:T(8,128)S(1)}, u32[]{:S(2)}, u32[]{:S(2)}) collective-permute-start(f32[7,1,8,256]{3,2,0,1:T(8,128)S(1)} %get-tuple-element.251), channel_id=1, source_target_pairs={{0,16},{8,24},{16,0},{24,8},{1,17},{9,25},{17,1},{25,9},{2,18},{10... | collective-permute-start | bytes 172040 | tf_op jit(solution)/shard_map/ppermute | solution.py:83
  22.9 11.8 %collective-permute-start.4 = (f32[7,1,8,256]{3,2,0,1:T(8,128)S(1)}, f32[7,1,8,256]{3,2,0,1:T(8,128)S(1)}, u32[]{:S(2)}, u32[]{:S(2)}) collective-permute-start(f32[7,1,8,256]{3,2,0,1:T(8,128)S(1)} %get-tuple-element.251), channel_id=1, source_target_pairs={{0,8},{8,16},{16,24},{24,0},{1,9},{9,17},{17,25},{25,1},{2,10},{10... | collective-permute-start | bytes 172040 | tf_op jit(solution)/shard_map/ppermute | solution.py:83
  24.5 7.9 %collective-permute-start.6 = (f32[7,1,8,256]{3,2,1,0:T(8,128)S(1)}, f32[7,1,8,256]{3,2,1,0:T(8,128)S(1)}, u32[]{:S(2)}, u32[]{:S(2)}) collective-permute-start(f32[7,1,8,256]{3,2,1,0:T(8,128)S(1)} %get-tuple-element.252), channel_id=1, source_target_pairs={{0,24},{8,0},{16,8},{24,16},{1,25},{9,1},{17,9},{25,17},{2,26},{10... | collective-permute-start | bytes 172040 | tf_op jit(solution)/shard_map/ppermute | solution.py:83
  28.3 14.5 %collective-permute-start.7 = (f32[7,16,1,256]{3,2,1,0:T(1,128)S(1)}, f32[7,16,1,256]{3,2,1,0:T(1,128)S(1)}, u32[]{:S(2)}, u32[]{:S(2)}) collective-permute-start(f32[7,16,1,256]{3,2,1,0:T(1,128)S(1)} %pad_maximum_fusion.3), channel_id=1, source_target_pairs={{0,1},{1,2},{2,3},{3,4},{4,5},{5,6},{6,7},{7,0},{8,9},{9,10},{10,1... | collective-permute-start | bytes 344072 | tf_op jit(solution)/shard_map/ppermute | solution.py:83
  30.0 14.6 %collective-permute-start.8 = (f32[7,16,1,256]{3,2,1,0:T(1,128)S(1)}, f32[7,16,1,256]{3,2,1,0:T(1,128)S(1)}, u32[]{:S(2)}, u32[]{:S(2)}) collective-permute-start(f32[7,16,1,256]{3,2,1,0:T(1,128)S(1)} %pad_maximum_fusion.3), channel_id=1, source_target_pairs={{0,2},{1,3},{2,4},{3,5},{4,6},{5,7},{6,0},{7,1},{8,10},{9,11},{10,... | collective-permute-start | bytes 344072 | tf_op jit(solution)/shard_map/ppermute | solution.py:83
  32.4 14.6 %collective-permute-start.9 = (f32[7,16,1,256]{3,2,1,0:T(1,128)S(1)}, f32[7,16,1,256]{3,2,1,0:T(1,128)S(1)}, u32[]{:S(2)}, u32[]{:S(2)}) collective-permute-start(f32[7,16,1,256]{3,2,1,0:T(1,128)S(1)} %pad_maximum_fusion.3), channel_id=1, source_target_pairs={{0,3},{1,4},{2,5},{3,6},{4,7},{5,0},{6,1},{7,2},{8,11},{9,12},{10,... | collective-permute-start | bytes 344072 | tf_op jit(solution)/shard_map/ppermute | solution.py:83
  34.2 12.8 %collective-permute-start.10 = (f32[7,16,1,256]{3,2,1,0:T(1,128)S(1)}, f32[7,16,1,256]{3,2,1,0:T(1,128)S(1)}, u32[]{:S(2)}, u32[]{:S(2)}) collective-permute-start(f32[7,16,1,256]{3,2,1,0:T(1,128)S(1)} %pad_maximum_fusion.3), channel_id=1, source_target_pairs={{0,4},{1,5},{2,6},{3,7},{4,0},{5,1},{6,2},{7,3},{8,12},{9,13},{10,... | collective-permute-start | bytes 344072 | tf_op jit(solution)/shard_map/ppermute | solution.py:83
  34.7 12.4 %collective-permute-start.11 = (f32[7,16,1,256]{3,2,1,0:T(1,128)S(1)}, f32[7,16,1,256]{3,2,1,0:T(1,128)S(1)}, u32[]{:S(2)}, u32[]{:S(2)}) collective-permute-start(f32[7,16,1,256]{3,2,1,0:T(1,128)S(1)} %pad_maximum_fusion.3), channel_id=1, source_target_pairs={{0,5},{1,6},{2,7},{3,0},{4,1},{5,2},{6,3},{7,4},{8,13},{9,14},{10,... | collective-permute-start | bytes 344072 | tf_op jit(solution)/shard_map/ppermute | solution.py:83
  41.2 0.9 %copy-start.10 = (f32[16,8,256]{2,1,0:T(8,128)}, f32[16,8,256]{2,1,0:T(8,128)S(1)}, u32[]{:S(2)}) copy-start(f32[16,8,256]{2,1,0:T(8,128)S(1)} %fusion.25) | copy-start | bytes 393220
  41.4 0.8 %copy-start.12 = (f32[16,8,256]{2,1,0:T(8,128)}, f32[16,8,256]{2,1,0:T(8,128)S(1)}, u32[]{:S(2)}) copy-start(f32[16,8,256]{2,1,0:T(8,128)S(1)} %fusion.5) | copy-start | bytes 393220
  42.8 5.7 %collective-permute-start.12 = (f32[7,16,1,256]{3,2,1,0:T(1,128)S(1)}, f32[7,16,1,256]{3,2,1,0:T(1,128)S(1)}, u32[]{:S(2)}, u32[]{:S(2)}) collective-permute-start(f32[7,16,1,256]{3,2,1,0:T(1,128)S(1)} %pad_maximum_fusion.3), channel_id=1, source_target_pairs={{0,6},{1,7},{2,0},{3,1},{4,2},{5,3},{6,4},{7,5},{8,14},{9,15},{10,... | collective-permute-start | bytes 344072 | tf_op jit(solution)/shard_map/ppermute | solution.py:83
  44.6 4.7 %collective-permute-start.13 = (f32[7,16,1,256]{3,2,1,0:T(1,128)S(1)}, f32[7,16,1,256]{3,2,1,0:T(1,128)S(1)}, u32[]{:S(2)}, u32[]{:S(2)}) collective-permute-start(f32[7,16,1,256]{3,2,1,0:T(1,128)S(1)} %pad_maximum_fusion.3), channel_id=1, source_target_pairs={{0,7},{1,0},{2,1},{3,2},{4,3},{5,4},{6,5},{7,6},{8,15},{9,8},{10,9... | collective-permute-start | bytes 344072 | tf_op jit(solution)/shard_map/ppermute | solution.py:83
  50.7 0.7 %copy-start.11 = (f32[16,8,256]{2,1,0:T(8,128)}, f32[16,8,256]{2,1,0:T(8,128)S(1)}, u32[]{:S(2)}) copy-start(f32[16,8,256]{2,1,0:T(8,128)S(1)} %fusion.1) | copy-start | bytes 393220

commit v6 on v5

--- a/solution.py
+++ b/solution.py
@@ -4,6 +4,7 @@
 from jax.sharding import PartitionSpec as P
 
 step_ratio = 1024.0
+LIMIT = 2
 
 
 def passed_along(value, axis, steps):
@@ -79,11 +80,19 @@
 
 def gathered(values, axis):
     count = lax.axis_size(axis)
-    shifted = [values] + [
-        lax.ppermute(values, axis, [(source, (source + shift) % count) for source in range(count)])
-        for shift in range(1, count)
-    ]
-    return jnp.stack(shifted)
+    direct = count if count <= LIMIT else (count + 1) // 2
+    shifted = jnp.stack(
+        [values]
+        + [
+            lax.ppermute(values, axis, [(source, (source + shift) % count) for source in range(count)])
+            for shift in range(1, direct)
+        ]
+    )
+    while shifted.shape[0] < count:
+        have = shifted.shape[0]
+        moved = lax.ppermute(shifted, axis, [(source, (source + have) % count) for source in range(count)])
+        shifted = jnp.concatenate([shifted, moved])[:count]
+    return shifted
 
 
 def block_spikes(lower_band, main_band, upper_band, right_side, direction):

time: 52.6 us -> 51.8 us (0.985)
  starting transfers between devices: 27.8 us -> 23.1 us
  waiting for transfers between devices: 3.91 us -> 6.93 us
  local copies, waits for them, and re-layouts: 9.01 us -> 9.75 us
    ppermute x10 -> x4, starting transfers between devices: 18.7 us -> 8.54 us  [gathered(): lax.ppermute(values, axis, [(source, (source + shift) % count) for source...]
    ppermute x0 -> x2, starting transfers between devices: none -> 5.47 us  [gathered(): lax.ppermute(shifted, axis, [(source, (source + have) % count) for source...]
    ppermute x0 -> x2, waiting for transfers between devices: none -> 2.15 us  [gathered(): lax.ppermute(shifted, axis, [(source, (source + have) % count) for source...]
    ppermute x10 -> x4, waiting for transfers between devices: 2.24 us -> 3.12 us  [gathered(): lax.ppermute(values, axis, [(source, (source + shift) % count) for source...]
    unnamed x36 -> x33, local copies, waits for them, and re-layouts: 3.33 us -> 3.73 us
  transfers between devices with their start and end apart: 14 -> 10, of which waited for: 3 -> 4; matrix products, arithmetic and copies ran while one was open for 17% -> 18% of each run, Pallas kernels for 0% -> 0%
where the time goes in v6:
time: 51.8 us; the launch traced here: 51.4 us
  starting transfers between devices  23.1 us (45%)
  local copies, waits for them, and re-layouts  9.75 us (19%)
  other arithmetic  9.36 us (18%)
  waiting for transfers between devices  6.93 us (13%)
  between operations  2.29 us (4%)
    ppermute x4, starting transfers between devices, passed_along(): lax.ppermute(value, axis, [(source, source + steps) for source in range(f...  9.11 us
    ppermute x4, starting transfers between devices, gathered(): lax.ppermute(values, axis, [(source, (source + shift) % count) for source...  8.54 us
    ppermute x2, starting transfers between devices, gathered(): lax.ppermute(shifted, axis, [(source, (source + have) % count) for source...  5.47 us
    slice x78, local copies, waits for them, and re-layouts, take_rows(): return lax.slice_in_dim(values, start, start + length, axis=direction)  4.84 us
    unnamed x33, local copies, waits for them, and re-layouts  3.73 us
    ppermute x4, waiting for transfers between devices, gathered(): lax.ppermute(values, axis, [(source, (source + shift) % count) for source...  3.12 us
    ppermute x2, waiting for transfers between devices, gathered(): lax.ppermute(shifted, axis, [(source, (source + have) % count) for source...  2.15 us
    add x12, other arithmetic, reduce_lines(): right_side + ratio_low[None] * low_right + ratio_high[None] * high_right  2.01 us
  transfers between devices with their start and end apart: 10, of which 4 were waited for; matrix products, arithmetic and copies ran while one was open for 18% of the time, Pallas kernels for 0%

profile of v6, /device:TPU:0, one launch (start us, length us, event | category | flops | bytes accessed | tf_op | source)
XLA Modules:
  0.0 51.4 jit_solution(11530903495426235022)
XLA Ops:
  0.6 0.7 %slice_bitcast_fusion.19 = f32[1,1,8,256]{3,2,1,0:T(8,128)S(1)} fusion(f32[16,8,256]{2,1,0:T(8,128)} %param.11), kind=kLoop, calls=%fused_computation.472 | loop fusion | bytes 16384 | tf_op jit(solution)/shard_map/stack | solution.py:179
  1.3 1.1 %slice.774 = f32[16,8,255]{2,1,0:T(8,128)S(1)} slice(f32[16,8,256]{2,1,0:T(8,128)} %param.9), slice={[0:16], [0:8], [1:256]} | slice | bytes 261120 | tf_op jit(solution)/shard_map/slice | solution.py:17
  2.5 0.8 %copy-done.1 = f32[16,8,256]{2,1,0:T(8,128)S(1)} copy-done((f32[16,8,256]{2,1,0:T(8,128)S(1)}, f32[16,8,256]{2,1,0:T(8,128)}, u32[]{:S(2)}) %copy-start.1) | copy-done | bytes 131096
  3.3 5.1 %collective-permute-start = (f32[3,1,8,256]{3,2,1,0:T(8,128)S(1)}, f32[3,1,8,256]{3,2,1,0:T(8,128)S(1)}, u32[]{:S(2)}, u32[]{:S(2)}) collective-permute-start(f32[3,1,8,256]{3,2,1,0:T(8,128)S(1)} %pad_maximum_fusion.8), channel_id=1, source_target_pairs={{0,8},{8,16},{16,24},{1,9},{9,17},{17,25},{2,10},{10,18},{18,26},{... | collective-permute-start | bytes 73736 | tf_op jit(solution)/shard_map/ppermute | solution.py:13
  8.4 1.3 %collective-permute-start.1 = (f32[1,8,256]{2,1,0:T(8,128)S(1)}, f32[1,8,256]{2,1,0:T(8,128)S(1)}, u32[]{:S(2)}, u32[]{:S(2)}) collective-permute-start(f32[1,8,256]{2,1,0:T(8,128)S(1)} %slice.777), channel_id=1, source_target_pairs={{8,0},{16,8},{24,16},{9,1},{17,9},{25,17},{10,2},{18,10},{26,18},{... | collective-permute-start | bytes 24584 | tf_op jit(solution)/shard_map/ppermute | solution.py:13
  9.9 1.5 %collective-permute-start.2 = (f32[3,16,1,256]{3,2,1,0:T(1,128)S(1)}, f32[3,16,1,256]{3,2,1,0:T(1,128)S(1)}, u32[]{:S(2)}, u32[]{:S(2)}) collective-permute-start(f32[3,16,1,256]{3,2,1,0:T(1,128)S(1)} %pad_maximum_fusion.7), channel_id=1, source_target_pairs={{0,1},{1,2},{2,3},{3,4},{4,5},{5,6},{6,7},{8,9},{9,10},{10,11},{11... | collective-permute-start | bytes 147464 | tf_op jit(solution)/shard_map/ppermute | solution.py:13
  11.4 1.3 %collective-permute-start.3 = (f32[16,1,256]{2,1,0:T(1,128)S(1)}, f32[16,1,256]{2,1,0:T(1,128)S(1)}, u32[]{:S(2)}, u32[]{:S(2)}) collective-permute-start(f32[16,1,256]{2,1,0:T(1,128)S(1)} %slice.781), channel_id=1, source_target_pairs={{1,0},{2,1},{3,2},{4,3},{5,4},{6,5},{7,6},{9,8},{10,9},{11,10},{12... | collective-permute-start | bytes 49160 | tf_op jit(solution)/shard_map/ppermute | solution.py:13
  12.9 0.8 %copy-done.5 = f32[16,8,256]{2,1,0:T(8,128)S(1)} copy-done((f32[16,8,256]{2,1,0:T(8,128)S(1)}, f32[16,8,256]{2,1,0:T(8,128)}, u32[]{:S(2)}) %copy-start.5) | copy-done | bytes 131096
  14.4 1.7 %collective-permute-done.3 = f32[16,1,256]{2,1,0:T(1,128)S(1)} collective-permute-done((f32[16,1,256]{2,1,0:T(1,128)S(1)}, f32[16,1,256]{2,1,0:T(1,128)S(1)}, u32[]{:S(2)}, u32[]{:S(2)}) %collective-permute-start.3) | collective-permute-done | bytes 16416 | tf_op jit(solution)/shard_map/ppermute | solution.py:13
  16.2 0.8 %copy-done.4 = f32[16,8,256]{2,1,0:T(8,128)S(1)} copy-done((f32[16,8,256]{2,1,0:T(8,128)S(1)}, f32[16,8,256]{2,1,0:T(8,128)}, u32[]{:S(2)}) %copy-start.4) | copy-done | bytes 131096
  17.2 0.2 fusion.20
  17.4 0.3 select_select_fusion.1
  18.0 0.1 multiply_add_fusion.4
  19.1 2.7 %collective-permute-start.4 = (f32[7,1,8,256]{3,2,1,0:T(8,128)S(1)}, f32[7,1,8,256]{3,2,1,0:T(8,128)S(1)}, u32[]{:S(2)}, u32[]{:S(2)}) collective-permute-start(f32[7,1,8,256]{3,2,1,0:T(8,128)S(1)} %get-tuple-element.253), channel_id=1, source_target_pairs={{0,8},{8,16},{16,24},{24,0},{1,9},{9,17},{17,25},{25,1},{2,10},{10... | collective-permute-start | bytes 172040 | tf_op jit(solution)/shard_map/ppermute | solution.py:87
  22.1 0.1 multiply_add_fusion.1
  22.9 0.1 add_divide_fusion
  23.1 0.2 constant_dynamic-update-slice_fusion.4
  23.3 2.2 %collective-permute-start.6 = (f32[7,16,1,256]{3,2,1,0:T(1,128)S(1)}, f32[7,16,1,256]{3,2,1,0:T(1,128)S(1)}, u32[]{:S(2)}, u32[]{:S(2)}) collective-permute-start(f32[7,16,1,256]{3,2,1,0:T(1,128)S(1)} %get-tuple-element.75), channel_id=1, source_target_pairs={{0,1},{1,2},{2,3},{3,4},{4,5},{5,6},{6,7},{7,0},{8,9},{9,10},{10,1... | collective-permute-start | bytes 344072 | tf_op jit(solution)/shard_map/ppermute | solution.py:87
  25.6 2.4 %collective-permute-start.7 = (f32[7,16,1,256]{3,2,1,0:T(1,128)S(1)}, f32[7,16,1,256]{3,2,1,0:T(1,128)S(1)}, u32[]{:S(2)}, u32[]{:S(2)}) collective-permute-start(f32[7,16,1,256]{3,2,1,0:T(1,128)S(1)} %get-tuple-element.75), channel_id=1, source_target_pairs={{0,2},{1,3},{2,4},{3,5},{4,6},{5,7},{6,0},{7,1},{8,10},{9,11},{10,... | collective-permute-start | bytes 344072 | tf_op jit(solution)/shard_map/ppermute | solution.py:87
  28.0 1.2 %collective-permute-start.8 = (f32[7,16,1,256]{3,2,1,0:T(1,128)S(1)}, f32[7,16,1,256]{3,2,1,0:T(1,128)S(1)}, u32[]{:S(2)}, u32[]{:S(2)}) collective-permute-start(f32[7,16,1,256]{3,2,1,0:T(1,128)S(1)} %get-tuple-element.75), channel_id=1, source_target_pairs={{0,3},{1,4},{2,5},{3,6},{4,7},{5,0},{6,1},{7,2},{8,11},{9,12},{10,... | collective-permute-start | bytes 344072 | tf_op jit(solution)/shard_map/ppermute | solution.py:87
  29.2 2.7 %collective-permute-start.5 = (f32[2,7,1,8,256]{4,3,1,2,0:T(8,128)S(1)}, f32[2,7,1,8,256]{4,3,1,2,0:T(8,128)S(1)}, u32[]{:S(2)}, u32[]{:S(2)}) collective-permute-start(f32[2,7,1,8,256]{4,3,1,2,0:T(8,128)S(1)} %pad_maximum_fusion.4), channel_id=1, source_target_pairs={{0,16},{8,24},{16,0},{24,8},{1,17},{9,25},{17,1},{25,9},{2,18},{10... | collective-permute-start | bytes 344072 | tf_op jit(solution)/shard_map/ppermute | solution.py:93
  31.9 0.4 collective-permute-done.7
  32.3 2.7 %collective-permute-done.8 = f32[7,16,1,256]{3,2,1,0:T(1,128)S(1)} collective-permute-done((f32[7,16,1,256]{3,2,1,0:T(1,128)S(1)}, f32[7,16,1,256]{3,2,1,0:T(1,128)S(1)}, u32[]{:S(2)}, u32[]{:S(2)}) %collective-permute-start.8) | collective-permute-done | bytes 114720 | tf_op jit(solution)/shard_map/ppermute | solution.py:87
  35.0 0.4 pad_maximum_fusion
  35.4 2.8 %collective-permute-start.9 = (f32[4,7,16,1,256]{4,3,2,1,0:T(1,128)S(1)}, f32[4,7,16,1,256]{4,3,2,1,0:T(1,128)S(1)}, u32[]{:S(2)}, u32[]{:S(2)}) collective-permute-start(f32[4,7,16,1,256]{4,3,2,1,0:T(1,128)S(1)} %pad_maximum_fusion), channel_id=1, source_target_pairs={{0,4},{1,5},{2,6},{3,7},{4,0},{5,1},{6,2},{7,3},{8,12},{9,13},{10,... | collective-permute-start | bytes 1376264 | tf_op jit(solution)/shard_map/ppermute | solution.py:93
  38.7 0.1 fusion.40
  39.1 0.1 multiply_add_fusion.11
  39.4 0.2 fusion.38
  39.9 0.1 multiply_add_fusion.10
  40.2 0.2 fusion.36
  40.7 0.1 multiply_add_fusion.9
  40.9 0.2 fusion.34
  41.5 0.1 multiply_add_fusion.8
  41.7 0.2 fusion.32
  42.3 0.1 multiply_add_fusion.7
  42.5 0.2 fusion.30
  43.0 0.1 multiply_add_fusion.6
  43.3 0.2 fusion.28
  43.7 0.2 pad_multiply_fusion
  44.3 0.5 copy-done.10
  44.7 0.7 %add_subtract_fusion = f32[16,8,256]{2,1,0:T(8,128)} fusion(f32[16,8,256]{2,1,0:T(8,128)S(1)} %maximum_subtract_fusion.6, f32[16,8,256]{2,1,0:T(8,128)S(1)} %copy-done.2, f32[16,8,256]{2,1,0:T(8,128)S(1)} %fusion.25, f32[16,8,255]{2,1,0:T(8,128)S(1)} %slice.1139), kind=kLoop, calls=%fused_computation.86 | loop fusion | flops 98304 | bytes 654848 | tf_op jit(solution)/shard_map/sub | solution.py:244
  45.4 0.7 %fusion.24 = f32[16,8,256]{2,1,0:T(8,128)} fusion(f32[16,8,256]{2,1,0:T(8,128)S(1)} %copy-done.4, f32[16,8,256]{2,1,0:T(8,128)S(1)} %copy-done.1, f32[1,8,256]{2,1,0:T(8,128)S(1)} %bitcast.781, f32[15,8,256]{2,1,0:T(8,128)S(1)} %slice.1140, f32[8,256]{1,0:T(8,128)S(1)} %bitcast.780, f32[3,16,8,256]{3,2,1,0:T(8,128)S(1)} %add_divide_fusion.1, ...), kind=kLoop, calls=%fused_computation.51 | loop fusion | flops 262144 | bytes 933888 | tf_op jit(solution)/shard_map/sub | solution.py:246
  46.1 2.1 %collective-permute-done.9 = f32[4,7,16,1,256]{4,3,2,1,0:T(1,128)S(1)} collective-permute-done((f32[4,7,16,1,256]{4,3,2,1,0:T(1,128)S(1)}, f32[4,7,16,1,256]{4,3,2,1,0:T(1,128)S(1)}, u32[]{:S(2)}, u32[]{:S(2)}) %collective-permute-start.9) | collective-permute-done | bytes 458784 | tf_op jit(solution)/shard_map/ppermute | solution.py:93
  48.3 0.3 constant_dynamic-update-slice_fusion
  48.6 0.6 %fusion.120 = (f32[1,16,1,256]{3,2,1,0:T(1,128)S(1)}, f32[1,16,1,256]{3,2,1,0:T(1,128)S(1)}, f32[1,16,1,256]{3,2,1,0:T(1,128)S(1)}, f32[1,16,1,256]{3,2,1,0:T(1,...) fusion(f32[8,7,16,1,256]{4,3,2,1,0:T(1,128)S(1)} %constant_dyna, ...), kind=kLoop, calls=%fused_computation.358 | loop fusion | flops 385024 | bytes 1130548 | tf_op jit(solution)/shard_map/mul | solution.py:123
  49.3 0.3 constant_dynamic-update-slice_fusion.12
  50.1 0.6 %copy-done.11 = f32[16,8,256]{2,1,0:T(8,128)} copy-done((f32[16,8,256]{2,1,0:T(8,128)}, f32[16,8,256]{2,1,0:T(8,128)S(1)}, u32[]{:S(2)}) %copy-start.11) | copy-done | bytes 131096
  50.7 0.7 %fusion.22 = f32[16,8,256]{2,1,0:T(8,128)} fusion(f32[16,8,256]{2,1,0:T(8,128)S(1)} %maximum_subtract_fusion.4, f32[16,8,256]{2,1,0:T(8,128)S(1)} %copy-done, f32[16,1,256]{2,1,0:T(1,128)S(1)} %fusion.282, f32[16,7,256]{2,1,0:T(8,128)S(1)} %slice.1138, f32[16,256]{1,0:T(8,128)S(1)} %bitcast.776, f32[3,16,8,256]{3,2,1,0:T(8,128)S(1)} %add_divide_fusion, ...), kind=kLoop, calls=%fused_computation.48 | loop fusion | flops 262144 | bytes 950272 | tf_op jit(solution)/shard_map/sub | solution.py:242
  (183 shorter events, 6.3 us)
Async XLA Ops:
  1.3 1.1 %copy-start.9 = (f32[16,8,256]{2,1,0:T(8,128)S(1)}, f32[16,8,256]{2,1,0:T(8,128)}, u32[]{:S(2)}) copy-start(f32[16,8,256]{2,1,0:T(8,128)} %param.9) | copy-start | bytes 393220
  2.4 0.9 %copy-start.1 = (f32[16,8,256]{2,1,0:T(8,128)S(1)}, f32[16,8,256]{2,1,0:T(8,128)}, u32[]{:S(2)}) copy-start(f32[16,8,256]{2,1,0:T(8,128)} %param.13) | copy-start | bytes 393220
  2.4 6.0 %copy-start.6 = (f32[16,8,256]{2,1,0:T(8,128)S(1)}, f32[16,8,256]{2,1,0:T(8,128)}, u32[]{:S(2)}) copy-start(f32[16,8,256]{2,1,0:T(8,128)} %param.10) | copy-start | bytes 393220
  2.4 7.4 %copy-start.2 = (f32[16,8,256]{2,1,0:T(8,128)S(1)}, f32[16,8,256]{2,1,0:T(8,128)}, u32[]{:S(2)}) copy-start(f32[16,8,256]{2,1,0:T(8,128)} %param.12) | copy-start | bytes 393220
  3.3 9.5 %copy-start.3 = (f32[16,8,256]{2,1,0:T(8,128)}, f32[16,8,256]{2,1,0:T(8,128)S(1)}, u32[]{:S(2)}) copy-start(f32[16,8,256]{2,1,0:T(8,128)S(1)} %pad_subtract_fusion) | copy-start | bytes 393220
  3.3 6.4 %copy-start = (f32[16,8,256]{2,1,0:T(8,128)S(1)}, f32[16,8,256]{2,1,0:T(8,128)}, u32[]{:S(2)}) copy-start(f32[16,8,256]{2,1,0:T(8,128)} %param.11) | copy-start | bytes 393220
  3.3 8.0 %copy-start.8 = (f32[16,8,256]{2,1,0:T(8,128)S(1)}, f32[16,8,256]{2,1,0:T(8,128)}, u32[]{:S(2)}) copy-start(f32[16,8,256]{2,1,0:T(8,128)} %param.8) | copy-start | bytes 393220
  3.3 12.7 %collective-permute-start = (f32[3,1,8,256]{3,2,1,0:T(8,128)S(1)}, f32[3,1,8,256]{3,2,1,0:T(8,128)S(1)}, u32[]{:S(2)}, u32[]{:S(2)}) collective-permute-start(f32[3,1,8,256]{3,2,1,0:T(8,128)S(1)} %pad_maximum_fusion.8), channel_id=1, source_target_pairs={{0,8},{8,16},{16,24},{1,9},{9,17},{17,25},{2,10},{10,18},{18,26},{... | collective-permute-start | bytes 73736 | tf_op jit(solution)/shard_map/ppermute | solution.py:13
  8.4 5.8 %collective-permute-start.1 = (f32[1,8,256]{2,1,0:T(8,128)S(1)}, f32[1,8,256]{2,1,0:T(8,128)S(1)}, u32[]{:S(2)}, u32[]{:S(2)}) collective-permute-start(f32[1,8,256]{2,1,0:T(8,128)S(1)} %slice.777), channel_id=1, source_target_pairs={{8,0},{16,8},{24,16},{9,1},{17,9},{25,17},{10,2},{18,10},{26,18},{... | collective-permute-start | bytes 24584 | tf_op jit(solution)/shard_map/ppermute | solution.py:13
  9.9 6.1 %collective-permute-start.2 = (f32[3,16,1,256]{3,2,1,0:T(1,128)S(1)}, f32[3,16,1,256]{3,2,1,0:T(1,128)S(1)}, u32[]{:S(2)}, u32[]{:S(2)}) collective-permute-start(f32[3,16,1,256]{3,2,1,0:T(1,128)S(1)} %pad_maximum_fusion.7), channel_id=1, source_target_pairs={{0,1},{1,2},{2,3},{3,4},{4,5},{5,6},{6,7},{8,9},{9,10},{10,11},{11... | collective-permute-start | bytes 147464 | tf_op jit(solution)/shard_map/ppermute | solution.py:13
  11.4 4.6 %collective-permute-start.3 = (f32[16,1,256]{2,1,0:T(1,128)S(1)}, f32[16,1,256]{2,1,0:T(1,128)S(1)}, u32[]{:S(2)}, u32[]{:S(2)}) collective-permute-start(f32[16,1,256]{2,1,0:T(1,128)S(1)} %slice.781), channel_id=1, source_target_pairs={{1,0},{2,1},{3,2},{4,3},{5,4},{6,5},{7,6},{9,8},{10,9},{11,10},{12... | collective-permute-start | bytes 49160 | tf_op jit(solution)/shard_map/ppermute | solution.py:13
  12.8 0.9 %copy-start.5 = (f32[16,8,256]{2,1,0:T(8,128)S(1)}, f32[16,8,256]{2,1,0:T(8,128)}, u32[]{:S(2)}) copy-start(f32[16,8,256]{2,1,0:T(8,128)} %param.14) | copy-start | bytes 393220
  12.8 1.0 %copy-start.13 = (f32[16,8,256]{2,1,0:T(8,128)S(1)}, f32[16,8,256]{2,1,0:T(8,128)}, u32[]{:S(2)}) copy-start(f32[16,8,256]{2,1,0:T(8,128)} %param.15) | copy-start | bytes 393220
  14.2 1.9 %copy-start.7 = (f32[16,8,256]{2,1,0:T(8,128)S(1)}, f32[16,8,256]{2,1,0:T(8,128)}, u32[]{:S(2)}) copy-start(f32[16,8,256]{2,1,0:T(8,128)} %param.10) | copy-start | bytes 393220
  14.2 1.9 %slice-start.3 = ((f32[16,8,256]{2,1,0:T(8,128)}), f32[15,8,256]{2,1,0:T(8,128)S(1)}, s32[]{:S(2)}) async-start(f32[16,8,256]{2,1,0:T(8,128)} %param.10), calls=%async_computation.3 | async-start | bytes 245760 | tf_op jit(solution)/shard_map/slice | solution.py:17
  16.1 0.9 %copy-start.4 = (f32[16,8,256]{2,1,0:T(8,128)S(1)}, f32[16,8,256]{2,1,0:T(8,128)}, u32[]{:S(2)}) copy-start(f32[16,8,256]{2,1,0:T(8,128)} %copy-done.3) | copy-start | bytes 393220
  16.1 0.9 %slice-start = ((f32[16,8,256]{2,1,0:T(8,128)}), f32[15,8,256]{2,1,0:T(8,128)S(1)}, s32[]{:S(2)}) async-start(f32[16,8,256]{2,1,0:T(8,128)} %param.11), calls=%async_computation | async-start | bytes 245760 | tf_op jit(solution)/shard_map/slice | solution.py:17
  16.1 1.0 %slice-start.1 = ((f32[16,8,256]{2,1,0:T(8,128)}), f32[15,8,256]{2,1,0:T(8,128)S(1)}, s32[]{:S(2)}) async-start(f32[16,8,256]{2,1,0:T(8,128)} %param.13), calls=%async_computation.1 | async-start | bytes 245760 | tf_op jit(solution)/shard_map/slice | solution.py:17
  16.1 1.0 %slice-start.2 = ((f32[16,8,256]{2,1,0:T(8,128)}), f32[15,8,256]{2,1,0:T(8,128)S(1)}, s32[]{:S(2)}) async-start(f32[16,8,256]{2,1,0:T(8,128)} %copy-done.3), calls=%async_computation.2 | async-start | bytes 245760 | tf_op jit(solution)/shard_map/slice | solution.py:17
  19.1 10.1 %collective-permute-start.4 = (f32[7,1,8,256]{3,2,1,0:T(8,128)S(1)}, f32[7,1,8,256]{3,2,1,0:T(8,128)S(1)}, u32[]{:S(2)}, u32[]{:S(2)}) collective-permute-start(f32[7,1,8,256]{3,2,1,0:T(8,128)S(1)} %get-tuple-element.253), channel_id=1, source_target_pairs={{0,8},{8,16},{16,24},{24,0},{1,9},{9,17},{17,25},{25,1},{2,10},{10... | collective-permute-start | bytes 172040 | tf_op jit(solution)/shard_map/ppermute | solution.py:87
  23.3 8.5 %collective-permute-start.6 = (f32[7,16,1,256]{3,2,1,0:T(1,128)S(1)}, f32[7,16,1,256]{3,2,1,0:T(1,128)S(1)}, u32[]{:S(2)}, u32[]{:S(2)}) collective-permute-start(f32[7,16,1,256]{3,2,1,0:T(1,128)S(1)} %get-tuple-element.75), channel_id=1, source_target_pairs={{0,1},{1,2},{2,3},{3,4},{4,5},{5,6},{6,7},{7,0},{8,9},{9,10},{10,1... | collective-permute-start | bytes 344072 | tf_op jit(solution)/shard_map/ppermute | solution.py:87
  25.6 6.7 %collective-permute-start.7 = (f32[7,16,1,256]{3,2,1,0:T(1,128)S(1)}, f32[7,16,1,256]{3,2,1,0:T(1,128)S(1)}, u32[]{:S(2)}, u32[]{:S(2)}) collective-permute-start(f32[7,16,1,256]{3,2,1,0:T(1,128)S(1)} %get-tuple-element.75), channel_id=1, source_target_pairs={{0,2},{1,3},{2,4},{3,5},{4,6},{5,7},{6,0},{7,1},{8,10},{9,11},{10,... | collective-permute-start | bytes 344072 | tf_op jit(solution)/shard_map/ppermute | solution.py:87
  28.0 7.0 %collective-permute-start.8 = (f32[7,16,1,256]{3,2,1,0:T(1,128)S(1)}, f32[7,16,1,256]{3,2,1,0:T(1,128)S(1)}, u32[]{:S(2)}, u32[]{:S(2)}) collective-permute-start(f32[7,16,1,256]{3,2,1,0:T(1,128)S(1)} %get-tuple-element.75), channel_id=1, source_target_pairs={{0,3},{1,4},{2,5},{3,6},{4,7},{5,0},{6,1},{7,2},{8,11},{9,12},{10,... | collective-permute-start | bytes 344072 | tf_op jit(solution)/shard_map/ppermute | solution.py:87
  29.2 9.1 %collective-permute-start.5 = (f32[2,7,1,8,256]{4,3,1,2,0:T(8,128)S(1)}, f32[2,7,1,8,256]{4,3,1,2,0:T(8,128)S(1)}, u32[]{:S(2)}, u32[]{:S(2)}) collective-permute-start(f32[2,7,1,8,256]{4,3,1,2,0:T(8,128)S(1)} %pad_maximum_fusion.4), channel_id=1, source_target_pairs={{0,16},{8,24},{16,0},{24,8},{1,17},{9,25},{17,1},{25,9},{2,18},{10... | collective-permute-start | bytes 344072 | tf_op jit(solution)/shard_map/ppermute | solution.py:93
  35.4 12.9 %collective-permute-start.9 = (f32[4,7,16,1,256]{4,3,2,1,0:T(1,128)S(1)}, f32[4,7,16,1,256]{4,3,2,1,0:T(1,128)S(1)}, u32[]{:S(2)}, u32[]{:S(2)}) collective-permute-start(f32[4,7,16,1,256]{4,3,2,1,0:T(1,128)S(1)} %pad_maximum_fusion), channel_id=1, source_target_pairs={{0,4},{1,5},{2,6},{3,7},{4,0},{5,1},{6,2},{7,3},{8,12},{9,13},{10,... | collective-permute-start | bytes 1376264 | tf_op jit(solution)/shard_map/ppermute | solution.py:93
  44.1 0.7 %copy-start.10 = (f32[16,8,256]{2,1,0:T(8,128)}, f32[16,8,256]{2,1,0:T(8,128)S(1)}, u32[]{:S(2)}) copy-start(f32[16,8,256]{2,1,0:T(8,128)S(1)} %fusion.25) | copy-start | bytes 393220
  44.2 1.2 %copy-start.12 = (f32[16,8,256]{2,1,0:T(8,128)}, f32[16,8,256]{2,1,0:T(8,128)S(1)}, u32[]{:S(2)}) copy-start(f32[16,8,256]{2,1,0:T(8,128)S(1)} %fusion.5) | copy-start | bytes 393220
  50.0 0.7 %copy-start.11 = (f32[16,8,256]{2,1,0:T(8,128)}, f32[16,8,256]{2,1,0:T(8,128)S(1)}, u32[]{:S(2)}) copy-start(f32[16,8,256]{2,1,0:T(8,128)S(1)} %fusion.1) | copy-start | bytes 393220

commit v7 on v6

--- a/solution.py
+++ b/solution.py
@@ -4,6 +4,7 @@
 from jax.sharding import PartitionSpec as P
 
 step_ratio = 1024.0
+DIRECT = {8: 5}
 LIMIT = 2
 
 
@@ -80,7 +81,7 @@
 
 def gathered(values, axis):
     count = lax.axis_size(axis)
-    direct = count if count <= LIMIT else (count + 1) // 2
+    direct = count if count <= LIMIT else DIRECT.get(count, (count + 1) // 2)
     shifted = jnp.stack(
         [values]
         + [
@@ -90,8 +91,10 @@
     )
     while shifted.shape[0] < count:
         have = shifted.shape[0]
-        moved = lax.ppermute(shifted, axis, [(source, (source + have) % count) for source in range(count)])
-        shifted = jnp.concatenate([shifted, moved])[:count]
+        moved = lax.ppermute(
+            shifted[: count - have], axis, [(source, (source + have) % count) for source in range(count)]
+        )
+        shifted = jnp.concatenate([shifted, moved])
     return shifted
 
 

time: 51.8 us -> 49.7 us (0.959)
  waiting for transfers between devices: 6.93 us -> 4.13 us
  starting transfers between devices: 23.1 us -> 23.9 us
    ppermute x4 -> x5, waiting for transfers between devices: 3.12 us -> 0.7 us  [gathered(): lax.ppermute(values, axis, [(source, (source + shift) % count) for source...]
    ppermute x4 -> x5, starting transfers between devices: 8.54 us -> 9.04 us  [gathered(): lax.ppermute(values, axis, [(source, (source + shift) % count) for source...]
    unnamed x33 -> x34, local copies, waits for them, and re-layouts: 3.73 us -> 3.84 us
  transfers between devices with their start and end apart: 10 -> 11, of which waited for: 4 -> 4; matrix products, arithmetic and copies ran while one was open for 18% -> 19% of each run, Pallas kernels for 0% -> 0%
where the time goes in v7:
time: 49.7 us; the launch traced here: 49.4 us
  starting transfers between devices  23.9 us (48%)
  local copies, waits for them, and re-layouts  9.76 us (20%)
  other arithmetic  9.38 us (19%)
  waiting for transfers between devices  4.13 us (8%)
  between operations  2.22 us (4%)
    ppermute x4, starting transfers between devices, passed_along(): lax.ppermute(value, axis, [(source, source + steps) for source in range(f...  9.11 us
    ppermute x5, starting transfers between devices, gathered(): lax.ppermute(values, axis, [(source, (source + shift) % count) for source...  9.04 us
    ppermute x2, starting transfers between devices, gathered(): lax.ppermute(shifted[:count - have], axis, [(source, (source + have) % co...  5.77 us
    slice x78, local copies, waits for them, and re-layouts, take_rows(): return lax.slice_in_dim(values, start, start + length, axis=direction)  4.83 us
    unnamed x34, local copies, waits for them, and re-layouts  3.84 us
    add x12, other arithmetic, reduce_lines(): right_side + ratio_low[None] * low_right + ratio_high[None] * high_right  2.13 us
    ppermute x2, waiting for transfers between devices, gathered(): lax.ppermute(shifted[:count - have], axis, [(source, (source + have) % co...  1.77 us
    ppermute x4, waiting for transfers between devices, passed_along(): lax.ppermute(value, axis, [(source, source + steps) for source in range(f...  1.67 us
  transfers between devices with their start and end apart: 11, of which 4 were waited for; matrix products, arithmetic and copies ran while one was open for 19% of the time, Pallas kernels for 0%

profile of v7, /device:TPU:0, one launch (start us, length us, event | category | flops | bytes accessed | tf_op | source)
XLA Modules:
  0.0 49.4 jit_solution(18235320732391667942)
XLA Ops:
  0.6 0.7 %slice_bitcast_fusion.19 = f32[1,1,8,256]{3,2,1,0:T(8,128)S(1)} fusion(f32[16,8,256]{2,1,0:T(8,128)} %param.11), kind=kLoop, calls=%fused_computation.473 | loop fusion | bytes 16384 | tf_op jit(solution)/shard_map/stack | solution.py:182
  1.3 1.1 %slice.776 = f32[16,8,255]{2,1,0:T(8,128)S(1)} slice(f32[16,8,256]{2,1,0:T(8,128)} %param.9), slice={[0:16], [0:8], [1:256]} | slice | bytes 261120 | tf_op jit(solution)/shard_map/slice | solution.py:18
  2.5 0.8 %copy-done.1 = f32[16,8,256]{2,1,0:T(8,128)S(1)} copy-done((f32[16,8,256]{2,1,0:T(8,128)S(1)}, f32[16,8,256]{2,1,0:T(8,128)}, u32[]{:S(2)}) %copy-start.1) | copy-done | bytes 131096
  3.3 5.1 %collective-permute-start = (f32[3,1,8,256]{3,2,1,0:T(8,128)S(1)}, f32[3,1,8,256]{3,2,1,0:T(8,128)S(1)}, u32[]{:S(2)}, u32[]{:S(2)}) collective-permute-start(f32[3,1,8,256]{3,2,1,0:T(8,128)S(1)} %pad_maximum_fusion.8), channel_id=1, source_target_pairs={{0,8},{8,16},{16,24},{1,9},{9,17},{17,25},{2,10},{10,18},{18,26},{... | collective-permute-start | bytes 73736 | tf_op jit(solution)/shard_map/ppermute | solution.py:14
  8.4 1.3 %collective-permute-start.1 = (f32[1,8,256]{2,1,0:T(8,128)S(1)}, f32[1,8,256]{2,1,0:T(8,128)S(1)}, u32[]{:S(2)}, u32[]{:S(2)}) collective-permute-start(f32[1,8,256]{2,1,0:T(8,128)S(1)} %slice.779), channel_id=1, source_target_pairs={{8,0},{16,8},{24,16},{9,1},{17,9},{25,17},{10,2},{18,10},{26,18},{... | collective-permute-start | bytes 24584 | tf_op jit(solution)/shard_map/ppermute | solution.py:14
  9.9 1.5 %collective-permute-start.2 = (f32[3,16,1,256]{3,2,1,0:T(1,128)S(1)}, f32[3,16,1,256]{3,2,1,0:T(1,128)S(1)}, u32[]{:S(2)}, u32[]{:S(2)}) collective-permute-start(f32[3,16,1,256]{3,2,1,0:T(1,128)S(1)} %pad_maximum_fusion.7), channel_id=1, source_target_pairs={{0,1},{1,2},{2,3},{3,4},{4,5},{5,6},{6,7},{8,9},{9,10},{10,11},{11... | collective-permute-start | bytes 147464 | tf_op jit(solution)/shard_map/ppermute | solution.py:14
  11.4 1.3 %collective-permute-start.3 = (f32[16,1,256]{2,1,0:T(1,128)S(1)}, f32[16,1,256]{2,1,0:T(1,128)S(1)}, u32[]{:S(2)}, u32[]{:S(2)}) collective-permute-start(f32[16,1,256]{2,1,0:T(1,128)S(1)} %slice.783), channel_id=1, source_target_pairs={{1,0},{2,1},{3,2},{4,3},{5,4},{6,5},{7,6},{9,8},{10,9},{11,10},{12... | collective-permute-start | bytes 49160 | tf_op jit(solution)/shard_map/ppermute | solution.py:14
  12.9 0.8 %copy-done.5 = f32[16,8,256]{2,1,0:T(8,128)S(1)} copy-done((f32[16,8,256]{2,1,0:T(8,128)S(1)}, f32[16,8,256]{2,1,0:T(8,128)}, u32[]{:S(2)}) %copy-start.5) | copy-done | bytes 131096
  14.4 1.7 %collective-permute-done.3 = f32[16,1,256]{2,1,0:T(1,128)S(1)} collective-permute-done((f32[16,1,256]{2,1,0:T(1,128)S(1)}, f32[16,1,256]{2,1,0:T(1,128)S(1)}, u32[]{:S(2)}, u32[]{:S(2)}) %collective-permute-start.3) | collective-permute-done | bytes 16416 | tf_op jit(solution)/shard_map/ppermute | solution.py:14
  16.2 0.8 %copy-done.4 = f32[16,8,256]{2,1,0:T(8,128)S(1)} copy-done((f32[16,8,256]{2,1,0:T(8,128)S(1)}, f32[16,8,256]{2,1,0:T(8,128)}, u32[]{:S(2)}) %copy-start.4) | copy-done | bytes 131096
  17.2 0.2 fusion.20
  17.4 0.3 select_select_fusion.1
  18.0 0.1 multiply_add_fusion.4
  19.2 2.7 %collective-permute-start.4 = (f32[7,1,8,256]{3,2,1,0:T(8,128)S(1)}, f32[7,1,8,256]{3,2,1,0:T(8,128)S(1)}, u32[]{:S(2)}, u32[]{:S(2)}) collective-permute-start(f32[7,1,8,256]{3,2,1,0:T(8,128)S(1)} %get-tuple-element.253), channel_id=1, source_target_pairs={{0,8},{8,16},{16,24},{24,0},{1,9},{9,17},{17,25},{25,1},{2,10},{10... | collective-permute-start | bytes 172040 | tf_op jit(solution)/shard_map/ppermute | solution.py:88
  22.1 0.2 multiply_add_fusion.1
  22.6 0.1 multiply_add_fusion
  23.2 0.1 constant_dynamic-update-slice_fusion.3
  23.4 2.2 %collective-permute-start.6 = (f32[7,16,1,256]{3,2,1,0:T(1,128)S(1)}, f32[7,16,1,256]{3,2,1,0:T(1,128)S(1)}, u32[]{:S(2)}, u32[]{:S(2)}) collective-permute-start(f32[7,16,1,256]{3,2,1,0:T(1,128)S(1)} %get-tuple-element.75), channel_id=1, source_target_pairs={{0,1},{1,2},{2,3},{3,4},{4,5},{5,6},{6,7},{7,0},{8,9},{9,10},{10,1... | collective-permute-start | bytes 344072 | tf_op jit(solution)/shard_map/ppermute | solution.py:88
  25.6 2.4 %collective-permute-start.7 = (f32[7,16,1,256]{3,2,1,0:T(1,128)S(1)}, f32[7,16,1,256]{3,2,1,0:T(1,128)S(1)}, u32[]{:S(2)}, u32[]{:S(2)}) collective-permute-start(f32[7,16,1,256]{3,2,1,0:T(1,128)S(1)} %get-tuple-element.75), channel_id=1, source_target_pairs={{0,2},{1,3},{2,4},{3,5},{4,6},{5,7},{6,0},{7,1},{8,10},{9,11},{10,... | collective-permute-start | bytes 344072 | tf_op jit(solution)/shard_map/ppermute | solution.py:88
  28.0 1.2 %collective-permute-start.8 = (f32[7,16,1,256]{3,2,1,0:T(1,128)S(1)}, f32[7,16,1,256]{3,2,1,0:T(1,128)S(1)}, u32[]{:S(2)}, u32[]{:S(2)}) collective-permute-start(f32[7,16,1,256]{3,2,1,0:T(1,128)S(1)} %get-tuple-element.75), channel_id=1, source_target_pairs={{0,3},{1,4},{2,5},{3,6},{4,7},{5,0},{6,1},{7,2},{8,11},{9,12},{10,... | collective-permute-start | bytes 344072 | tf_op jit(solution)/shard_map/ppermute | solution.py:88
  29.2 0.5 %collective-permute-start.9 = (f32[7,16,1,256]{3,2,1,0:T(1,128)S(1)}, f32[7,16,1,256]{3,2,1,0:T(1,128)S(1)}, u32[]{:S(2)}, u32[]{:S(2)}) collective-permute-start(f32[7,16,1,256]{3,2,1,0:T(1,128)S(1)} %get-tuple-element.75), channel_id=1, source_target_pairs={{0,4},{1,5},{2,6},{3,7},{4,0},{5,1},{6,2},{7,3},{8,12},{9,13},{10,... | collective-permute-start | bytes 344072 | tf_op jit(solution)/shard_map/ppermute | solution.py:88
  29.7 2.7 %collective-permute-start.5 = (f32[2,7,1,8,256]{4,3,1,2,0:T(8,128)S(1)}, f32[2,7,1,8,256]{4,3,1,2,0:T(8,128)S(1)}, u32[]{:S(2)}, u32[]{:S(2)}) collective-permute-start(f32[2,7,1,8,256]{4,3,1,2,0:T(8,128)S(1)} %pad_maximum_fusion.4), channel_id=1, source_target_pairs={{0,16},{8,24},{16,0},{24,8},{1,17},{9,25},{17,1},{25,9},{2,18},{10... | collective-permute-start | bytes 344072 | tf_op jit(solution)/shard_map/ppermute | solution.py:94
  32.4 0.3 pad_maximum_fusion.2
  32.7 3.1 %collective-permute-start.10 = (f32[3,7,16,1,256]{4,3,2,1,0:T(1,128)S(1)}, f32[3,7,16,1,256]{4,3,2,1,0:T(1,128)S(1)}, u32[]{:S(2)}, u32[]{:S(2)}) collective-permute-start(f32[3,7,16,1,256]{4,3,2,1,0:T(1,128)S(1)} %pad_maximum_fusion.2), channel_id=1, source_target_pairs={{0,5},{1,6},{2,7},{3,0},{4,1},{5,2},{6,3},{7,4},{8,13},{9,14},{10,... | collective-permute-start | bytes 1032200 | tf_op jit(solution)/shard_map/ppermute | solution.py:94
  36.0 0.6 %collective-permute-done.9 = f32[7,16,1,256]{3,2,1,0:T(1,128)S(1)} collective-permute-done((f32[7,16,1,256]{3,2,1,0:T(1,128)S(1)}, f32[7,16,1,256]{3,2,1,0:T(1,128)S(1)}, u32[]{:S(2)}, u32[]{:S(2)}) %collective-permute-start.9) | collective-permute-done | bytes 114720 | tf_op jit(solution)/shard_map/ppermute | solution.py:88
  36.6 1.8 %collective-permute-done.5 = f32[2,7,1,8,256]{4,3,1,2,0:T(8,128)S(1)} collective-permute-done((f32[2,7,1,8,256]{4,3,1,2,0:T(8,128)S(1)}, f32[2,7,1,8,256]{4,3,1,2,0:T(8,128)S(1)}, u32[]{:S(2)}, u32[]{:S(2)}) %collective-permute-start.5) | collective-permute-done | bytes 114720 | tf_op jit(solution)/shard_map/ppermute | solution.py:94
  38.7 0.1 fusion.40
  39.2 0.1 multiply_add_fusion.11
  39.5 0.2 fusion.38
  40.0 0.1 multiply_add_fusion.10
  40.2 0.2 fusion.36
  40.8 0.1 multiply_add_fusion.9
  41.0 0.2 fusion.34
  41.6 0.1 multiply_add_fusion.8
  41.8 0.2 fusion.32
  42.4 0.1 multiply_add_fusion.7
  42.6 0.2 fusion.30
  43.1 0.1 multiply_add_fusion.6
  43.4 0.2 fusion.28
  43.8 0.2 pad_multiply_fusion
  44.3 0.5 %copy-done.10 = f32[16,8,256]{2,1,0:T(8,128)} copy-done((f32[16,8,256]{2,1,0:T(8,128)}, f32[16,8,256]{2,1,0:T(8,128)S(1)}, u32[]{:S(2)}) %copy-start.10) | copy-done | bytes 131096
  44.8 0.7 %add_subtract_fusion = f32[16,8,256]{2,1,0:T(8,128)} fusion(f32[16,8,256]{2,1,0:T(8,128)S(1)} %maximum_subtract_fusion.6, f32[16,8,256]{2,1,0:T(8,128)S(1)} %copy-done.2, f32[16,8,256]{2,1,0:T(8,128)S(1)} %fusion.25, f32[16,8,255]{2,1,0:T(8,128)S(1)} %slice.1141), kind=kLoop, calls=%fused_computation.86 | loop fusion | flops 98304 | bytes 654848 | tf_op jit(solution)/shard_map/sub | solution.py:247
  45.6 0.7 %fusion.24 = f32[16,8,256]{2,1,0:T(8,128)} fusion(f32[16,8,256]{2,1,0:T(8,128)S(1)} %copy-done.4, f32[16,8,256]{2,1,0:T(8,128)S(1)} %copy-done.1, f32[1,8,256]{2,1,0:T(8,128)S(1)} %bitcast.782, f32[15,8,256]{2,1,0:T(8,128)S(1)} %slice.1142, f32[8,256]{1,0:T(8,128)S(1)} %bitcast.781, f32[3,16,8,256]{3,2,1,0:T(8,128)S(1)} %add_divide_fusion.1, ...), kind=kLoop, calls=%fused_computation.51 | loop fusion | flops 262144 | bytes 933888 | tf_op jit(solution)/shard_map/sub | solution.py:249
  46.3 0.3 constant_dynamic-update-slice_fusion
  46.6 0.6 %fusion.120 = (f32[1,16,1,256]{3,2,1,0:T(1,128)S(1)}, f32[1,16,1,256]{3,2,1,0:T(1,128)S(1)}, f32[1,16,1,256]{3,2,1,0:T(1,128)S(1)}, f32[1,16,1,256]{3,2,1,0:T(1,...) fusion(f32[8,7,16,1,256]{4,3,2,1,0:T(1,128)S(1)} %constant_dyna, ...), kind=kLoop, calls=%fused_computation.359 | loop fusion | flops 385024 | bytes 1130548 | tf_op jit(solution)/shard_map/mul | solution.py:126
  47.2 0.3 constant_dynamic-update-slice_fusion.11
  48.0 0.6 %copy-done.11 = f32[16,8,256]{2,1,0:T(8,128)} copy-done((f32[16,8,256]{2,1,0:T(8,128)}, f32[16,8,256]{2,1,0:T(8,128)S(1)}, u32[]{:S(2)}) %copy-start.11) | copy-done | bytes 131096
  48.7 0.7 %fusion.22 = f32[16,8,256]{2,1,0:T(8,128)} fusion(f32[16,8,256]{2,1,0:T(8,128)S(1)} %maximum_subtract_fusion.4, f32[16,8,256]{2,1,0:T(8,128)S(1)} %copy-done, f32[16,1,256]{2,1,0:T(1,128)S(1)} %fusion.282, f32[16,7,256]{2,1,0:T(8,128)S(1)} %slice.1140, f32[16,256]{1,0:T(8,128)S(1)} %bitcast.777, f32[3,16,8,256]{3,2,1,0:T(8,128)S(1)} %add_divide_fusion, ...), kind=kLoop, calls=%fused_computation.48 | loop fusion | flops 262144 | bytes 950272 | tf_op jit(solution)/shard_map/sub | solution.py:245
  (186 shorter events, 6.5 us)
Async XLA Ops:
  1.3 1.1 %copy-start.9 = (f32[16,8,256]{2,1,0:T(8,128)S(1)}, f32[16,8,256]{2,1,0:T(8,128)}, u32[]{:S(2)}) copy-start(f32[16,8,256]{2,1,0:T(8,128)} %param.9) | copy-start | bytes 393220
  2.4 0.9 %copy-start.1 = (f32[16,8,256]{2,1,0:T(8,128)S(1)}, f32[16,8,256]{2,1,0:T(8,128)}, u32[]{:S(2)}) copy-start(f32[16,8,256]{2,1,0:T(8,128)} %param.13) | copy-start | bytes 393220
  2.4 6.0 %copy-start.6 = (f32[16,8,256]{2,1,0:T(8,128)S(1)}, f32[16,8,256]{2,1,0:T(8,128)}, u32[]{:S(2)}) copy-start(f32[16,8,256]{2,1,0:T(8,128)} %param.10) | copy-start | bytes 393220
  2.4 7.4 %copy-start.2 = (f32[16,8,256]{2,1,0:T(8,128)S(1)}, f32[16,8,256]{2,1,0:T(8,128)}, u32[]{:S(2)}) copy-start(f32[16,8,256]{2,1,0:T(8,128)} %param.12) | copy-start | bytes 393220
  3.3 9.5 %copy-start.3 = (f32[16,8,256]{2,1,0:T(8,128)}, f32[16,8,256]{2,1,0:T(8,128)S(1)}, u32[]{:S(2)}) copy-start(f32[16,8,256]{2,1,0:T(8,128)S(1)} %pad_subtract_fusion) | copy-start | bytes 393220
  3.3 6.4 %copy-start = (f32[16,8,256]{2,1,0:T(8,128)S(1)}, f32[16,8,256]{2,1,0:T(8,128)}, u32[]{:S(2)}) copy-start(f32[16,8,256]{2,1,0:T(8,128)} %param.11) | copy-start | bytes 393220
  3.3 8.0 %copy-start.8 = (f32[16,8,256]{2,1,0:T(8,128)S(1)}, f32[16,8,256]{2,1,0:T(8,128)}, u32[]{:S(2)}) copy-start(f32[16,8,256]{2,1,0:T(8,128)} %param.8) | copy-start | bytes 393220
  3.3 12.7 %collective-permute-start = (f32[3,1,8,256]{3,2,1,0:T(8,128)S(1)}, f32[3,1,8,256]{3,2,1,0:T(8,128)S(1)}, u32[]{:S(2)}, u32[]{:S(2)}) collective-permute-start(f32[3,1,8,256]{3,2,1,0:T(8,128)S(1)} %pad_maximum_fusion.8), channel_id=1, source_target_pairs={{0,8},{8,16},{16,24},{1,9},{9,17},{17,25},{2,10},{10,18},{18,26},{... | collective-permute-start | bytes 73736 | tf_op jit(solution)/shard_map/ppermute | solution.py:14
  8.4 5.8 %collective-permute-start.1 = (f32[1,8,256]{2,1,0:T(8,128)S(1)}, f32[1,8,256]{2,1,0:T(8,128)S(1)}, u32[]{:S(2)}, u32[]{:S(2)}) collective-permute-start(f32[1,8,256]{2,1,0:T(8,128)S(1)} %slice.779), channel_id=1, source_target_pairs={{8,0},{16,8},{24,16},{9,1},{17,9},{25,17},{10,2},{18,10},{26,18},{... | collective-permute-start | bytes 24584 | tf_op jit(solution)/shard_map/ppermute | solution.py:14
  9.9 6.1 %collective-permute-start.2 = (f32[3,16,1,256]{3,2,1,0:T(1,128)S(1)}, f32[3,16,1,256]{3,2,1,0:T(1,128)S(1)}, u32[]{:S(2)}, u32[]{:S(2)}) collective-permute-start(f32[3,16,1,256]{3,2,1,0:T(1,128)S(1)} %pad_maximum_fusion.7), channel_id=1, source_target_pairs={{0,1},{1,2},{2,3},{3,4},{4,5},{5,6},{6,7},{8,9},{9,10},{10,11},{11... | collective-permute-start | bytes 147464 | tf_op jit(solution)/shard_map/ppermute | solution.py:14
  11.4 4.6 %collective-permute-start.3 = (f32[16,1,256]{2,1,0:T(1,128)S(1)}, f32[16,1,256]{2,1,0:T(1,128)S(1)}, u32[]{:S(2)}, u32[]{:S(2)}) collective-permute-start(f32[16,1,256]{2,1,0:T(1,128)S(1)} %slice.783), channel_id=1, source_target_pairs={{1,0},{2,1},{3,2},{4,3},{5,4},{6,5},{7,6},{9,8},{10,9},{11,10},{12... | collective-permute-start | bytes 49160 | tf_op jit(solution)/shard_map/ppermute | solution.py:14
  12.8 0.9 %copy-start.5 = (f32[16,8,256]{2,1,0:T(8,128)S(1)}, f32[16,8,256]{2,1,0:T(8,128)}, u32[]{:S(2)}) copy-start(f32[16,8,256]{2,1,0:T(8,128)} %param.14) | copy-start | bytes 393220
  12.8 1.0 %copy-start.13 = (f32[16,8,256]{2,1,0:T(8,128)S(1)}, f32[16,8,256]{2,1,0:T(8,128)}, u32[]{:S(2)}) copy-start(f32[16,8,256]{2,1,0:T(8,128)} %param.15) | copy-start | bytes 393220
  14.2 1.9 %copy-start.7 = (f32[16,8,256]{2,1,0:T(8,128)S(1)}, f32[16,8,256]{2,1,0:T(8,128)}, u32[]{:S(2)}) copy-start(f32[16,8,256]{2,1,0:T(8,128)} %param.10) | copy-start | bytes 393220
  14.2 1.9 %slice-start.3 = ((f32[16,8,256]{2,1,0:T(8,128)}), f32[15,8,256]{2,1,0:T(8,128)S(1)}, s32[]{:S(2)}) async-start(f32[16,8,256]{2,1,0:T(8,128)} %param.10), calls=%async_computation.3 | async-start | bytes 245760 | tf_op jit(solution)/shard_map/slice | solution.py:18
  16.1 0.9 %copy-start.4 = (f32[16,8,256]{2,1,0:T(8,128)S(1)}, f32[16,8,256]{2,1,0:T(8,128)}, u32[]{:S(2)}) copy-start(f32[16,8,256]{2,1,0:T(8,128)} %copy-done.3) | copy-start | bytes 393220
  16.1 0.9 %slice-start = ((f32[16,8,256]{2,1,0:T(8,128)}), f32[15,8,256]{2,1,0:T(8,128)S(1)}, s32[]{:S(2)}) async-start(f32[16,8,256]{2,1,0:T(8,128)} %param.11), calls=%async_computation | async-start | bytes 245760 | tf_op jit(solution)/shard_map/slice | solution.py:18
  16.1 1.0 %slice-start.1 = ((f32[16,8,256]{2,1,0:T(8,128)}), f32[15,8,256]{2,1,0:T(8,128)S(1)}, s32[]{:S(2)}) async-start(f32[16,8,256]{2,1,0:T(8,128)} %param.13), calls=%async_computation.1 | async-start | bytes 245760 | tf_op jit(solution)/shard_map/slice | solution.py:18
  16.1 1.0 %slice-start.2 = ((f32[16,8,256]{2,1,0:T(8,128)}), f32[15,8,256]{2,1,0:T(8,128)S(1)}, s32[]{:S(2)}) async-start(f32[16,8,256]{2,1,0:T(8,128)} %copy-done.3), calls=%async_computation.2 | async-start | bytes 245760 | tf_op jit(solution)/shard_map/slice | solution.py:18
  19.2 10.6 %collective-permute-start.4 = (f32[7,1,8,256]{3,2,1,0:T(8,128)S(1)}, f32[7,1,8,256]{3,2,1,0:T(8,128)S(1)}, u32[]{:S(2)}, u32[]{:S(2)}) collective-permute-start(f32[7,1,8,256]{3,2,1,0:T(8,128)S(1)} %get-tuple-element.253), channel_id=1, source_target_pairs={{0,8},{8,16},{16,24},{24,0},{1,9},{9,17},{17,25},{25,1},{2,10},{10... | collective-permute-start | bytes 172040 | tf_op jit(solution)/shard_map/ppermute | solution.py:88
  23.4 9.0 %collective-permute-start.6 = (f32[7,16,1,256]{3,2,1,0:T(1,128)S(1)}, f32[7,16,1,256]{3,2,1,0:T(1,128)S(1)}, u32[]{:S(2)}, u32[]{:S(2)}) collective-permute-start(f32[7,16,1,256]{3,2,1,0:T(1,128)S(1)} %get-tuple-element.75), channel_id=1, source_target_pairs={{0,1},{1,2},{2,3},{3,4},{4,5},{5,6},{6,7},{7,0},{8,9},{9,10},{10,1... | collective-permute-start | bytes 344072 | tf_op jit(solution)/shard_map/ppermute | solution.py:88
  25.6 6.8 %collective-permute-start.7 = (f32[7,16,1,256]{3,2,1,0:T(1,128)S(1)}, f32[7,16,1,256]{3,2,1,0:T(1,128)S(1)}, u32[]{:S(2)}, u32[]{:S(2)}) collective-permute-start(f32[7,16,1,256]{3,2,1,0:T(1,128)S(1)} %get-tuple-element.75), channel_id=1, source_target_pairs={{0,2},{1,3},{2,4},{3,5},{4,6},{5,7},{6,0},{7,1},{8,10},{9,11},{10,... | collective-permute-start | bytes 344072 | tf_op jit(solution)/shard_map/ppermute | solution.py:88
  28.0 8.0 %collective-permute-start.8 = (f32[7,16,1,256]{3,2,1,0:T(1,128)S(1)}, f32[7,16,1,256]{3,2,1,0:T(1,128)S(1)}, u32[]{:S(2)}, u32[]{:S(2)}) collective-permute-start(f32[7,16,1,256]{3,2,1,0:T(1,128)S(1)} %get-tuple-element.75), channel_id=1, source_target_pairs={{0,3},{1,4},{2,5},{3,6},{4,7},{5,0},{6,1},{7,2},{8,11},{9,12},{10,... | collective-permute-start | bytes 344072 | tf_op jit(solution)/shard_map/ppermute | solution.py:88
  29.2 7.4 %collective-permute-start.9 = (f32[7,16,1,256]{3,2,1,0:T(1,128)S(1)}, f32[7,16,1,256]{3,2,1,0:T(1,128)S(1)}, u32[]{:S(2)}, u32[]{:S(2)}) collective-permute-start(f32[7,16,1,256]{3,2,1,0:T(1,128)S(1)} %get-tuple-element.75), channel_id=1, source_target_pairs={{0,4},{1,5},{2,6},{3,7},{4,0},{5,1},{6,2},{7,3},{8,12},{9,13},{10,... | collective-permute-start | bytes 344072 | tf_op jit(solution)/shard_map/ppermute | solution.py:88
  29.7 8.6 %collective-permute-start.5 = (f32[2,7,1,8,256]{4,3,1,2,0:T(8,128)S(1)}, f32[2,7,1,8,256]{4,3,1,2,0:T(8,128)S(1)}, u32[]{:S(2)}, u32[]{:S(2)}) collective-permute-start(f32[2,7,1,8,256]{4,3,1,2,0:T(8,128)S(1)} %pad_maximum_fusion.4), channel_id=1, source_target_pairs={{0,16},{8,24},{16,0},{24,8},{1,17},{9,25},{17,1},{25,9},{2,18},{10... | collective-permute-start | bytes 344072 | tf_op jit(solution)/shard_map/ppermute | solution.py:94
  32.7 13.6 %collective-permute-start.10 = (f32[3,7,16,1,256]{4,3,2,1,0:T(1,128)S(1)}, f32[3,7,16,1,256]{4,3,2,1,0:T(1,128)S(1)}, u32[]{:S(2)}, u32[]{:S(2)}) collective-permute-start(f32[3,7,16,1,256]{4,3,2,1,0:T(1,128)S(1)} %pad_maximum_fusion.2), channel_id=1, source_target_pairs={{0,5},{1,6},{2,7},{3,0},{4,1},{5,2},{6,3},{7,4},{8,13},{9,14},{10,... | collective-permute-start | bytes 1032200 | tf_op jit(solution)/shard_map/ppermute | solution.py:94
  44.2 0.7 %copy-start.10 = (f32[16,8,256]{2,1,0:T(8,128)}, f32[16,8,256]{2,1,0:T(8,128)S(1)}, u32[]{:S(2)}) copy-start(f32[16,8,256]{2,1,0:T(8,128)S(1)} %fusion.25) | copy-start | bytes 393220
  45.6 0.8 %copy-start.12 = (f32[16,8,256]{2,1,0:T(8,128)}, f32[16,8,256]{2,1,0:T(8,128)S(1)}, u32[]{:S(2)}) copy-start(f32[16,8,256]{2,1,0:T(8,128)S(1)} %fusion.5) | copy-start | bytes 393220
  48.0 0.7 %copy-start.11 = (f32[16,8,256]{2,1,0:T(8,128)}, f32[16,8,256]{2,1,0:T(8,128)S(1)}, u32[]{:S(2)}) copy-start(f32[16,8,256]{2,1,0:T(8,128)S(1)} %fusion.1) | copy-start | bytes 393220

commit v8 on v1

--- a/solution.py
+++ b/solution.py
@@ -4,6 +4,9 @@
 from jax.sharding import PartitionSpec as P
 
 step_ratio = 1024.0
+DIRECT = {8: 5}
+HOPS = {8: ((1, 2, 3, 7), 4)}
+LIMIT = 2
 
 
 def passed_along(value, axis, steps):
@@ -77,8 +80,34 @@
     return (lower_band, main_band, upper_band)
 
 
+def cyclic_shift(values, axis, shift):
+    count = lax.axis_size(axis)
+    return lax.ppermute(values, axis, [(source, (source + shift) % count) for source in range(count)])
+
+
 def gathered(values, axis):
-    return lax.all_gather(values, axis)
+    count = lax.axis_size(axis)
+    if count in HOPS:
+        direct, hop = HOPS[count]
+        held = {0: values}
+        for shift in direct:
+            held[shift] = cyclic_shift(values, axis, shift)
+        carried = [shift for shift in range(count) if shift + hop < count and shift + hop not in held]
+        moved = cyclic_shift(jnp.stack([held[shift] for shift in carried]), axis, hop)
+        for index, shift in enumerate(carried):
+            held[shift + hop] = moved[index]
+        return jnp.stack([held[shift] for shift in range(count)]), held
+    direct = count if count <= LIMIT else DIRECT.get(count, (count + 1) // 2)
+    pieces = [values] + [cyclic_shift(values, axis, shift) for shift in range(1, direct)]
+    held = dict(enumerate(pieces))
+    shifted = jnp.stack(pieces)
+    while shifted.shape[0] < count:
+        have = shifted.shape[0]
+        moved = cyclic_shift(shifted[: count - have], axis, have)
+        for index in range(moved.shape[0]):
+            held[have + index] = moved[index]
+        shifted = jnp.concatenate([shifted, moved])
+    return shifted, held
 
 
 def block_spikes(lower_band, main_band, upper_band, right_side, direction):
@@ -98,9 +127,13 @@
     blocks = coefficients.shape[0]
     alpha = jnp.zeros_like(coefficients[0, 0])
     beta = jnp.zeros_like(alpha)
+    handed = jnp.zeros_like(alpha)
     carried = []
     for block in range(blocks):
-        a0, a1, a2, b0, b1, b2 = [coefficients[block, index] for index in range(6)]
+        held = lax.dynamic_index_in_dim(coefficients, (position - block) % blocks, 0, False)
+        a0, a1, a2, b0, b1, b2, passed = [held[index] for index in range(7)]
+        alpha = alpha + handed
+        handed = passed
         scale = 1.0 / (1.0 - a1 * beta)
         p_term = (a0 + a1 * alpha) * scale
         q_term = a2 * scale
@@ -124,16 +157,28 @@
     )
 
 
-def partitioned(lower_band, main_band, upper_band, right_side, direction, axis):
+def partitioned(lower_band, main_band, upper_band, right_side, direction, axis, handed_on, extra):
     length = main_band.shape[direction]
     solved = block_spikes(lower_band, main_band, upper_band, right_side, direction)
     edges = jnp.concatenate(
-        [take_rows(solved, direction + 1, 0, 1), take_rows(solved, direction + 1, length - 1, 1)]
-    )
-    everyone = gathered(edges, axis)
+        [
+            take_rows(solved, direction + 1, 0, 1),
+            take_rows(solved, direction + 1, length - 1, 1),
+            handed_on,
+            extra,
+        ]
+    )
+    everyone, held = gathered(edges, axis)
+    count = lax.axis_size(axis)
+    position = lax.axis_index(axis)
+    from_below = jnp.where(position >= 1, held[1][7], 0.0)
+    from_above = jnp.where(position <= count - 2, held[count - 1][7], 0.0)
+    return solved, everyone, from_below, from_above
+
+
+def finished(solved, everyone, axis):
     earlier, following = interface_sweep(everyone, lax.axis_index(axis))
-    result = solved[0] + solved[1] * earlier + solved[2] * following
-    return result, following
+    return solved[0] + solved[1] * earlier + solved[2] * following, following
 
 
 def body(
@@ -153,56 +198,55 @@
     size_z = electric_x.shape[1]
     size_x = electric_x.shape[2]
     cross_y = ahead_diff(electric_y, 2, edge_zeros(electric_y, 2))
-    below_y = passed_along(
-        jnp.stack(
-            [
-                take_rows(magnetic_z, 0, size_y - 1, 1),
-                take_rows(cross_y, 0, size_y - 1, 1),
-                take_rows(magnetic_x, 0, size_y - 1, 1),
-            ]
-        ),
-        "gy",
-        1,
-    )
+    below_my = passed_along(take_rows(magnetic_y, 1, size_z - 1, 1), "gz", 1)
     above_ez = passed_along(take_rows(electric_z, 0, 0, 1), "gy", -1)
     cross_z = ahead_diff(electric_z, 0, above_ez)
-    below_z = passed_along(
-        jnp.stack(
-            [
-                take_rows(magnetic_y, 1, size_z - 1, 1),
-                take_rows(magnetic_x, 1, size_z - 1, 1),
-                take_rows(cross_z, 1, size_z - 1, 1),
-            ]
-        ),
+    source_x = keeping * electric_x + coupling * (
+        behind_diff(magnetic_z, 0, edge_zeros(magnetic_z, 0))
+        - behind_diff(cross_y, 0, edge_zeros(cross_y, 0))
+        - behind_diff(magnetic_y, 1, below_my)
+    )
+    source_y = keeping * electric_y + coupling * (
+        behind_diff(magnetic_x, 1, edge_zeros(magnetic_x, 1))
+        - behind_diff(cross_z, 1, edge_zeros(cross_z, 1))
+        - behind_diff(magnetic_z, 2, edge_zeros(magnetic_z, 2))
+    )
+    index_z = lax.broadcasted_iota(jnp.int32, coupling.shape, 1) + lax.axis_index("gz") * size_z
+    lower_z, main_z, upper_z = bands(coupling, damping, index_z, size_z * lax.axis_size("gz"))
+    solved_z, everyone_z, _, above_ex = partitioned(
+        lower_z,
+        main_z,
+        upper_z,
+        source_y,
+        1,
         "gz",
-        1,
-    )
-    above_ex = passed_along(take_rows(electric_x, 1, 0, 1), "gz", -1)
+        (take_rows(cross_z, 1, size_z - 1, 1) - take_rows(magnetic_x, 1, size_z - 1, 1))[None],
+        take_rows(electric_x, 1, 0, 1)[None],
+    )
+    index_y = lax.broadcasted_iota(jnp.int32, coupling.shape, 0) + lax.axis_index("gy") * size_y
+    lower_y, main_y, upper_y = bands(coupling, damping, index_y, size_y * lax.axis_size("gy"))
+    solved_y, everyone_y, below_mx, _ = partitioned(
+        lower_y,
+        main_y,
+        upper_y,
+        source_x,
+        0,
+        "gy",
+        (take_rows(cross_y, 0, size_y - 1, 1) - take_rows(magnetic_z, 0, size_y - 1, 1))[None],
+        take_rows(magnetic_x, 0, size_y - 1, 1)[None],
+    )
+    half_electric_x, fresh_ex = finished(solved_y, everyone_y, "gy")
     cross_x = ahead_diff(electric_x, 1, above_ex)
-    source_x = keeping * electric_x + coupling * (
-        behind_diff(magnetic_z, 0, below_y[0])
-        - behind_diff(cross_y, 0, below_y[1])
-        - behind_diff(magnetic_y, 1, below_z[0])
-    )
-    source_y = keeping * electric_y + coupling * (
-        behind_diff(magnetic_x, 1, below_z[1])
-        - behind_diff(cross_z, 1, below_z[2])
-        - behind_diff(magnetic_z, 2, edge_zeros(magnetic_z, 2))
-    )
     source_z = keeping * electric_z + coupling * (
         behind_diff(magnetic_y, 2, edge_zeros(magnetic_y, 2))
         - behind_diff(cross_x, 2, edge_zeros(cross_x, 2))
-        - behind_diff(magnetic_x, 0, below_y[2])
+        - behind_diff(magnetic_x, 0, below_mx)
     )
     index_x = lax.broadcasted_iota(jnp.int32, coupling.shape, 2)
     lower_x, main_x, upper_x = bands(coupling, damping, index_x, size_x)
     half_electric_z = reduce_lines(lower_x, main_x, upper_x, source_z[None], 2)[0]
-    index_z = lax.broadcasted_iota(jnp.int32, coupling.shape, 1) + lax.axis_index("gz") * size_z
-    lower_z, main_z, upper_z = bands(coupling, damping, index_z, size_z * lax.axis_size("gz"))
-    half_electric_y, fresh_ey = partitioned(lower_z, main_z, upper_z, source_y, 1, "gz")
-    index_y = lax.broadcasted_iota(jnp.int32, coupling.shape, 0) + lax.axis_index("gy") * size_y
-    lower_y, main_y, upper_y = bands(coupling, damping, index_y, size_y * lax.axis_size("gy"))
-    half_electric_x, fresh_ex = partitioned(lower_y, main_y, upper_y, source_x, 0, "gy")
+    half_electric_z, everyone_z = lax.optimization_barrier((half_electric_z, everyone_z))
+    half_electric_y, fresh_ey = finished(solved_z, everyone_z, "gz")
     half_magnetic_x = magnetic_x + ahead_diff(half_electric_y, 1, fresh_ey) - cross_z
     half_magnetic_y = (
         magnetic_y + ahead_diff(half_electric_z, 2, edge_zeros(half_electric_z, 2)) - cross_x

time: 67.8 us -> 48 us (0.71)
  blocking collectives: 29.1 us -> 0 us
  starting transfers between devices: 11.2 us -> 17.1 us
  other arithmetic: 9.39 us -> 12.5 us
  local copies, waits for them, and re-layouts: 13.7 us -> 14.6 us
  waiting for transfers between devices: 2.19 us -> 1.38 us
    all_gather x2 -> x0, blocking collectives: 29.1 us -> none  [gathered(): return lax.all_gather(values, axis)]
    ppermute x0 -> x7, starting transfers between devices: none -> 13.5 us  [cyclic_shift(): lax.ppermute(values, axis, [(source, (source + shift) % count) for source...]
    ppermute x4 -> x2, starting transfers between devices: 11.2 us -> 3.62 us  [passed_along(): lax.ppermute(value, axis, [(source, source + steps) for source in range(f...]
    slice x74 -> x75, local copies, waits for them, and re-layouts: 5.69 us -> 8.61 us  [take_rows(): return lax.slice_in_dim(values, start, start + length, axis=direction)]
    ppermute x4 -> x2, waiting for transfers between devices: 2.19 us -> 0.01 us  [passed_along(): lax.ppermute(value, axis, [(source, source + steps) for source in range(f...]
    another operation x7 -> x2, local copies, waits for them, and re-layouts: 1.66 us -> 0.02 us  [the longest x1 0.02 us: gathered(): return (jnp.stack([held[shift] for shift in range(count)]), held)]
    ppermute x0 -> x7, waiting for transfers between devices: none -> 1.38 us  [cyclic_shift(): lax.ppermute(values, axis, [(source, (source + shift) % count) for source...]
    another operation x1 -> x3, other arithmetic: 0.05 us -> 1.16 us  [block_spikes(): stacked = jnp.stack([right_side, left_column, right_column])]
  transfers between devices with their start and end apart: 4 -> 9, of which waited for: 2 -> 1; matrix products, arithmetic and copies ran while one was open for 6% -> 31% of each run, Pallas kernels for 0% -> 0%
where the time goes in v8:
time: 48 us; the launch traced here: 47.7 us
  starting transfers between devices  17.1 us (36%)
  local copies, waits for them, and re-layouts  14.6 us (30%)
  other arithmetic  12.5 us (26%)
  between operations  2.06 us (4%)
  waiting for transfers between devices  1.38 us (3%)
    ppermute x7, starting transfers between devices, cyclic_shift(): lax.ppermute(values, axis, [(source, (source + shift) % count) for source...  13.5 us
    slice x75, local copies, waits for them, and re-layouts, take_rows(): return lax.slice_in_dim(values, start, start + length, axis=direction)  8.61 us
    unnamed x44, local copies, waits for them, and re-layouts  5.93 us
    ppermute x2, starting transfers between devices, passed_along(): lax.ppermute(value, axis, [(source, source + steps) for source in range(f...  3.62 us
    add x12, other arithmetic, reduce_lines(): right_side + ratio_low[None] * low_right + ratio_high[None] * high_right  2.07 us
    ppermute x7, waiting for transfers between devices, cyclic_shift(): lax.ppermute(values, axis, [(source, (source + shift) % count) for source...  1.38 us
    add x13, other arithmetic, reduce_lines(): main_band = main_band + ratio_low * low_upper + ratio_high * high_lower  1.26 us
    another operation x3, other arithmetic, block_spikes(): stacked = jnp.stack([right_side, left_column, right_column])  1.16 us
  transfers between devices with their start and end apart: 9, of which 1 were waited for; matrix products, arithmetic and copies ran while one was open for 31% of the time, Pallas kernels for 0%

profile of v8, /device:TPU:0, one launch (start us, length us, event | category | flops | bytes accessed | tf_op | source)
XLA Modules:
  0.0 47.7 jit_solution(860803941714294505)
XLA Ops:
  0.6 1.3 %slice.824 = f32[1,8,256]{2,1,0:T(8,128)} slice(f32[16,8,256]{2,1,0:T(8,128)} %param.10), slice={[0:1], [0:8], [0:256]} | slice | bytes 16384 | tf_op jit(solution)/shard_map/slice | solution.py:19
  1.9 1.3 %collective-permute-start.3 = (f32[1,8,256]{2,1,0:T(8,128)}, f32[1,8,256]{2,1,0:T(8,128)}, u32[]{:S(2)}, u32[]{:S(2)}) collective-permute-start(f32[1,8,256]{2,1,0:T(8,128)} %slice.824), channel_id=1, source_target_pairs={{8,0},{16,8},{24,16},{9,1},{17,9},{25,17},{10,2},{18,10},{26,18},{... | collective-permute-start | bytes 24584 | tf_op jit(solution)/shard_map/ppermute | solution.py:15
  3.2 1.5 %slice.758 = f32[16,1,256]{2,1,0:T(1,128)} slice(f32[16,8,256]{2,1,0:T(8,128)} %param.12), slice={[0:16], [7:8], [0:256]} | slice | bytes 32768 | tf_op jit(solution)/shard_map/slice | solution.py:19
  4.7 2.3 %collective-permute-start = (f32[16,1,256]{2,1,0:T(1,128)}, f32[16,1,256]{2,1,0:T(1,128)S(1)}, u32[]{:S(2)}, u32[]{:S(2)}) collective-permute-start(f32[16,1,256]{2,1,0:T(1,128)} %slice.758), channel_id=1, source_target_pairs={{0,1},{1,2},{2,3},{3,4},{4,5},{5,6},{6,7},{8,9},{9,10},{10,11},{11... | collective-permute-start | bytes 49160 | tf_op jit(solution)/shard_map/ppermute | solution.py:15
  7.2 0.6 %broadcast_select_fusion.4 = f32[8]{0:T(128)} fusion(s32[]{:T(128)S(6)} %mul.6940), kind=kLoop, calls=%fused_computation.474 | loop fusion | flops 24 | bytes 36 | tf_op jit(solution)/shard_map/jit(_where)/select_n | solution.py:79
  7.7 0.5 %broadcast_select_fusion.5 = f32[16]{0:T(128)} fusion(s32[]{:T(128)S(6)} %mul.6865), kind=kLoop, calls=%fused_computation.475 | loop fusion | flops 48 | bytes 68 | tf_op jit(solution)/shard_map/jit(_where)/select_n | solution.py:79
  8.4 0.9 %copy-done.2 = f32[16,8,256]{2,1,0:T(8,128)S(1)} copy-done((f32[16,8,256]{2,1,0:T(8,128)S(1)}, f32[16,8,256]{2,1,0:T(8,128)}, u32[]{:S(2)}) %copy-start.2) | copy-done | bytes 131096
  9.4 0.7 %slice.755 = f32[15,8,256]{2,1,0:T(8,128)} slice(f32[16,8,256]{2,1,0:T(8,128)S(1)} %copy-done.2), slice={[0:15], [0:8], [0:256]} | slice | bytes 245760 | tf_op jit(solution)/shard_map/slice | solution.py:19
  10.0 0.6 %iota_compare_fusion = (pred[256]{0:T(512)(128)(4,1)}, pred[256]{0:T(512)(128)(4,1)}) fusion(), kind=kLoop, calls=%fused_computation.461 | loop fusion | flops 512 | bytes 512 | tf_op jit(solution)/shard_map/le | solution.py:78
  10.6 0.2 select_select_fusion.1
  10.8 0.7 %fusion.279 = (f32[15,8,256]{2,1,0:T(8,128)}, f32[15,8,256]{2,1,0:T(8,128)S(1)}) fusion(f32[16,8,256]{2,1,0:T(8,128)S(1)} %get-tuple-element.217), kind=kLoop, calls=%fused_computation.531 | loop fusion | bytes 491520 | tf_op jit(solution)/shard_map/slice | solution.py:19
  11.5 0.7 %fusion.278 = (f32[15,8,256]{2,1,0:T(8,128)}, f32[15,8,256]{2,1,0:T(8,128)S(1)}) fusion(f32[16,8,256]{2,1,0:T(8,128)S(1)} %get-tuple-element.219), kind=kLoop, calls=%fused_computation.530 | loop fusion | bytes 491520 | tf_op jit(solution)/shard_map/slice | solution.py:19
  12.1 0.3 copy-done.1
  12.5 0.9 %copy-done.6 = f32[16,8,256]{2,1,0:T(8,128)S(1)} copy-done((f32[16,8,256]{2,1,0:T(8,128)S(1)}, f32[16,8,256]{2,1,0:T(8,128)}, u32[]{:S(2)}) %copy-start.6) | copy-done | bytes 131096
  13.8 0.7 %copy-done.8 = f32[16,8,256]{2,1,0:T(8,128)S(1)} copy-done((f32[16,8,256]{2,1,0:T(8,128)S(1)}, f32[16,8,256]{2,1,0:T(8,128)}, u32[]{:S(2)}) %copy-start.8) | copy-done | bytes 131096
  14.5 0.8 %maximum_subtract_fusion.1 = f32[16,8,256]{2,1,0:T(8,128)S(1)} fusion(f32[16,8,256]{2,1,0:T(8,128)S(1)} %copy-done.8, f32[1,8,256]{2,1,0:T(8,128)} %collective-permute-done.3, f32[15,8,256]{2,1,0:T(8,128)S(1)} %slice-done.1), kind=kLoop, calls=%fused_computation.31 | loop fusion | flops 65536 | bytes 393216 | tf_op jit(solution)/shard_map/sub | solution.py:29
  15.5 0.5 %copy-done.17 = f32[8]{0:T(128)S(1)} copy-done((f32[8]{0:T(128)S(1)}, f32[8]{0:T(128)}, u32[]{:S(2)}) %copy-start.17) | copy-done | bytes 56
  16.0 1.1 %add_bitcast_fusion = (f32[1,16,8,256]{3,2,1,0:T(8,128)S(1)}, f32[1,16,8,256]{3,2,1,0:T(8,128)S(1)}, f32[16,8,256]{2,1,0:T(8,128)S(1)}, f32[16,8,256]{2,1,0:T(8,128)S(1)}) fusion(f32[16,8,256]{2,1,0:T(8,128)S(1)} %copy-done.2, f32[16,8,255]{2,1,0:T(8,128)S(1)} %bitcast.747, f32[16,8,256]{2,1,0:T(8,128)S(1)} %maximum_subtract_fusion.1, ...), kind=kLoop, calls=%fused_computation.134 | loop fusion | flops 786432 | bytes 2440800 | tf_op jit(solution)/shard_map/stack | solution.py:122
  17.2 0.8 %copy-done.12 = f32[15,8,256]{2,1,0:T(8,128)S(1)} copy-done((f32[15,8,256]{2,1,0:T(8,128)S(1)}, f32[15,8,256]{2,1,0:T(8,128)}, u32[]{:S(2)}) %copy-start.12) | copy-done | bytes 122904
  19.4 3.1 %collective-permute-start.1 = (f32[8,1,8,256]{3,2,1,0:T(8,128)S(1)}, f32[8,1,8,256]{3,2,1,0:T(8,128)S(1)}, u32[]{:S(2)}, u32[]{:S(2)}) collective-permute-start(f32[8,1,8,256]{3,2,1,0:T(8,128)S(1)} %get-tuple-element.243), channel_id=1, source_target_pairs={{0,8},{8,16},{16,24},{24,0},{1,9},{9,17},{17,25},{25,1},{2,10},{10... | collective-permute-start | bytes 196616 | tf_op jit(solution)/shard_map/ppermute | solution.py:85
  23.1 0.1 multiply_add_fusion.1
  23.8 0.2 constant_dynamic-update-slice_fusion.3
  23.9 2.0 %collective-permute-start.5 = (f32[8,16,1,256]{3,2,1,0:T(1,128)S(1)}, f32[8,16,1,256]{3,2,1,0:T(1,128)S(1)}, u32[]{:S(2)}, u32[]{:S(2)}) collective-permute-start(f32[8,16,1,256]{3,2,1,0:T(1,128)S(1)} %get-tuple-element.46), channel_id=1, source_target_pairs={{0,1},{1,2},{2,3},{3,4},{4,5},{5,6},{6,7},{7,0},{8,9},{9,10},{10,1... | collective-permute-start | bytes 393224 | tf_op jit(solution)/shard_map/ppermute | solution.py:85
  25.9 1.5 %collective-permute-start.6 = (f32[8,16,1,256]{3,2,1,0:T(1,128)S(1)}, f32[8,16,1,256]{3,2,1,0:T(1,128)S(1)}, u32[]{:S(2)}, u32[]{:S(2)}) collective-permute-start(f32[8,16,1,256]{3,2,1,0:T(1,128)S(1)} %get-tuple-element.46), channel_id=1, source_target_pairs={{0,2},{1,3},{2,4},{3,5},{4,6},{5,7},{6,0},{7,1},{8,10},{9,11},{10,... | collective-permute-start | bytes 393224 | tf_op jit(solution)/shard_map/ppermute | solution.py:85
  27.4 1.1 %collective-permute-start.7 = (f32[8,16,1,256]{3,2,1,0:T(1,128)S(1)}, f32[8,16,1,256]{3,2,1,0:T(1,128)S(1)}, u32[]{:S(2)}, u32[]{:S(2)}) collective-permute-start(f32[8,16,1,256]{3,2,1,0:T(1,128)S(1)} %get-tuple-element.46), channel_id=1, source_target_pairs={{0,3},{1,4},{2,5},{3,6},{4,7},{5,0},{6,1},{7,2},{8,11},{9,12},{10,... | collective-permute-start | bytes 393224 | tf_op jit(solution)/shard_map/ppermute | solution.py:85
  28.5 1.6 %collective-permute-start.4 = (f32[8,16,1,256]{3,2,1,0:T(1,128)S(1)}, f32[8,16,1,256]{3,2,1,0:T(1,128)S(1)}, u32[]{:S(2)}, u32[]{:S(2)}) collective-permute-start(f32[8,16,1,256]{3,2,1,0:T(1,128)S(1)} %get-tuple-element.46), channel_id=1, source_target_pairs={{0,7},{1,0},{2,1},{3,2},{4,3},{5,4},{6,5},{7,6},{8,15},{9,8},{10,9... | collective-permute-start | bytes 393224 | tf_op jit(solution)/shard_map/ppermute | solution.py:85
  30.1 3.2 %collective-permute-start.2 = (f32[2,8,1,8,256]{4,3,2,1,0:T(8,128)S(1)}, f32[2,8,1,8,256]{4,3,2,1,0:T(8,128)S(1)}, u32[]{:S(2)}, u32[]{:S(2)}) collective-permute-start(f32[2,8,1,8,256]{4,3,2,1,0:T(8,128)S(1)} %pad_maximum_fusion.4), channel_id=1, source_target_pairs={{0,16},{8,24},{16,0},{24,8},{1,17},{9,25},{17,1},{25,9},{2,18},{10... | collective-permute-start | bytes 393224 | tf_op jit(solution)/shard_map/ppermute | solution.py:85
  33.4 0.4 pad_maximum_fusion.2
  33.8 1.0 %collective-permute-start.8 = (f32[3,8,16,1,256]{4,3,2,1,0:T(1,128)S(1)}, f32[3,8,16,1,256]{4,3,2,1,0:T(1,128)S(1)}, u32[]{:S(2)}, u32[]{:S(2)}) collective-permute-start(f32[3,8,16,1,256]{4,3,2,1,0:T(1,128)S(1)} %pad_maximum_fusion.2), channel_id=1, source_target_pairs={{0,4},{1,5},{2,6},{3,7},{4,0},{5,1},{6,2},{7,3},{8,12},{9,13},{10,... | collective-permute-start | bytes 1179656 | tf_op jit(solution)/shard_map/ppermute | solution.py:85
  34.9 0.2 fusion.15
  35.1 0.6 %copy-done.15 = pred[256]{0:T(512)(128)(4,1)S(1)} copy-done((pred[256]{0:T(512)(128)(4,1)S(1)}, pred[256]{0:T(512)(128)(4,1)}, u32[]{:S(2)}) %copy-start.15) | copy-done | bytes 280
  36.1 0.1 multiply_add_fusion.11
  36.5 0.2 fusion.33
  37.3 0.2 fusion.31
  37.7 0.1 multiply_add_fusion.9
  38.1 0.2 fusion.29
  38.9 0.2 fusion.27
  39.6 0.2 fusion.25
  40.4 0.2 fusion.23
  40.9 0.2 pad_multiply_fusion
  41.7 0.7 %fusion.19 = f32[16,8,256]{2,1,0:T(8,128)} fusion(f32[16,8,256]{2,1,0:T(8,128)S(1)} %copy-done.4, f32[16,8,256]{2,1,0:T(8,128)S(1)} %copy-done.2, f32[1,8,256]{2,1,0:T(8,128)S(1)} %bitcast.760, f32[15,8,256]{2,1,0:T(8,128)S(1)} %slice.1112, f32[8,256]{1,0:T(8,128)S(1)} %bitcast.759, f32[3,16,8,256]{3,2,1,0:T(8,128)S(1)} %add_divide_fusion.1, ...), kind=kLoop, calls=%fused_computation.44 | loop fusion | flops 262144 | bytes 933888 | tf_op jit(solution)/shard_map/sub | solution.py:254
  42.4 1.4 %collective-permute-done.8 = f32[3,8,16,1,256]{4,3,2,1,0:T(1,128)S(1)} collective-permute-done((f32[3,8,16,1,256]{4,3,2,1,0:T(1,128)S(1)}, f32[3,8,16,1,256]{4,3,2,1,0:T(1,128)S(1)}, u32[]{:S(2)}, u32[]{:S(2)}) %collective-permute-start.8) | collective-permute-done | bytes 393248 | tf_op jit(solution)/shard_map/ppermute | solution.py:85
  43.8 0.3 constant_dynamic-update-slice_fusion
  44.1 0.6 %fusion.114 = (f32[1,16,1,256]{3,2,1,0:T(1,128)S(1)}, f32[1,16,1,256]{3,2,1,0:T(1,128)S(1)}, f32[1,16,1,256]{3,2,1,0:T(1,128)S(1)}, f32[1,16,1,256]{3,2,1,0:T(1,...) fusion(f32[8,8,16,1,256]{4,3,2,1,0:T(1,128)S(1)} %bitcast_dynam, ...), kind=kLoop, calls=%fused_computation.349 | loop fusion | flops 385024 | bytes 1130548 | tf_op jit(solution)/shard_map/mul | solution.py:138
  44.7 0.3 constant_dynamic-update-slice_fusion.11
  45.5 0.7 %add_subtract_fusion = f32[16,8,256]{2,1,0:T(8,128)} fusion(f32[16,8,256]{2,1,0:T(8,128)S(1)} %maximum_subtract_fusion.2, f32[16,8,256]{2,1,0:T(8,128)S(1)} %copy-done, f32[16,8,256]{2,1,0:T(8,128)S(1)} %fusion.20, f32[16,8,255]{2,1,0:T(8,128)S(1)} %slice.978), kind=kLoop, calls=%fused_computation.81 | loop fusion | flops 98304 | bytes 654848 | tf_op jit(solution)/shard_map/sub | solution.py:252
  46.3 0.6 %copy-done.10 = f32[16,8,256]{2,1,0:T(8,128)} copy-done((f32[16,8,256]{2,1,0:T(8,128)}, f32[16,8,256]{2,1,0:T(8,128)S(1)}, u32[]{:S(2)}) %copy-start.10) | copy-done | bytes 131096
  46.9 0.7 %fusion.17 = f32[16,8,256]{2,1,0:T(8,128)} fusion(f32[16,8,256]{2,1,0:T(8,128)S(1)} %maximum_subtract_fusion.1, f32[16,8,256]{2,1,0:T(8,128)S(1)} %copy-done.1, f32[16,1,256]{2,1,0:T(1,128)S(1)} %fusion.281, f32[16,7,256]{2,1,0:T(8,128)S(1)} %slice.1111, f32[16,256]{1,0:T(8,128)S(1)} %bitcast.755, f32[3,16,8,256]{3,2,1,0:T(8,128)S(1)} %add_divide_fusion, ...), kind=kLoop, calls=%fused_computation.41 | loop fusion | flops 262144 | bytes 950272 | tf_op jit(solution)/shard_map/sub | solution.py:250
  (181 shorter events, 7.2 us)
Async XLA Ops:
  1.9 11.8 %collective-permute-start.3 = (f32[1,8,256]{2,1,0:T(8,128)}, f32[1,8,256]{2,1,0:T(8,128)}, u32[]{:S(2)}, u32[]{:S(2)}) collective-permute-start(f32[1,8,256]{2,1,0:T(8,128)} %slice.824), channel_id=1, source_target_pairs={{8,0},{16,8},{24,16},{9,1},{17,9},{25,17},{10,2},{18,10},{26,18},{... | collective-permute-start | bytes 24584 | tf_op jit(solution)/shard_map/ppermute | solution.py:15
  4.7 10.6 %collective-permute-start = (f32[16,1,256]{2,1,0:T(1,128)}, f32[16,1,256]{2,1,0:T(1,128)S(1)}, u32[]{:S(2)}, u32[]{:S(2)}) collective-permute-start(f32[16,1,256]{2,1,0:T(1,128)} %slice.758), channel_id=1, source_target_pairs={{0,1},{1,2},{2,3},{3,4},{4,5},{5,6},{6,7},{8,9},{9,10},{10,11},{11... | collective-permute-start | bytes 49160 | tf_op jit(solution)/shard_map/ppermute | solution.py:15
  7.1 1.1 %copy-start.7 = (f32[16,8,256]{2,1,0:T(8,128)S(1)}, f32[16,8,256]{2,1,0:T(8,128)}, u32[]{:S(2)}) copy-start(f32[16,8,256]{2,1,0:T(8,128)} %param.9) | copy-start | bytes 393220
  8.4 1.6 %copy-start.3 = (f32[16,8,256]{2,1,0:T(8,128)}, f32[16,8,256]{2,1,0:T(8,128)S(1)}, u32[]{:S(2)}) copy-start(f32[16,8,256]{2,1,0:T(8,128)S(1)} %pad_subtract_fusion) | copy-start | bytes 393220
  8.4 1.0 %copy-start.2 = (f32[16,8,256]{2,1,0:T(8,128)S(1)}, f32[16,8,256]{2,1,0:T(8,128)}, u32[]{:S(2)}) copy-start(f32[16,8,256]{2,1,0:T(8,128)} %param.13) | copy-start | bytes 393220
  9.4 1.3 %copy-start.5 = (f32[16,8,256]{2,1,0:T(8,128)S(1)}, f32[16,8,256]{2,1,0:T(8,128)}, u32[]{:S(2)}) copy-start(f32[16,8,256]{2,1,0:T(8,128)} %param.14) | copy-start | bytes 393220
  9.4 1.3 %copy-start.14 = (f32[16,8,256]{2,1,0:T(8,128)S(1)}, f32[16,8,256]{2,1,0:T(8,128)}, u32[]{:S(2)}) copy-start(f32[16,8,256]{2,1,0:T(8,128)} %param.15) | copy-start | bytes 393220
  11.5 0.9 %copy-start.1 = (f32[16,8,256]{2,1,0:T(8,128)S(1)}, f32[16,8,256]{2,1,0:T(8,128)}, u32[]{:S(2)}) copy-start(f32[16,8,256]{2,1,0:T(8,128)} %param.11) | copy-start | bytes 393220
  12.4 0.9 %copy-start.6 = (f32[16,8,256]{2,1,0:T(8,128)S(1)}, f32[16,8,256]{2,1,0:T(8,128)}, u32[]{:S(2)}) copy-start(f32[16,8,256]{2,1,0:T(8,128)} %param.8) | copy-start | bytes 393220
  13.5 0.9 %copy-start.8 = (f32[16,8,256]{2,1,0:T(8,128)S(1)}, f32[16,8,256]{2,1,0:T(8,128)}, u32[]{:S(2)}) copy-start(f32[16,8,256]{2,1,0:T(8,128)} %param.10) | copy-start | bytes 393220
  13.6 1.0 %slice-start.1 = ((f32[16,8,256]{2,1,0:T(8,128)}), f32[15,8,256]{2,1,0:T(8,128)S(1)}, s32[]{:S(2)}) async-start(f32[16,8,256]{2,1,0:T(8,128)} %param.10), calls=%async_computation.1 | async-start | bytes 245760 | tf_op jit(solution)/shard_map/slice | solution.py:19
  13.7 1.6 %copy-start = (f32[16,8,256]{2,1,0:T(8,128)S(1)}, f32[16,8,256]{2,1,0:T(8,128)}, u32[]{:S(2)}) copy-start(f32[16,8,256]{2,1,0:T(8,128)} %param.12) | copy-start | bytes 393220
  13.7 1.6 %copy-start.4 = (f32[16,8,256]{2,1,0:T(8,128)S(1)}, f32[16,8,256]{2,1,0:T(8,128)}, u32[]{:S(2)}) copy-start(f32[16,8,256]{2,1,0:T(8,128)} %copy-done.3) | copy-start | bytes 393220
  14.5 0.9 %slice-start = ((f32[16,8,256]{2,1,0:T(8,128)}), f32[15,8,256]{2,1,0:T(8,128)S(1)}, s32[]{:S(2)}) async-start(f32[16,8,256]{2,1,0:T(8,128)} %copy-done.3), calls=%async_computation | async-start | bytes 245760 | tf_op jit(solution)/shard_map/slice | solution.py:19
  15.3 0.7 %copy-start.17 = (f32[8]{0:T(128)S(1)}, f32[8]{0:T(128)}, u32[]{:S(2)}) copy-start(f32[8]{0:T(128)} %broadcast_select_fusion.4) | copy-start | bytes 100
  15.3 0.7 %copy-start.18 = (f32[16]{0:T(128)S(1)}, f32[16]{0:T(128)}, u32[]{:S(2)}) copy-start(f32[16]{0:T(128)} %broadcast_select_fusion.5) | copy-start | bytes 196
  17.2 0.9 %copy-start.12 = (f32[15,8,256]{2,1,0:T(8,128)S(1)}, f32[15,8,256]{2,1,0:T(8,128)}, u32[]{:S(2)}) copy-start(f32[15,8,256]{2,1,0:T(8,128)} %get-tuple-element.238) | copy-start | bytes 368644
  17.2 1.0 %copy-start.13 = (f32[15,8,256]{2,1,0:T(8,128)S(1)}, f32[15,8,256]{2,1,0:T(8,128)}, u32[]{:S(2)}) copy-start(f32[15,8,256]{2,1,0:T(8,128)} %get-tuple-element.236) | copy-start | bytes 368644
  19.4 10.7 %collective-permute-start.1 = (f32[8,1,8,256]{3,2,1,0:T(8,128)S(1)}, f32[8,1,8,256]{3,2,1,0:T(8,128)S(1)}, u32[]{:S(2)}, u32[]{:S(2)}) collective-permute-start(f32[8,1,8,256]{3,2,1,0:T(8,128)S(1)} %get-tuple-element.243), channel_id=1, source_target_pairs={{0,8},{8,16},{16,24},{24,0},{1,9},{9,17},{17,25},{25,1},{2,10},{10... | collective-permute-start | bytes 196616 | tf_op jit(solution)/shard_map/ppermute | solution.py:85
  23.9 9.4 %collective-permute-start.5 = (f32[8,16,1,256]{3,2,1,0:T(1,128)S(1)}, f32[8,16,1,256]{3,2,1,0:T(1,128)S(1)}, u32[]{:S(2)}, u32[]{:S(2)}) collective-permute-start(f32[8,16,1,256]{3,2,1,0:T(1,128)S(1)} %get-tuple-element.46), channel_id=1, source_target_pairs={{0,1},{1,2},{2,3},{3,4},{4,5},{5,6},{6,7},{7,0},{8,9},{9,10},{10,1... | collective-permute-start | bytes 393224 | tf_op jit(solution)/shard_map/ppermute | solution.py:85
  25.9 7.4 %collective-permute-start.6 = (f32[8,16,1,256]{3,2,1,0:T(1,128)S(1)}, f32[8,16,1,256]{3,2,1,0:T(1,128)S(1)}, u32[]{:S(2)}, u32[]{:S(2)}) collective-permute-start(f32[8,16,1,256]{3,2,1,0:T(1,128)S(1)} %get-tuple-element.46), channel_id=1, source_target_pairs={{0,2},{1,3},{2,4},{3,5},{4,6},{5,7},{6,0},{7,1},{8,10},{9,11},{10,... | collective-permute-start | bytes 393224 | tf_op jit(solution)/shard_map/ppermute | solution.py:85
  27.4 13.9 %collective-permute-start.7 = (f32[8,16,1,256]{3,2,1,0:T(1,128)S(1)}, f32[8,16,1,256]{3,2,1,0:T(1,128)S(1)}, u32[]{:S(2)}, u32[]{:S(2)}) collective-permute-start(f32[8,16,1,256]{3,2,1,0:T(1,128)S(1)} %get-tuple-element.46), channel_id=1, source_target_pairs={{0,3},{1,4},{2,5},{3,6},{4,7},{5,0},{6,1},{7,2},{8,11},{9,12},{10,... | collective-permute-start | bytes 393224 | tf_op jit(solution)/shard_map/ppermute | solution.py:85
  28.5 6.3 %collective-permute-start.4 = (f32[8,16,1,256]{3,2,1,0:T(1,128)S(1)}, f32[8,16,1,256]{3,2,1,0:T(1,128)S(1)}, u32[]{:S(2)}, u32[]{:S(2)}) collective-permute-start(f32[8,16,1,256]{3,2,1,0:T(1,128)S(1)} %get-tuple-element.46), channel_id=1, source_target_pairs={{0,7},{1,0},{2,1},{3,2},{4,3},{5,4},{6,5},{7,6},{8,15},{9,8},{10,9... | collective-permute-start | bytes 393224 | tf_op jit(solution)/shard_map/ppermute | solution.py:85
  30.1 11.2 %collective-permute-start.2 = (f32[2,8,1,8,256]{4,3,2,1,0:T(8,128)S(1)}, f32[2,8,1,8,256]{4,3,2,1,0:T(8,128)S(1)}, u32[]{:S(2)}, u32[]{:S(2)}) collective-permute-start(f32[2,8,1,8,256]{4,3,2,1,0:T(8,128)S(1)} %pad_maximum_fusion.4), channel_id=1, source_target_pairs={{0,16},{8,24},{16,0},{24,8},{1,17},{9,25},{17,1},{25,9},{2,18},{10... | collective-permute-start | bytes 393224 | tf_op jit(solution)/shard_map/ppermute | solution.py:85
  33.8 10.0 %collective-permute-start.8 = (f32[3,8,16,1,256]{4,3,2,1,0:T(1,128)S(1)}, f32[3,8,16,1,256]{4,3,2,1,0:T(1,128)S(1)}, u32[]{:S(2)}, u32[]{:S(2)}) collective-permute-start(f32[3,8,16,1,256]{4,3,2,1,0:T(1,128)S(1)} %pad_maximum_fusion.2), channel_id=1, source_target_pairs={{0,4},{1,5},{2,6},{3,7},{4,0},{5,1},{6,2},{7,3},{8,12},{9,13},{10,... | collective-permute-start | bytes 1179656 | tf_op jit(solution)/shard_map/ppermute | solution.py:85
  35.1 0.6 %copy-start.15 = (pred[256]{0:T(512)(128)(4,1)S(1)}, pred[256]{0:T(512)(128)(4,1)}, u32[]{:S(2)}) copy-start(pred[256]{0:T(512)(128)(4,1)} %get-tuple-element.268) | copy-start | bytes 772
  35.1 0.7 %copy-start.16 = (pred[256]{0:T(512)(128)(4,1)S(1)}, pred[256]{0:T(512)(128)(4,1)}, u32[]{:S(2)}) copy-start(pred[256]{0:T(512)(128)(4,1)} %get-tuple-element.269) | copy-start | bytes 772
  41.2 4.3 %copy-start.9 = (f32[16,8,256]{2,1,0:T(8,128)}, f32[16,8,256]{2,1,0:T(8,128)S(1)}, u32[]{:S(2)}) copy-start(f32[16,8,256]{2,1,0:T(8,128)S(1)} %fusion.20) | copy-start | bytes 393220
  41.6 0.8 %copy-start.11 = (f32[16,8,256]{2,1,0:T(8,128)}, f32[16,8,256]{2,1,0:T(8,128)S(1)}, u32[]{:S(2)}) copy-start(f32[16,8,256]{2,1,0:T(8,128)S(1)} %fusion.5) | copy-start | bytes 393220
  46.3 0.7 %copy-start.10 = (f32[16,8,256]{2,1,0:T(8,128)}, f32[16,8,256]{2,1,0:T(8,128)S(1)}, u32[]{:S(2)}) copy-start(f32[16,8,256]{2,1,0:T(8,128)S(1)} %fusion.1) | copy-start | bytes 393220

commit v9 on v8

--- a/solution.py
+++ b/solution.py
@@ -5,7 +5,7 @@
 
 step_ratio = 1024.0
 DIRECT = {8: 5}
-HOPS = {8: ((1, 2, 3, 7), 4)}
+HOPS = {8: ((1, 2, 3, 4, 7), 5)}
 LIMIT = 2
 
 

time: 48 us -> 47.4 us (0.987)
  waiting for transfers between devices: 1.38 us -> 0.03 us
  starting transfers between devices: 17.1 us -> 18.1 us
    ppermute x7 -> x8, waiting for transfers between devices: 1.38 us -> 0.02 us  [cyclic_shift(): lax.ppermute(values, axis, [(source, (source + shift) % count) for source...]
    ppermute x7 -> x8, starting transfers between devices: 13.5 us -> 14.5 us  [cyclic_shift(): lax.ppermute(values, axis, [(source, (source + shift) % count) for source...]
    unnamed x44 -> x45, local copies, waits for them, and re-layouts: 5.93 us -> 5.83 us
  transfers between devices with their start and end apart: 9 -> 10, of which waited for: 1 -> 0; matrix products, arithmetic and copies ran while one was open for 31% -> 31% of each run, Pallas kernels for 0% -> 0%
where the time goes in v9:
time: 47.4 us; the launch traced here: 47.1 us
  starting transfers between devices  18.1 us (38%)
  local copies, waits for them, and re-layouts  14.5 us (31%)
  other arithmetic  12.3 us (26%)
  between operations  2.09 us (4%)
    ppermute x8, starting transfers between devices, cyclic_shift(): lax.ppermute(values, axis, [(source, (source + shift) % count) for source...  14.5 us
    slice x75, local copies, waits for them, and re-layouts, take_rows(): return lax.slice_in_dim(values, start, start + length, axis=direction)  8.61 us
    unnamed x45, local copies, waits for them, and re-layouts  5.83 us
    ppermute x2, starting transfers between devices, passed_along(): lax.ppermute(value, axis, [(source, source + steps) for source in range(f...  3.62 us
    add x12, other arithmetic, reduce_lines(): right_side + ratio_low[None] * low_right + ratio_high[None] * high_right  2.07 us
    add x13, other arithmetic, reduce_lines(): main_band = main_band + ratio_low * low_upper + ratio_high * high_lower  1.26 us
    another operation x3, other arithmetic, block_spikes(): stacked = jnp.stack([right_side, left_column, right_column])  1.16 us
    select_n x3, other arithmetic, bands(): main_band = 1.0 + damping + coupling * jnp.where(row_index >= 1, 2.0, 1.0)  1.04 us
  transfers between devices with their start and end apart: 10, of which 0 were waited for; matrix products, arithmetic and copies ran while one was open for 31% of the time, Pallas kernels for 0%

profile of v9, /device:TPU:0, one launch (start us, length us, event | category | flops | bytes accessed | tf_op | source)
XLA Modules:
  0.0 47.1 jit_solution(9588494128031305103)
XLA Ops:
  0.6 1.3 %slice.823 = f32[1,8,256]{2,1,0:T(8,128)} slice(f32[16,8,256]{2,1,0:T(8,128)} %param.10), slice={[0:1], [0:8], [0:256]} | slice | bytes 16384 | tf_op jit(solution)/shard_map/slice | solution.py:19
  1.9 1.3 %collective-permute-start.3 = (f32[1,8,256]{2,1,0:T(8,128)}, f32[1,8,256]{2,1,0:T(8,128)}, u32[]{:S(2)}, u32[]{:S(2)}) collective-permute-start(f32[1,8,256]{2,1,0:T(8,128)} %slice.823), channel_id=1, source_target_pairs={{8,0},{16,8},{24,16},{9,1},{17,9},{25,17},{10,2},{18,10},{26,18},{... | collective-permute-start | bytes 24584 | tf_op jit(solution)/shard_map/ppermute | solution.py:15
  3.2 1.5 %slice.757 = f32[16,1,256]{2,1,0:T(1,128)} slice(f32[16,8,256]{2,1,0:T(8,128)} %param.12), slice={[0:16], [7:8], [0:256]} | slice | bytes 32768 | tf_op jit(solution)/shard_map/slice | solution.py:19
  4.7 2.3 %collective-permute-start = (f32[16,1,256]{2,1,0:T(1,128)}, f32[16,1,256]{2,1,0:T(1,128)S(1)}, u32[]{:S(2)}, u32[]{:S(2)}) collective-permute-start(f32[16,1,256]{2,1,0:T(1,128)} %slice.757), channel_id=1, source_target_pairs={{0,1},{1,2},{2,3},{3,4},{4,5},{5,6},{6,7},{8,9},{9,10},{10,11},{11... | collective-permute-start | bytes 49160 | tf_op jit(solution)/shard_map/ppermute | solution.py:15
  7.2 0.5 %broadcast_select_fusion.4 = f32[8]{0:T(128)} fusion(s32[]{:T(128)S(6)} %mul.6940), kind=kLoop, calls=%fused_computation.475 | loop fusion | flops 24 | bytes 36 | tf_op jit(solution)/shard_map/jit(_where)/select_n | solution.py:79
  7.7 0.5 %broadcast_select_fusion.5 = f32[16]{0:T(128)} fusion(s32[]{:T(128)S(6)} %mul.6865), kind=kLoop, calls=%fused_computation.476 | loop fusion | flops 48 | bytes 68 | tf_op jit(solution)/shard_map/jit(_where)/select_n | solution.py:79
  8.4 0.9 %copy-done.2 = f32[16,8,256]{2,1,0:T(8,128)S(1)} copy-done((f32[16,8,256]{2,1,0:T(8,128)S(1)}, f32[16,8,256]{2,1,0:T(8,128)}, u32[]{:S(2)}) %copy-start.2) | copy-done | bytes 131096
  9.3 0.7 %slice.754 = f32[15,8,256]{2,1,0:T(8,128)} slice(f32[16,8,256]{2,1,0:T(8,128)S(1)} %copy-done.2), slice={[0:15], [0:8], [0:256]} | slice | bytes 245760 | tf_op jit(solution)/shard_map/slice | solution.py:19
  10.0 0.6 %iota_compare_fusion = (pred[256]{0:T(512)(128)(4,1)}, pred[256]{0:T(512)(128)(4,1)}) fusion(), kind=kLoop, calls=%fused_computation.462 | loop fusion | flops 512 | bytes 512 | tf_op jit(solution)/shard_map/le | solution.py:78
  10.6 0.2 select_select_fusion.1
  10.7 0.7 %fusion.279 = (f32[15,8,256]{2,1,0:T(8,128)}, f32[15,8,256]{2,1,0:T(8,128)S(1)}) fusion(f32[16,8,256]{2,1,0:T(8,128)S(1)} %get-tuple-element.217), kind=kLoop, calls=%fused_computation.532 | loop fusion | bytes 491520 | tf_op jit(solution)/shard_map/slice | solution.py:19
  11.4 0.7 %fusion.278 = (f32[15,8,256]{2,1,0:T(8,128)}, f32[15,8,256]{2,1,0:T(8,128)S(1)}) fusion(f32[16,8,256]{2,1,0:T(8,128)S(1)} %get-tuple-element.219), kind=kLoop, calls=%fused_computation.531 | loop fusion | bytes 491520 | tf_op jit(solution)/shard_map/slice | solution.py:19
  12.1 0.3 copy-done.1
  12.4 0.9 %copy-done.6 = f32[16,8,256]{2,1,0:T(8,128)S(1)} copy-done((f32[16,8,256]{2,1,0:T(8,128)S(1)}, f32[16,8,256]{2,1,0:T(8,128)}, u32[]{:S(2)}) %copy-start.6) | copy-done | bytes 131096
  13.7 0.7 %copy-done.8 = f32[16,8,256]{2,1,0:T(8,128)S(1)} copy-done((f32[16,8,256]{2,1,0:T(8,128)S(1)}, f32[16,8,256]{2,1,0:T(8,128)}, u32[]{:S(2)}) %copy-start.8) | copy-done | bytes 131096
  14.5 0.8 %maximum_subtract_fusion.1 = f32[16,8,256]{2,1,0:T(8,128)S(1)} fusion(f32[16,8,256]{2,1,0:T(8,128)S(1)} %copy-done.8, f32[1,8,256]{2,1,0:T(8,128)} %collective-permute-done.3, f32[15,8,256]{2,1,0:T(8,128)S(1)} %slice-done.1), kind=kLoop, calls=%fused_computation.31 | loop fusion | flops 65536 | bytes 393216 | tf_op jit(solution)/shard_map/sub | solution.py:29
  15.4 0.5 %copy-done.17 = f32[8]{0:T(128)S(1)} copy-done((f32[8]{0:T(128)S(1)}, f32[8]{0:T(128)}, u32[]{:S(2)}) %copy-start.17) | copy-done | bytes 56
  15.9 1.1 %add_bitcast_fusion = (f32[1,16,8,256]{3,2,1,0:T(8,128)S(1)}, f32[1,16,8,256]{3,2,1,0:T(8,128)S(1)}, f32[16,8,256]{2,1,0:T(8,128)S(1)}, f32[16,8,256]{2,1,0:T(8,128)S(1)}) fusion(f32[16,8,256]{2,1,0:T(8,128)S(1)} %copy-done.2, f32[16,8,255]{2,1,0:T(8,128)S(1)} %bitcast.749, f32[16,8,256]{2,1,0:T(8,128)S(1)} %maximum_subtract_fusion.1, ...), kind=kLoop, calls=%fused_computation.136 | loop fusion | flops 786432 | bytes 2440800 | tf_op jit(solution)/shard_map/stack | solution.py:122
  17.1 0.8 %copy-done.12 = f32[15,8,256]{2,1,0:T(8,128)S(1)} copy-done((f32[15,8,256]{2,1,0:T(8,128)S(1)}, f32[15,8,256]{2,1,0:T(8,128)}, u32[]{:S(2)}) %copy-start.12) | copy-done | bytes 122904
  19.3 3.1 %collective-permute-start.1 = (f32[8,1,8,256]{3,2,1,0:T(8,128)S(1)}, f32[8,1,8,256]{3,2,1,0:T(8,128)S(1)}, u32[]{:S(2)}, u32[]{:S(2)}) collective-permute-start(f32[8,1,8,256]{3,2,1,0:T(8,128)S(1)} %get-tuple-element.243), channel_id=1, source_target_pairs={{0,8},{8,16},{16,24},{24,0},{1,9},{9,17},{17,25},{25,1},{2,10},{10... | collective-permute-start | bytes 196616 | tf_op jit(solution)/shard_map/ppermute | solution.py:85
  23.0 0.1 multiply_add_fusion.1
  23.7 0.2 constant_dynamic-update-slice_fusion.2
  23.9 2.0 %collective-permute-start.5 = (f32[8,16,1,256]{3,2,1,0:T(1,128)S(1)}, f32[8,16,1,256]{3,2,1,0:T(1,128)S(1)}, u32[]{:S(2)}, u32[]{:S(2)}) collective-permute-start(f32[8,16,1,256]{3,2,1,0:T(1,128)S(1)} %get-tuple-element.46), channel_id=1, source_target_pairs={{0,1},{1,2},{2,3},{3,4},{4,5},{5,6},{6,7},{7,0},{8,9},{9,10},{10,1... | collective-permute-start | bytes 393224 | tf_op jit(solution)/shard_map/ppermute | solution.py:85
  25.8 1.5 %collective-permute-start.6 = (f32[8,16,1,256]{3,2,1,0:T(1,128)S(1)}, f32[8,16,1,256]{3,2,1,0:T(1,128)S(1)}, u32[]{:S(2)}, u32[]{:S(2)}) collective-permute-start(f32[8,16,1,256]{3,2,1,0:T(1,128)S(1)} %get-tuple-element.46), channel_id=1, source_target_pairs={{0,2},{1,3},{2,4},{3,5},{4,6},{5,7},{6,0},{7,1},{8,10},{9,11},{10,... | collective-permute-start | bytes 393224 | tf_op jit(solution)/shard_map/ppermute | solution.py:85
  27.3 1.1 %collective-permute-start.7 = (f32[8,16,1,256]{3,2,1,0:T(1,128)S(1)}, f32[8,16,1,256]{3,2,1,0:T(1,128)S(1)}, u32[]{:S(2)}, u32[]{:S(2)}) collective-permute-start(f32[8,16,1,256]{3,2,1,0:T(1,128)S(1)} %get-tuple-element.46), channel_id=1, source_target_pairs={{0,3},{1,4},{2,5},{3,6},{4,7},{5,0},{6,1},{7,2},{8,11},{9,12},{10,... | collective-permute-start | bytes 393224 | tf_op jit(solution)/shard_map/ppermute | solution.py:85
  28.4 0.5 %collective-permute-start.8 = (f32[8,16,1,256]{3,2,1,0:T(1,128)S(1)}, f32[8,16,1,256]{3,2,1,0:T(1,128)S(1)}, u32[]{:S(2)}, u32[]{:S(2)}) collective-permute-start(f32[8,16,1,256]{3,2,1,0:T(1,128)S(1)} %get-tuple-element.46), channel_id=1, source_target_pairs={{0,4},{1,5},{2,6},{3,7},{4,0},{5,1},{6,2},{7,3},{8,12},{9,13},{10,... | collective-permute-start | bytes 393224 | tf_op jit(solution)/shard_map/ppermute | solution.py:85
  29.0 1.3 %collective-permute-start.4 = (f32[8,16,1,256]{3,2,1,0:T(1,128)S(1)}, f32[8,16,1,256]{3,2,1,0:T(1,128)S(1)}, u32[]{:S(2)}, u32[]{:S(2)}) collective-permute-start(f32[8,16,1,256]{3,2,1,0:T(1,128)S(1)} %get-tuple-element.46), channel_id=1, source_target_pairs={{0,7},{1,0},{2,1},{3,2},{4,3},{5,4},{6,5},{7,6},{8,15},{9,8},{10,9... | collective-permute-start | bytes 393224 | tf_op jit(solution)/shard_map/ppermute | solution.py:85
  30.3 3.2 %collective-permute-start.2 = (f32[2,8,1,8,256]{4,3,2,1,0:T(8,128)S(1)}, f32[2,8,1,8,256]{4,3,2,1,0:T(8,128)S(1)}, u32[]{:S(2)}, u32[]{:S(2)}) collective-permute-start(f32[2,8,1,8,256]{4,3,2,1,0:T(8,128)S(1)} %pad_maximum_fusion.4), channel_id=1, source_target_pairs={{0,16},{8,24},{16,0},{24,8},{1,17},{9,25},{17,1},{25,9},{2,18},{10... | collective-permute-start | bytes 393224 | tf_op jit(solution)/shard_map/ppermute | solution.py:85
  33.5 0.3 pad_maximum_fusion.3
  33.8 1.8 %collective-permute-start.9 = (f32[2,8,16,1,256]{4,3,2,1,0:T(1,128)S(1)}, f32[2,8,16,1,256]{4,3,2,1,0:T(1,128)S(1)}, u32[]{:S(2)}, u32[]{:S(2)}) collective-permute-start(f32[2,8,16,1,256]{4,3,2,1,0:T(1,128)S(1)} %pad_maximum_fusion.3), channel_id=1, source_target_pairs={{0,5},{1,6},{2,7},{3,0},{4,1},{5,2},{6,3},{7,4},{8,13},{9,14},{10,... | collective-permute-start | bytes 786440 | tf_op jit(solution)/shard_map/ppermute | solution.py:85
  35.6 0.2 fusion.15
  35.9 0.7 %copy-done.15 = pred[256]{0:T(512)(128)(4,1)S(1)} copy-done((pred[256]{0:T(512)(128)(4,1)S(1)}, pred[256]{0:T(512)(128)(4,1)}, u32[]{:S(2)}) %copy-start.15) | copy-done | bytes 280
  36.9 0.1 multiply_add_fusion.11
  37.3 0.2 fusion.33
  38.1 0.2 fusion.31
  38.5 0.1 multiply_add_fusion.9
  38.9 0.2 fusion.29
  39.7 0.2 fusion.27
  40.4 0.2 fusion.25
  41.2 0.2 fusion.23
  41.7 0.2 pad_multiply_fusion
  42.5 0.7 %fusion.19 = f32[16,8,256]{2,1,0:T(8,128)} fusion(f32[16,8,256]{2,1,0:T(8,128)S(1)} %copy-done.4, f32[16,8,256]{2,1,0:T(8,128)S(1)} %copy-done.2, f32[1,8,256]{2,1,0:T(8,128)S(1)} %bitcast.761, f32[15,8,256]{2,1,0:T(8,128)S(1)} %slice.1111, f32[8,256]{1,0:T(8,128)S(1)} %bitcast.760, f32[3,16,8,256]{3,2,1,0:T(8,128)S(1)} %add_divide_fusion.1, ...), kind=kLoop, calls=%fused_computation.44 | loop fusion | flops 262144 | bytes 933888 | tf_op jit(solution)/shard_map/sub | solution.py:254
  43.3 0.2 constant_dynamic-update-slice_fusion
  43.5 0.6 %fusion.114 = (f32[1,16,1,256]{3,2,1,0:T(1,128)S(1)}, f32[1,16,1,256]{3,2,1,0:T(1,128)S(1)}, f32[1,16,1,256]{3,2,1,0:T(1,128)S(1)}, f32[1,16,1,256]{3,2,1,0:T(1,...) fusion(f32[8,8,16,1,256]{4,3,2,1,0:T(1,128)S(1)} %bitcast_dynam, ...), kind=kLoop, calls=%fused_computation.350 | loop fusion | flops 385024 | bytes 1130548 | tf_op jit(solution)/shard_map/mul | solution.py:138
  44.1 0.3 constant_dynamic-update-slice_fusion.10
  44.9 0.7 %add_subtract_fusion = f32[16,8,256]{2,1,0:T(8,128)} fusion(f32[16,8,256]{2,1,0:T(8,128)S(1)} %maximum_subtract_fusion.2, f32[16,8,256]{2,1,0:T(8,128)S(1)} %copy-done, f32[16,8,256]{2,1,0:T(8,128)S(1)} %fusion.20, f32[16,8,255]{2,1,0:T(8,128)S(1)} %slice.977), kind=kLoop, calls=%fused_computation.83 | loop fusion | flops 98304 | bytes 654848 | tf_op jit(solution)/shard_map/sub | solution.py:252
  45.7 0.6 %copy-done.10 = f32[16,8,256]{2,1,0:T(8,128)} copy-done((f32[16,8,256]{2,1,0:T(8,128)}, f32[16,8,256]{2,1,0:T(8,128)S(1)}, u32[]{:S(2)}) %copy-start.10) | copy-done | bytes 131096
  46.3 0.7 %fusion.17 = f32[16,8,256]{2,1,0:T(8,128)} fusion(f32[16,8,256]{2,1,0:T(8,128)S(1)} %maximum_subtract_fusion.1, f32[16,8,256]{2,1,0:T(8,128)S(1)} %copy-done.1, f32[16,1,256]{2,1,0:T(1,128)S(1)} %fusion.281, f32[16,7,256]{2,1,0:T(8,128)S(1)} %slice.1110, f32[16,256]{1,0:T(8,128)S(1)} %bitcast.756, f32[3,16,8,256]{3,2,1,0:T(8,128)S(1)} %add_divide_fusion, ...), kind=kLoop, calls=%fused_computation.41 | loop fusion | flops 262144 | bytes 950272 | tf_op jit(solution)/shard_map/sub | solution.py:250
  (184 shorter events, 7.1 us)
Async XLA Ops:
  1.9 11.8 %collective-permute-start.3 = (f32[1,8,256]{2,1,0:T(8,128)}, f32[1,8,256]{2,1,0:T(8,128)}, u32[]{:S(2)}, u32[]{:S(2)}) collective-permute-start(f32[1,8,256]{2,1,0:T(8,128)} %slice.823), channel_id=1, source_target_pairs={{8,0},{16,8},{24,16},{9,1},{17,9},{25,17},{10,2},{18,10},{26,18},{... | collective-permute-start | bytes 24584 | tf_op jit(solution)/shard_map/ppermute | solution.py:15
  4.7 10.5 %collective-permute-start = (f32[16,1,256]{2,1,0:T(1,128)}, f32[16,1,256]{2,1,0:T(1,128)S(1)}, u32[]{:S(2)}, u32[]{:S(2)}) collective-permute-start(f32[16,1,256]{2,1,0:T(1,128)} %slice.757), channel_id=1, source_target_pairs={{0,1},{1,2},{2,3},{3,4},{4,5},{5,6},{6,7},{8,9},{9,10},{10,11},{11... | collective-permute-start | bytes 49160 | tf_op jit(solution)/shard_map/ppermute | solution.py:15
  7.1 1.1 %copy-start.7 = (f32[16,8,256]{2,1,0:T(8,128)S(1)}, f32[16,8,256]{2,1,0:T(8,128)}, u32[]{:S(2)}) copy-start(f32[16,8,256]{2,1,0:T(8,128)} %param.9) | copy-start | bytes 393220
  8.3 1.6 %copy-start.3 = (f32[16,8,256]{2,1,0:T(8,128)}, f32[16,8,256]{2,1,0:T(8,128)S(1)}, u32[]{:S(2)}) copy-start(f32[16,8,256]{2,1,0:T(8,128)S(1)} %pad_subtract_fusion) | copy-start | bytes 393220
  8.4 1.0 %copy-start.2 = (f32[16,8,256]{2,1,0:T(8,128)S(1)}, f32[16,8,256]{2,1,0:T(8,128)}, u32[]{:S(2)}) copy-start(f32[16,8,256]{2,1,0:T(8,128)} %param.13) | copy-start | bytes 393220
  9.3 1.3 %copy-start.5 = (f32[16,8,256]{2,1,0:T(8,128)S(1)}, f32[16,8,256]{2,1,0:T(8,128)}, u32[]{:S(2)}) copy-start(f32[16,8,256]{2,1,0:T(8,128)} %param.14) | copy-start | bytes 393220
  9.3 1.3 %copy-start.14 = (f32[16,8,256]{2,1,0:T(8,128)S(1)}, f32[16,8,256]{2,1,0:T(8,128)}, u32[]{:S(2)}) copy-start(f32[16,8,256]{2,1,0:T(8,128)} %param.15) | copy-start | bytes 393220
  11.4 0.9 %copy-start.1 = (f32[16,8,256]{2,1,0:T(8,128)S(1)}, f32[16,8,256]{2,1,0:T(8,128)}, u32[]{:S(2)}) copy-start(f32[16,8,256]{2,1,0:T(8,128)} %param.11) | copy-start | bytes 393220
  12.4 0.9 %copy-start.6 = (f32[16,8,256]{2,1,0:T(8,128)S(1)}, f32[16,8,256]{2,1,0:T(8,128)}, u32[]{:S(2)}) copy-start(f32[16,8,256]{2,1,0:T(8,128)} %param.8) | copy-start | bytes 393220
  13.5 0.9 %copy-start.8 = (f32[16,8,256]{2,1,0:T(8,128)S(1)}, f32[16,8,256]{2,1,0:T(8,128)}, u32[]{:S(2)}) copy-start(f32[16,8,256]{2,1,0:T(8,128)} %param.10) | copy-start | bytes 393220
  13.5 1.0 %slice-start.1 = ((f32[16,8,256]{2,1,0:T(8,128)}), f32[15,8,256]{2,1,0:T(8,128)S(1)}, s32[]{:S(2)}) async-start(f32[16,8,256]{2,1,0:T(8,128)} %param.10), calls=%async_computation.1 | async-start | bytes 245760 | tf_op jit(solution)/shard_map/slice | solution.py:19
  13.7 1.6 %copy-start = (f32[16,8,256]{2,1,0:T(8,128)S(1)}, f32[16,8,256]{2,1,0:T(8,128)}, u32[]{:S(2)}) copy-start(f32[16,8,256]{2,1,0:T(8,128)} %param.12) | copy-start | bytes 393220
  13.7 1.6 %copy-start.4 = (f32[16,8,256]{2,1,0:T(8,128)S(1)}, f32[16,8,256]{2,1,0:T(8,128)}, u32[]{:S(2)}) copy-start(f32[16,8,256]{2,1,0:T(8,128)} %copy-done.3) | copy-start | bytes 393220
  14.5 0.9 %slice-start = ((f32[16,8,256]{2,1,0:T(8,128)}), f32[15,8,256]{2,1,0:T(8,128)S(1)}, s32[]{:S(2)}) async-start(f32[16,8,256]{2,1,0:T(8,128)} %copy-done.3), calls=%async_computation | async-start | bytes 245760 | tf_op jit(solution)/shard_map/slice | solution.py:19
  15.3 0.6 %copy-start.17 = (f32[8]{0:T(128)S(1)}, f32[8]{0:T(128)}, u32[]{:S(2)}) copy-start(f32[8]{0:T(128)} %broadcast_select_fusion.4) | copy-start | bytes 100
  15.3 0.6 %copy-start.18 = (f32[16]{0:T(128)S(1)}, f32[16]{0:T(128)}, u32[]{:S(2)}) copy-start(f32[16]{0:T(128)} %broadcast_select_fusion.5) | copy-start | bytes 196
  17.1 0.9 %copy-start.12 = (f32[15,8,256]{2,1,0:T(8,128)S(1)}, f32[15,8,256]{2,1,0:T(8,128)}, u32[]{:S(2)}) copy-start(f32[15,8,256]{2,1,0:T(8,128)} %get-tuple-element.238) | copy-start | bytes 368644
  17.1 1.0 %copy-start.13 = (f32[15,8,256]{2,1,0:T(8,128)S(1)}, f32[15,8,256]{2,1,0:T(8,128)}, u32[]{:S(2)}) copy-start(f32[15,8,256]{2,1,0:T(8,128)} %get-tuple-element.236) | copy-start | bytes 368644
  19.3 9.7 %collective-permute-start.1 = (f32[8,1,8,256]{3,2,1,0:T(8,128)S(1)}, f32[8,1,8,256]{3,2,1,0:T(8,128)S(1)}, u32[]{:S(2)}, u32[]{:S(2)}) collective-permute-start(f32[8,1,8,256]{3,2,1,0:T(8,128)S(1)} %get-tuple-element.243), channel_id=1, source_target_pairs={{0,8},{8,16},{16,24},{24,0},{1,9},{9,17},{17,25},{25,1},{2,10},{10... | collective-permute-start | bytes 196616 | tf_op jit(solution)/shard_map/ppermute | solution.py:85
  23.9 6.4 %collective-permute-start.5 = (f32[8,16,1,256]{3,2,1,0:T(1,128)S(1)}, f32[8,16,1,256]{3,2,1,0:T(1,128)S(1)}, u32[]{:S(2)}, u32[]{:S(2)}) collective-permute-start(f32[8,16,1,256]{3,2,1,0:T(1,128)S(1)} %get-tuple-element.46), channel_id=1, source_target_pairs={{0,1},{1,2},{2,3},{3,4},{4,5},{5,6},{6,7},{7,0},{8,9},{9,10},{10,1... | collective-permute-start | bytes 393224 | tf_op jit(solution)/shard_map/ppermute | solution.py:85
  25.8 16.2 %collective-permute-start.6 = (f32[8,16,1,256]{3,2,1,0:T(1,128)S(1)}, f32[8,16,1,256]{3,2,1,0:T(1,128)S(1)}, u32[]{:S(2)}, u32[]{:S(2)}) collective-permute-start(f32[8,16,1,256]{3,2,1,0:T(1,128)S(1)} %get-tuple-element.46), channel_id=1, source_target_pairs={{0,2},{1,3},{2,4},{3,5},{4,6},{5,7},{6,0},{7,1},{8,10},{9,11},{10,... | collective-permute-start | bytes 393224 | tf_op jit(solution)/shard_map/ppermute | solution.py:85
  27.3 14.8 %collective-permute-start.7 = (f32[8,16,1,256]{3,2,1,0:T(1,128)S(1)}, f32[8,16,1,256]{3,2,1,0:T(1,128)S(1)}, u32[]{:S(2)}, u32[]{:S(2)}) collective-permute-start(f32[8,16,1,256]{3,2,1,0:T(1,128)S(1)} %get-tuple-element.46), channel_id=1, source_target_pairs={{0,3},{1,4},{2,5},{3,6},{4,7},{5,0},{6,1},{7,2},{8,11},{9,12},{10,... | collective-permute-start | bytes 393224 | tf_op jit(solution)/shard_map/ppermute | solution.py:85
  28.4 13.7 %collective-permute-start.8 = (f32[8,16,1,256]{3,2,1,0:T(1,128)S(1)}, f32[8,16,1,256]{3,2,1,0:T(1,128)S(1)}, u32[]{:S(2)}, u32[]{:S(2)}) collective-permute-start(f32[8,16,1,256]{3,2,1,0:T(1,128)S(1)} %get-tuple-element.46), channel_id=1, source_target_pairs={{0,4},{1,5},{2,6},{3,7},{4,0},{5,1},{6,2},{7,3},{8,12},{9,13},{10,... | collective-permute-start | bytes 393224 | tf_op jit(solution)/shard_map/ppermute | solution.py:85
  29.0 4.8 %collective-permute-start.4 = (f32[8,16,1,256]{3,2,1,0:T(1,128)S(1)}, f32[8,16,1,256]{3,2,1,0:T(1,128)S(1)}, u32[]{:S(2)}, u32[]{:S(2)}) collective-permute-start(f32[8,16,1,256]{3,2,1,0:T(1,128)S(1)} %get-tuple-element.46), channel_id=1, source_target_pairs={{0,7},{1,0},{2,1},{3,2},{4,3},{5,4},{6,5},{7,6},{8,15},{9,8},{10,9... | collective-permute-start | bytes 393224 | tf_op jit(solution)/shard_map/ppermute | solution.py:85
  30.3 11.9 %collective-permute-start.2 = (f32[2,8,1,8,256]{4,3,2,1,0:T(8,128)S(1)}, f32[2,8,1,8,256]{4,3,2,1,0:T(8,128)S(1)}, u32[]{:S(2)}, u32[]{:S(2)}) collective-permute-start(f32[2,8,1,8,256]{4,3,2,1,0:T(8,128)S(1)} %pad_maximum_fusion.4), channel_id=1, source_target_pairs={{0,16},{8,24},{16,0},{24,8},{1,17},{9,25},{17,1},{25,9},{2,18},{10... | collective-permute-start | bytes 393224 | tf_op jit(solution)/shard_map/ppermute | solution.py:85
  33.8 9.5 %collective-permute-start.9 = (f32[2,8,16,1,256]{4,3,2,1,0:T(1,128)S(1)}, f32[2,8,16,1,256]{4,3,2,1,0:T(1,128)S(1)}, u32[]{:S(2)}, u32[]{:S(2)}) collective-permute-start(f32[2,8,16,1,256]{4,3,2,1,0:T(1,128)S(1)} %pad_maximum_fusion.3), channel_id=1, source_target_pairs={{0,5},{1,6},{2,7},{3,0},{4,1},{5,2},{6,3},{7,4},{8,13},{9,14},{10,... | collective-permute-start | bytes 786440 | tf_op jit(solution)/shard_map/ppermute | solution.py:85
  35.9 0.7 %copy-start.15 = (pred[256]{0:T(512)(128)(4,1)S(1)}, pred[256]{0:T(512)(128)(4,1)}, u32[]{:S(2)}) copy-start(pred[256]{0:T(512)(128)(4,1)} %get-tuple-element.268) | copy-start | bytes 772
  35.9 0.7 %copy-start.16 = (pred[256]{0:T(512)(128)(4,1)S(1)}, pred[256]{0:T(512)(128)(4,1)}, u32[]{:S(2)}) copy-start(pred[256]{0:T(512)(128)(4,1)} %get-tuple-element.269) | copy-start | bytes 772
  42.0 2.9 %copy-start.9 = (f32[16,8,256]{2,1,0:T(8,128)}, f32[16,8,256]{2,1,0:T(8,128)S(1)}, u32[]{:S(2)}) copy-start(f32[16,8,256]{2,1,0:T(8,128)S(1)} %fusion.20) | copy-start | bytes 393220
  42.5 0.8 %copy-start.11 = (f32[16,8,256]{2,1,0:T(8,128)}, f32[16,8,256]{2,1,0:T(8,128)S(1)}, u32[]{:S(2)}) copy-start(f32[16,8,256]{2,1,0:T(8,128)S(1)} %fusion.5) | copy-start | bytes 393220
  45.7 0.7 %copy-start.10 = (f32[16,8,256]{2,1,0:T(8,128)}, f32[16,8,256]{2,1,0:T(8,128)S(1)}, u32[]{:S(2)}) copy-start(f32[16,8,256]{2,1,0:T(8,128)S(1)} %fusion.1) | copy-start | bytes 393220
